TPU v7x, 256 devices: a whole 4x4x8 slice. The times are simulated.
256 devices in a mesh: chain: 8 (over x, core), rows: 32 (over z, y).
Axes of the slice: x: 4, y: 4, z: 8, core: 2. Of those that a mesh axis runs over, the one named last changes fastest.
Arguments:
- right_spike: float32 [524288, 256], P(('chain', 'rows')), may hold values from -6 to 6
- left_spike: float32 [524288, 256], P(('chain', 'rows')), may hold values from -6 to 6
- loads: float32 [524288, 256], P(('chain', 'rows')), may hold values from -6 to 6
- tip_inverse: float32 [8, 3, 256, 512], P('chain'), may hold values from -0.0234375 to 0.0234375
Outputs:
- right_final: float32 [524288, 256], P(('chain', 'rows'))
- left_final: float32 [524288, 256], P(('chain', 'rows'))
- loads_final: float32 [524288, 256], P(('chain', 'rows'))
All inputs are finite; a program needn't handle non-finite values.
Results may differ from a plain program's by a relative error of at most 0.00019.
Values sent between devices are 32-bit elements; how exact they have to be, the bound alone decides.
No kernel may reach another device: no remote copies, remote signals or barrier semaphores. Data moves between devices by JAX's collectives and lax.ppermute only.
A program may use at most 64 MiB of HBM per device.

v0:
```python
import jax
import jax.numpy as jnp
from jax import lax
from jax.sharding import PartitionSpec as P

HALF_BAND = 256
LOAD_COLS = 256
LEVELS = 3


def partner_2(x, axis, distance):
    return lax.ppermute(x, axis, [(i, i ^ 1 << distance) for i in range(lax.axis_size(axis))])


def extended(cells, sides, width):
    for axis, dim in sides:
        count = lax.axis_size(axis)
        ends = count - 1
        head = lax.slice_in_dim(cells, 0, width, axis=dim)
        tail = lax.slice_in_dim(cells, cells.shape[dim] - width, cells.shape[dim], axis=dim)
        cells = jnp.concatenate(
            [
                lax.ppermute(tail, axis, [(i, (i + 1) % count) for i in range(ends)]),
                cells,
                lax.ppermute(head, axis, [((i + 1) % count, i) for i in range(ends)]),
            ],
            axis=dim,
        )
    return cells


def spread_block(block, level, chain_pos, side_low):
    source_bit = jnp.where(side_low, 1, 0)
    for bit in range(level):
        partner = partner_2(block, "chain", bit)
        own_bit = chain_pos // 2**bit % 2
        block = jnp.where(own_bit != source_bit, partner, block)
    return block


def on_device(right_spike, left_spike, loads, tip_inverse):
    precise = lax.Precision.HIGHEST
    band = HALF_BAND
    width = LOAD_COLS
    chain_pos = lax.axis_index("chain")
    row_pos = lax.axis_index("rows")
    row_last = lax.axis_size("rows") - 1
    spike_right = right_spike
    spike_left = left_spike
    load_block = loads
    for level in range(LEVELS):
        half = 2**level
        place = chain_pos % (2 * half)
        side_low = place < half
        top_tip = jnp.concatenate([spike_right[:band], load_block[:band]], 1)
        bottom_tip = jnp.concatenate([spike_left[-band:], load_block[-band:]], 1)
        top_whole, bottom_whole = lax.psum(
            (
                jnp.where(row_pos == 0, top_tip, 0.0),
                jnp.where(row_pos == row_last, bottom_tip, 0.0),
            ),
            "rows",
        )
        beside = extended(jnp.stack([top_whole, bottom_whole]), (("chain", 0),), 1)
        lower_tip = jnp.where(side_low, beside[2], beside[0])
        upper_tip = jnp.where(side_low, beside[3], beside[1])
        blank_block = jnp.zeros((band, band), jnp.float32)
        upper_rows = jnp.concatenate([lower_tip[:, band:], lower_tip[:, :band], blank_block], 1)
        lower_rows = jnp.concatenate([upper_tip[:, band:], blank_block, upper_tip[:, :band]], 1)
        tip_rhs = jnp.concatenate([upper_rows, lower_rows], 0)
        solved = jnp.dot(
            tip_inverse[0, level], tip_rhs, precision=precise, preferred_element_type=jnp.float32
        )
        solved = spread_block(solved, level, chain_pos, side_low)
        driver = jnp.where(side_low, spike_right, spike_left)
        product = jnp.dot(driver, solved, precision=precise, preferred_element_type=jnp.float32)
        left_term = product[:, width : width + band]
        right_term = product[:, width + band :]
        load_block = load_block - product[:, :width]
        new_left = jnp.where(side_low, spike_left - left_term, -left_term)
        new_right = jnp.where(side_low, -right_term, spike_right - right_term)
        spike_left = new_left
        spike_right = new_right
    return (spike_right, spike_left, load_block)


def solution(mesh):
    in_specs = (
        P(("chain", "rows"), None),
        P(("chain", "rows"), None),
        P(("chain", "rows"), None),
        P("chain", None, None, None),
    )
    out_specs = (P(("chain", "rows"), None), P(("chain", "rows"), None), P(("chain", "rows"), None))
    return jax.shard_map(
        on_device, mesh=mesh, in_specs=in_specs, out_specs=out_specs, check_vma=False
    )
```

profile of v0, /device:TPU:31, one launch (start us, length us, event | category | flops | bytes accessed | tf_op | source)
XLA Modules:
  0.0 589.6 jit_solution(4071442390023854634)
XLA Ops:
  7.2 0.0 all-reduce.11.cloned.1.call-start
  7.2 1.9 copy.7
  9.2 0.0 copy-start.5
  9.2 3.6 copy.8
  12.8 2.0 copy.10
  14.8 0.0 copy-start.8
  14.9 1.2 maximum_select_fusion
  16.1 0.0 all-reduce.11.cloned.1.call-update
  16.1 0.4 copy-done.8
  16.5 147.0 %all-reduce.11.cloned.1.call-done = (f32[256,512]{0,1:T(8,128)}, f32[256,512]{0,1:T(8,128)}) async-done(((f32[256,512]{0,1:T(8,128)}, f32[256,512]{0,1:T(8,128)}), (f32[256,512]{0,1:T(8,128)}, f32[256,512]{0,1:T(8,128)})) %all-reduce.11.cloned.1.call-update) | async-done | bytes 1048592 | tf_op jit(solution)/shard_map/psum | solution.py:57
  163.4 1.4 collective-permute-start
  164.9 7.6 %collective-permute-start.1 = (f32[1,256,512]{1,2,0:T(8,128)}, f32[1,256,512]{1,2,0:T(8,128)S(1)}, u32[]{:S(2)}, u32[]{:S(2)}) collective-permute-start(f32[1,256,512]{1,2,0:T(8,128)} %bitcast.32), channel_id=1, source_target_pairs={{32,0},{64,32},{96,64},{128,96},{160,128},{192,160},{224,192},{33,... | collective-permute-start | bytes 1572872 | tf_op jit(solution)/shard_map/ppermute | solution.py:25
  172.5 0.1 bitcast_select_fusion.5
  172.6 1.5 collective-permute-done.1
  174.2 0.1 bitcast_select_fusion.4
  174.3 0.0 copy-start.6
  174.3 0.0 copy-start.7
  174.3 2.6 fusion.7
  177.0 0.0 copy-start.9
  177.0 5.7 fusion.4
  182.7 2.9 slice_subtract_fusion.2
  185.6 1.3 copy-done.3
  186.9 1.1 fusion.59
  188.0 0.8 maximum_select_fusion.2
  188.9 0.9 maximum_select_fusion.3
  189.7 0.0 all-reduce.9.cloned.1.call-update
  189.8 0.0 all-reduce.7.cloned.1.call-start
  189.8 150.8 %all-reduce.9.cloned.1.call-done = (f32[256,512]{0,1:T(8,128)}, f32[256,512]{0,1:T(8,128)}) async-done(((f32[256,512]{0,1:T(8,128)}, f32[256,512]{0,1:T(8,128)}), (f32[256,512]{0,1:T(8,128)}, f32[256,512]{0,1:T(8,128)})) %all-reduce.9.cloned.1.call-update) | async-done | bytes 1048592 | tf_op jit(solution)/shard_map/psum | solution.py:57
  340.7 1.4 collective-permute-start.2
  342.1 7.8 %collective-permute-start.3 = (f32[1,256,512]{1,2,0:T(8,128)}, f32[1,256,512]{1,2,0:T(8,128)S(1)}, u32[]{:S(2)}, u32[]{:S(2)}) collective-permute-start(f32[1,256,512]{1,2,0:T(8,128)} %bitcast.34), channel_id=1, source_target_pairs={{32,0},{64,32},{96,64},{128,96},{160,128},{192,160},{224,192},{33,... | collective-permute-start | bytes 1572872 | tf_op jit(solution)/shard_map/ppermute | solution.py:25
  349.9 0.0 collective-permute-done.2
  349.9 1.1 bitcast_select_fusion.3
  351.1 0.3 collective-permute-done.3
  351.4 0.1 bitcast_select_fusion.2
  351.5 2.5 fusion.39
  354.0 7.1 %collective-permute-start.4 = (f32[256,768]{0,1:T(8,128)S(1)}, f32[256,768]{0,1:T(8,128)}, u32[]{:S(2)}, u32[]{:S(2)}) collective-permute-start(f32[256,768]{0,1:T(8,128)S(1)} %fusion.39), channel_id=1, source_target_pairs={{0,32},{32,0},{64,96},{96,64},{128,160},{160,128},{192,224},{224,1... | collective-permute-start | bytes 2359304 | tf_op jit(solution)/shard_map/ppermute | solution.py:12
  361.1 2.0 collective-permute-done.4
  363.1 6.8 %fusion.2 = f32[2048,768]{0,1:T(8,128)S(1)} fusion(f32[2048,256]{0,1:T(8,128)} %copy-done.3, f32[2048,256]{0,1:T(8,128)S(1)} %get-tuple-element.19, pred[]{:T(512)S(6)} %lt.34, f32[256,768]{0,1:T(8,128)} %collective-permute-done.4, f32[256,768]{0,1:T(8,128)S(1)} %fusion.39, pred[]{:T(512)S(6)} %ne.44), kind=kOutput, calls=%fused_computation.15 | convolution fusion | flops 4832559104 | bytes 12058626 | tf_op jit(solution)/shard_map/dot_general | solution.py:76
  370.0 3.2 slice_subtract_fusion.1
  373.2 0.0 copy-start
  373.2 0.0 copy-start.10
  373.2 1.3 copy-done
  374.5 0.7 copy-done.10
  375.2 0.9 maximum_select_fusion.4
  376.1 0.8 maximum_select_fusion.5
  376.9 0.0 all-reduce.7.cloned.1.call-update
  376.9 144.9 %all-reduce.7.cloned.1.call-done = (f32[256,512]{0,1:T(8,128)}, f32[256,512]{0,1:T(8,128)}) async-done(((f32[256,512]{0,1:T(8,128)}, f32[256,512]{0,1:T(8,128)}), (f32[256,512]{0,1:T(8,128)}, f32[256,512]{0,1:T(8,128)})) %all-reduce.7.cloned.1.call-update) | async-done | bytes 1048592 | tf_op jit(solution)/shard_map/psum | solution.py:57
  521.8 1.4 collective-permute-start.5
  523.2 7.6 %collective-permute-start.6 = (f32[1,256,512]{1,2,0:T(8,128)}, f32[1,256,512]{1,2,0:T(8,128)S(1)}, u32[]{:S(2)}, u32[]{:S(2)}) collective-permute-start(f32[1,256,512]{1,2,0:T(8,128)} %bitcast.35), channel_id=1, source_target_pairs={{32,0},{64,32},{96,64},{128,96},{160,128},{192,160},{224,192},{33,... | collective-permute-start | bytes 1572872 | tf_op jit(solution)/shard_map/ppermute | solution.py:25
  530.9 1.1 bitcast_select_fusion.1
  532.1 0.5 collective-permute-done.6
  532.6 0.1 bitcast_select_fusion
  532.7 2.5 fusion.36
  535.2 0.0 copy-start.14
  535.2 7.1 %collective-permute-start.7 = (f32[256,768]{0,1:T(8,128)S(1)}, f32[256,768]{0,1:T(8,128)}, u32[]{:S(2)}, u32[]{:S(2)}) collective-permute-start(f32[256,768]{0,1:T(8,128)S(1)} %fusion.36), channel_id=1, source_target_pairs={{0,32},{32,0},{64,96},{96,64},{128,160},{160,128},{192,224},{224,1... | collective-permute-start | bytes 2359304 | tf_op jit(solution)/shard_map/ppermute | solution.py:12
  542.3 2.0 collective-permute-done.7
  544.3 1.2 broadcast_select_fusion
  545.6 2.1 collective-permute-start.8
  547.6 17.7 %collective-permute-done.8 = f32[256,768]{0,1:T(8,128)} collective-permute-done((f32[256,768]{0,1:T(8,128)S(1)}, f32[256,768]{0,1:T(8,128)}, u32[]{:S(2)}, u32[]{:S(2)}) %collective-permute-start.8) | collective-permute-done | bytes 786464 | tf_op jit(solution)/shard_map/ppermute | solution.py:12
  565.3 6.8 %fusion = f32[2048,768]{0,1:T(8,128)S(1)} fusion(f32[2048,256]{0,1:T(8,128)} %copy-done, f32[2048,256]{0,1:T(8,128)S(1)} %get-tuple-element.16, pred[]{:T(512)S(6)} %lt.32, f32[256,768]{0,1:T(8,128)} %collective-permute-done.8, f32[256,768]{0,1:T(8,128)S(1)} %broadcast_select_fusion, pred[]{:T(512)S(6)} %ne.47), kind=kOutput, calls=%fused_computation.11 | convolution fusion | flops 4832559104 | bytes 12058626 | tf_op jit(solution)/shard_map/dot_general | solution.py:76
  572.2 3.2 slice_subtract_fusion
  575.4 2.9 copy.21
  578.2 3.0 copy.20
  581.3 1.8 copy.19
  (44 shorter events, 0.4 us)
Async XLA Ops:
  7.2 156.3 %all-reduce.11.cloned.1.call-start = ((), (), s32[]{:S(2)}) async-start(), calls=%async_computation.2 | async-start | bytes 2097152 | tf_op jit(solution)/shard_map/psum | solution.py:57
  9.2 3.7 copy-start.5
  12.8 2.1 slice-start
  12.8 2.1 slice-start.1
  14.8 1.7 copy-start.8
  16.5 324.2 %all-reduce.9.cloned.1.call-start = ((), (), s32[]{:S(2)}) async-start(), calls=%async_computation.1 | async-start | bytes 2097152 | tf_op jit(solution)/shard_map/psum | solution.py:57
  163.4 10.7 %copy-start.15 = (f32[256,512]{0,1:T(8,128)S(1)}, f32[256,512]{0,1:T(8,128)}, u32[]{:S(2)}) copy-start(f32[256,512]{0,1:T(8,128)} %get-tuple-element.10) | copy-start | bytes 1572868
  163.4 9.1 %collective-permute-start = (f32[1,256,512]{1,2,0:T(8,128)}, f32[1,256,512]{1,2,0:T(8,128)S(1)}, u32[]{:S(2)}, u32[]{:S(2)}) collective-permute-start(f32[1,256,512]{1,2,0:T(8,128)} %bitcast.33), channel_id=1, source_target_pairs={{0,32},{32,64},{64,96},{96,128},{128,160},{160,192},{192,224},{1,3... | collective-permute-start | bytes 1572872 | tf_op jit(solution)/shard_map/ppermute | solution.py:23
  164.9 9.3 %collective-permute-start.1 = (f32[1,256,512]{1,2,0:T(8,128)}, f32[1,256,512]{1,2,0:T(8,128)S(1)}, u32[]{:S(2)}, u32[]{:S(2)}) collective-permute-start(f32[1,256,512]{1,2,0:T(8,128)} %bitcast.32), channel_id=1, source_target_pairs={{32,0},{64,32},{96,64},{128,96},{160,128},{192,160},{224,192},{33,... | collective-permute-start | bytes 1572872 | tf_op jit(solution)/shard_map/ppermute | solution.py:25
  174.3 2.7 copy-start.6
  174.3 2.7 copy-start.7
  177.0 5.7 copy-start.9
  185.6 1.3 copy-start.3
  185.6 177.5 %copy-start.2 = (f32[2048,256]{0,1:T(8,128)}, f32[2048,256]{0,1:T(8,128)S(1)}, u32[]{:S(2)}) copy-start(f32[2048,256]{0,1:T(8,128)S(1)} %get-tuple-element.19) | copy-start | bytes 6291460
  189.8 332.1 %all-reduce.7.cloned.1.call-start = ((), (), s32[]{:S(2)}) async-start(), calls=%async_computation | async-start | bytes 2097152 | tf_op jit(solution)/shard_map/psum | solution.py:57
  340.6 10.7 %copy-start.16 = (f32[256,512]{0,1:T(8,128)S(1)}, f32[256,512]{0,1:T(8,128)}, u32[]{:S(2)}) copy-start(f32[256,512]{0,1:T(8,128)} %get-tuple-element.8) | copy-start | bytes 1572868
  340.7 9.2 %collective-permute-start.2 = (f32[1,256,512]{1,2,0:T(8,128)}, f32[1,256,512]{1,2,0:T(8,128)}, u32[]{:S(2)}, u32[]{:S(2)}) collective-permute-start(f32[1,256,512]{1,2,0:T(8,128)} %bitcast.36), channel_id=1, source_target_pairs={{0,32},{32,64},{64,96},{96,128},{128,160},{160,192},{192,224},{1,3... | collective-permute-start | bytes 1572872 | tf_op jit(solution)/shard_map/ppermute | solution.py:23
  342.1 9.3 %collective-permute-start.3 = (f32[1,256,512]{1,2,0:T(8,128)}, f32[1,256,512]{1,2,0:T(8,128)S(1)}, u32[]{:S(2)}, u32[]{:S(2)}) collective-permute-start(f32[1,256,512]{1,2,0:T(8,128)} %bitcast.34), channel_id=1, source_target_pairs={{32,0},{64,32},{96,64},{128,96},{160,128},{192,160},{224,192},{33,... | collective-permute-start | bytes 1572872 | tf_op jit(solution)/shard_map/ppermute | solution.py:25
  354.0 9.1 %collective-permute-start.4 = (f32[256,768]{0,1:T(8,128)S(1)}, f32[256,768]{0,1:T(8,128)}, u32[]{:S(2)}, u32[]{:S(2)}) collective-permute-start(f32[256,768]{0,1:T(8,128)S(1)} %fusion.39), channel_id=1, source_target_pairs={{0,32},{32,0},{64,96},{96,64},{128,160},{160,128},{192,224},{224,1... | collective-permute-start | bytes 2359304 | tf_op jit(solution)/shard_map/ppermute | solution.py:12
  361.1 8.9 %copy-start.4 = (f32[2048,256]{0,1:T(8,128)S(1)}, f32[2048,256]{0,1:T(8,128)}, u32[]{:S(2)}) copy-start(f32[2048,256]{0,1:T(8,128)} %copy-done.3) | copy-start | bytes 6291460
  361.1 8.9 %copy-start.12 = (f32[2048,256]{0,1:T(8,128)S(1)}, f32[2048,256]{0,1:T(8,128)}, u32[]{:S(2)}) copy-start(f32[2048,256]{0,1:T(8,128)} %get-tuple-element.18) | copy-start | bytes 6291460
  373.2 1.3 copy-start
  373.2 2.0 copy-start.10
  521.8 10.7 %copy-start.17 = (f32[256,512]{0,1:T(8,128)S(1)}, f32[256,512]{0,1:T(8,128)}, u32[]{:S(2)}) copy-start(f32[256,512]{0,1:T(8,128)} %get-tuple-element.6) | copy-start | bytes 1572868
  521.8 9.1 %collective-permute-start.5 = (f32[1,256,512]{1,2,0:T(8,128)}, f32[1,256,512]{1,2,0:T(8,128)}, u32[]{:S(2)}, u32[]{:S(2)}) collective-permute-start(f32[1,256,512]{1,2,0:T(8,128)} %bitcast.37), channel_id=1, source_target_pairs={{0,32},{32,64},{64,96},{96,128},{128,160},{160,192},{192,224},{1,3... | collective-permute-start | bytes 1572872 | tf_op jit(solution)/shard_map/ppermute | solution.py:23
  523.2 9.3 %collective-permute-start.6 = (f32[1,256,512]{1,2,0:T(8,128)}, f32[1,256,512]{1,2,0:T(8,128)S(1)}, u32[]{:S(2)}, u32[]{:S(2)}) collective-permute-start(f32[1,256,512]{1,2,0:T(8,128)} %bitcast.35), channel_id=1, source_target_pairs={{32,0},{64,32},{96,64},{128,96},{160,128},{192,160},{224,192},{33,... | collective-permute-start | bytes 1572872 | tf_op jit(solution)/shard_map/ppermute | solution.py:25
  535.2 7.1 %copy-start.14 = (f32[256,768]{0,1:T(8,128)}, f32[256,768]{0,1:T(8,128)S(1)}, u32[]{:S(2)}) copy-start(f32[256,768]{0,1:T(8,128)S(1)} %fusion.36) | copy-start | bytes 2359300
  535.2 9.1 %collective-permute-start.7 = (f32[256,768]{0,1:T(8,128)S(1)}, f32[256,768]{0,1:T(8,128)}, u32[]{:S(2)}, u32[]{:S(2)}) collective-permute-start(f32[256,768]{0,1:T(8,128)S(1)} %fusion.36), channel_id=1, source_target_pairs={{0,32},{32,0},{64,96},{96,64},{128,160},{160,128},{192,224},{224,1... | collective-permute-start | bytes 2359304 | tf_op jit(solution)/shard_map/ppermute | solution.py:12
  545.6 19.8 %collective-permute-start.8 = (f32[256,768]{0,1:T(8,128)S(1)}, f32[256,768]{0,1:T(8,128)}, u32[]{:S(2)}, u32[]{:S(2)}) collective-permute-start(f32[256,768]{0,1:T(8,128)S(1)} %broadcast_select_fusion), channel_id=1, source_target_pairs={{0,64},{32,96},{64,0},{96,32},{128,192},{160,224},{192,128},{224,1... | collective-permute-start | bytes 2359304 | tf_op jit(solution)/shard_map/ppermute | solution.py:12
  547.6 24.5 %copy-start.1 = (f32[2048,256]{0,1:T(8,128)S(1)}, f32[2048,256]{0,1:T(8,128)}, u32[]{:S(2)}) copy-start(f32[2048,256]{0,1:T(8,128)} %copy-done) | copy-start | bytes 6291460
  547.6 24.5 %copy-start.11 = (f32[2048,256]{0,1:T(8,128)S(1)}, f32[2048,256]{0,1:T(8,128)}, u32[]{:S(2)}) copy-start(f32[2048,256]{0,1:T(8,128)} %copy-done.10) | copy-start | bytes 6291460
  578.2 3.0 copy-start.13
Sparse Core Ops, SparseCore 0:
  16.2 147.1 all-reduce.10
  189.9 150.7 all-reduce.8
  377.0 144.7 all-reduce.6
where the time goes:
time: 595 us; the launch traced here: 590 us
  waiting for transfers between devices  467 us (78%)
  starting transfers between devices  43.6 us (7%)
  matrix products  26.8 us (5%)
  local copies, waits for them, and re-layouts  20.5 us (3%)
  other arithmetic  17.6 us (3%)
  between operations  14.2 us (2%)
    psum x3, waiting for transfers between devices, on_device(): lax.psum((jnp.where(row_pos == 0, top_tip, 0.0), jnp.where(row_pos == row...  443 us
    ppermute x3, starting transfers between devices, extended(): lax.ppermute(head, axis, [((i + 1) % count, i) for i in range(ends)])  23 us
    ppermute x3, waiting for transfers between devices, partner_2(): lax.ppermute(x, axis, [(i, i ^ 1 << distance) for i in range(lax.axis_siz...  21.8 us
    dot_general x3, matrix products, on_device(): jnp.dot(driver, solved, precision=precise, preferred_element_type=jnp.flo...  19.3 us
    unnamed x42, local copies, waits for them, and re-layouts  18.9 us
    ppermute x3, starting transfers between devices, partner_2(): lax.ppermute(x, axis, [(i, i ^ 1 << distance) for i in range(lax.axis_siz...  16.3 us
  transfers between devices with their start and end apart: 12, of which 9 were waited for; matrix products, arithmetic and copies ran while one was open for 0% of the time, Pallas kernels for 0%

commit v1 on v0

v1 whole, which is shorter than its diff:
```python
import jax
import jax.numpy as jnp
from jax import lax
from jax.sharding import PartitionSpec as P

HALF_BAND = 256
LOAD_COLS = 256
LEVELS = 3


def partner_2(x, axis, distance):
    return lax.ppermute(x, axis, [(i, i ^ 1 << distance) for i in range(lax.axis_size(axis))])


def spread_block(block, level, chain_pos, side_low):
    source_bit = jnp.where(side_low, 1, 0)
    for bit in range(level):
        partner = partner_2(block, "chain", bit)
        own_bit = chain_pos // 2**bit % 2
        block = jnp.where(own_bit != source_bit, partner, block)
    return block


def spread_tips(top, bottom, row_pos, count):
    step = count // 2
    while step >= 1:
        pairs = [(s, s + step) for s in range(0, count, 2 * step)]
        pairs += [(s, s - step) for s in range(2 * step - 1, count, 2 * step)]
        sent = jnp.where(row_pos % (2 * step) == 0, top, bottom)
        got = lax.ppermute(sent, "rows", pairs)
        top = jnp.where(row_pos % (2 * step) == step, got, top)
        bottom = jnp.where(row_pos % (2 * step) == step - 1, got, bottom)
        step //= 2
    return top, bottom


def on_device(right_spike, left_spike, loads, tip_inverse):
    precise = lax.Precision.HIGHEST
    band = HALF_BAND
    width = LOAD_COLS
    chain_pos = lax.axis_index("chain")
    row_pos = lax.axis_index("rows")
    chain_count = lax.axis_size("chain")
    spike_right = right_spike
    spike_left = left_spike
    load_block = loads
    top, bottom = spread_tips(
        jnp.concatenate([load_block[:band], spike_right[:band]], 1),
        jnp.concatenate([load_block[-band:], spike_left[-band:]], 1),
        row_pos,
        lax.axis_size("rows"),
    )
    blank_block = jnp.zeros((band, band), jnp.float32)
    for level in range(LEVELS):
        half = 2**level
        place = chain_pos % (2 * half)
        side_low = place < half
        lasts = list(range(half - 1, chain_count - 1, 2 * half))
        next_top = lax.ppermute(top, "chain", [(a + 1, a) for a in lasts])
        prev_bottom = lax.ppermute(bottom, "chain", [(a, a + 1) for a in lasts])
        lower_tip = jnp.where(side_low, bottom, prev_bottom)
        upper_tip = jnp.where(side_low, next_top, top)
        upper_rows = jnp.concatenate([lower_tip[:, :band], lower_tip[:, band:], blank_block], 1)
        lower_rows = jnp.concatenate([upper_tip[:, :band], blank_block, upper_tip[:, band:]], 1)
        tip_rhs = jnp.concatenate([upper_rows, lower_rows], 0)
        solved = jnp.dot(
            tip_inverse[0, level], tip_rhs, precision=precise, preferred_element_type=jnp.float32
        )
        solved = spread_block(solved, level, chain_pos, side_low)
        if level + 1 < LEVELS:
            bottom_prod = jnp.dot(
                bottom[:, band:], solved[:, : 2 * band], precision=precise, preferred_element_type=jnp.float32
            )
            bottom = jnp.concatenate([bottom[:, :band] - bottom_prod[:, :band], -bottom_prod[:, band:]], 1)
            top_prod = jnp.dot(
                top[:, band:],
                jnp.concatenate([solved[:, :band], solved[:, 2 * band :]], 1),
                precision=precise,
                preferred_element_type=jnp.float32,
            )
            top = jnp.concatenate([top[:, :band] - top_prod[:, :band], -top_prod[:, band:]], 1)
        driver = jnp.where(side_low, spike_right, spike_left)
        product = jnp.dot(driver, solved, precision=precise, preferred_element_type=jnp.float32)
        left_term = product[:, width : width + band]
        right_term = product[:, width + band :]
        load_block = load_block - product[:, :width]
        new_left = jnp.where(side_low, spike_left - left_term, -left_term)
        new_right = jnp.where(side_low, -right_term, spike_right - right_term)
        spike_left = new_left
        spike_right = new_right
    return (spike_right, spike_left, load_block)


def solution(mesh):
    in_specs = (
        P(("chain", "rows"), None),
        P(("chain", "rows"), None),
        P(("chain", "rows"), None),
        P("chain", None, None, None),
    )
    out_specs = (P(("chain", "rows"), None), P(("chain", "rows"), None), P(("chain", "rows"), None))
    return jax.shard_map(
        on_device, mesh=mesh, in_specs=in_specs, out_specs=out_specs, check_vma=False
    )
```

time: 595 us -> 177 us (0.30)
  the two profiles are of different devices: /device:TPU:31 before, /device:TPU:12 now
where the time goes in v1:
time: 177 us
  waiting for transfers between devices  91.7 us (52%)
  matrix products  34.3 us (19%)
  starting transfers between devices  25.2 us (14%)
  other arithmetic  18 us (10%)
  local copies, waits for them, and re-layouts  6.09 us (3%)
    ppermute x5, waiting for transfers between devices, spread_tips(): got = lax.ppermute(sent, 'rows', pairs)  69.4 us
    dot_general x3, matrix products, on_device(): jnp.dot(driver, solved, precision=precise, preferred_element_type=jnp.flo...  20.8 us
    ppermute x3, waiting for transfers between devices, partner_2(): lax.ppermute(x, axis, [(i, i ^ 1 << distance) for i in range(lax.axis_siz...  11.9 us
    dot_general x3, matrix products, on_device(): jnp.dot(tip_inverse[0, level], tip_rhs, precision=precise, preferred_elem...  11.1 us
    ppermute x3, starting transfers between devices, partner_2(): lax.ppermute(x, axis, [(i, i ^ 1 << distance) for i in range(lax.axis_siz...  9.53 us
    sub x1, other arithmetic, on_device(): load_block = load_block - product[:, :width]  6.59 us
    ppermute x3, waiting for transfers between devices, on_device(): prev_bottom = lax.ppermute(bottom, 'chain', [(a, a + 1) for a in lasts])  6.52 us
    ppermute x3, starting transfers between devices, on_device(): next_top = lax.ppermute(top, 'chain', [(a + 1, a) for a in lasts])  6.19 us
  transfers between devices with their start and end apart: 14, of which 7 were waited for; matrix products, arithmetic and copies ran while one was open for 10% of the time, Pallas kernels for 0%

profile of v1, /device:TPU:12, one launch (start us, length us, event | category | flops | bytes accessed | tf_op | source)
XLA Modules:
  0.0 176.6 jit_solution(15522553636641197536)
XLA Ops:
  0.6 1.0 slice.130
  1.6 1.0 slice.132
  2.6 1.1 fusion.83
  3.7 0.1 fusion.65
  3.7 0.7 collective-permute-start
  4.5 0.0 collective-permute-done
  4.5 0.2 broadcast_select_fusion.10
  4.7 0.7 collective-permute-start.1
  5.4 0.0 collective-permute-done.1
  5.4 0.2 broadcast_select_fusion.12
  5.6 1.5 collective-permute-start.2
  7.1 0.0 collective-permute-done.2
  7.1 1.3 broadcast_select_fusion.14
  8.3 1.3 collective-permute-start.3
  9.7 60.2 %collective-permute-done.3 = f32[256,512]{1,0:T(8,128)S(1)} collective-permute-done((f32[256,512]{1,0:T(8,128)S(1)}, f32[256,512]{1,0:T(8,128)S(1)}, u32[]{:S(2)}, u32[]{:S(2)}) %collective-permute-start.3) | collective-permute-done | bytes 524320 | tf_op jit(solution)/shard_map/ppermute | solution.py:30
  69.9 0.2 broadcast_select_fusion.17
  70.0 0.1 collective-permute-start.4
  70.1 9.2 %collective-permute-done.4 = f32[256,512]{1,0:T(8,128)S(1)} collective-permute-done((f32[256,512]{1,0:T(8,128)S(1)}, f32[256,512]{1,0:T(8,128)S(1)}, u32[]{:S(2)}, u32[]{:S(2)}) %collective-permute-start.4) | collective-permute-done | bytes 524320 | tf_op jit(solution)/shard_map/ppermute | solution.py:30
  79.3 0.2 broadcast_select_fusion.6
  79.5 1.3 collective-permute-start.6
  80.8 3.1 %collective-permute-start.5 = (f32[256,512]{1,0:T(8,128)S(1)}, f32[256,512]{1,0:T(8,128)S(1)}, u32[]{:S(2)}, u32[]{:S(2)}) collective-permute-start(f32[256,512]{1,0:T(8,128)S(1)} %get-tuple-element.17), channel_id=1, source_target_pairs={{0,32},{64,96},{128,160},{192,224},{1,33},{65,97},{129,161},{193,2... | collective-permute-start | bytes 1572872 | tf_op jit(solution)/shard_map/ppermute | solution.py:60
  83.9 0.1 broadcast_select_fusion.18
  84.1 1.3 collective-permute-done.5
  85.4 0.1 broadcast_select_fusion.19
  85.5 3.4 %fusion.8 = f32[768,256]{1,0:T(8,128)S(1)} fusion(f32[256,256]{1,0:T(8,128)S(1)} %broadcast_in_dim.3, f32[256,512]{1,0:T(8,128)S(1)} %broadcast_select_fusion.19, f32[256,256]{1,0:T(8,128)S(1)} %get-tuple-element.35, f32[256,256]{1,0:T(8,128)S(1)} %get-tuple-element.34, f32[1,3,256,512]{3,2,1,0:T(8,128)} %param.7), kind=kOutput, calls=%fused_computation.20 | convolution fusion | flops 1209925632 | bytes 2621440 | tf_op jit(solution)/shard_map/dot_general | solution.py:66
  89.0 0.0 copy-start.6
  89.0 0.6 fusion.48
  89.6 0.6 fusion.50
  90.3 0.1 slice_subtract_fusion.5
  90.4 0.9 pad_maximum_fusion.6
  91.3 1.4 collective-permute-start.8
  92.7 0.1 pad_maximum_fusion.5
  92.8 0.7 collective-permute-start.7
  93.5 1.2 broadcast_select_fusion.4
  94.7 0.1 broadcast_select_fusion.5
  94.8 3.3 %fusion.33 = f32[256,768]{0,1:T(8,128)S(1)} fusion(f32[256,256]{1,0:T(8,128)S(1)} %copy-done.8, f32[256,512]{1,0:T(8,128)S(1)} %broadcast_select_fusion.5, f32[256,256]{1,0:T(8,128)S(1)} %get-tuple-element.29, f32[256,256]{1,0:T(8,128)S(1)} %get-tuple-element.28, f32[1,3,256,512]{3,2,1,0:T(8,128)} %param.7), kind=kOutput, calls=%fused_computation.41 | convolution fusion | flops 1209925632 | bytes 2621440 | tf_op jit(solution)/shard_map/dot_general | solution.py:66
  98.1 9.5 %collective-permute-start.9 = (f32[256,768]{0,1:T(8,128)S(1)}, f32[256,768]{0,1:T(8,128)}, u32[]{:S(2)}, u32[]{:S(2)}) collective-permute-start(f32[256,768]{0,1:T(8,128)S(1)} %fusion.33), channel_id=1, source_target_pairs={{0,32},{32,0},{64,96},{96,64},{128,160},{160,128},{192,224},{224,1... | collective-permute-start | bytes 2359304 | tf_op jit(solution)/shard_map/ppermute | solution.py:12
  107.7 2.0 %collective-permute-done.9 = f32[256,768]{0,1:T(8,128)} collective-permute-done((f32[256,768]{0,1:T(8,128)S(1)}, f32[256,768]{0,1:T(8,128)}, u32[]{:S(2)}, u32[]{:S(2)}) %collective-permute-start.9) | collective-permute-done | bytes 786464 | tf_op jit(solution)/shard_map/ppermute | solution.py:12
  109.7 1.2 broadcast_select_fusion.1
  111.0 0.6 fusion.54
  111.6 0.1 slice_subtract_fusion.3
  111.7 0.9 pad_maximum_fusion.8
  112.5 3.4 %collective-permute-start.11 = (f32[256,512]{1,0:T(8,128)}, f32[256,512]{1,0:T(8,128)S(1)}, u32[]{:S(2)}, u32[]{:S(2)}) collective-permute-start(f32[256,512]{1,0:T(8,128)} %pad_maximum_fusion.8), channel_id=1, source_target_pairs={{128,96},{129,97},{130,98},{131,99},{132,100},{133,101},{134,102},... | collective-permute-start | bytes 1572872 | tf_op jit(solution)/shard_map/ppermute | solution.py:59
  116.0 0.6 fusion.46
  116.6 0.1 slice_subtract_fusion.4
  116.7 0.9 pad_maximum_fusion.7
  117.6 1.5 collective-permute-start.10
  119.1 3.9 %collective-permute-done.11 = f32[256,512]{1,0:T(8,128)S(1)} collective-permute-done((f32[256,512]{1,0:T(8,128)}, f32[256,512]{1,0:T(8,128)S(1)}, u32[]{:S(2)}, u32[]{:S(2)}) %collective-permute-start.11) | collective-permute-done | bytes 524320 | tf_op jit(solution)/shard_map/ppermute | solution.py:59
  123.0 0.1 broadcast_select_fusion.2
  123.1 5.2 %collective-permute-done.10 = f32[256,512]{1,0:T(8,128)S(1)} collective-permute-done((f32[256,512]{1,0:T(8,128)}, f32[256,512]{1,0:T(8,128)S(1)}, u32[]{:S(2)}, u32[]{:S(2)}) %collective-permute-start.10) | collective-permute-done | bytes 524320 | tf_op jit(solution)/shard_map/ppermute | solution.py:60
  128.3 0.1 broadcast_select_fusion.3
  128.3 0.0 copy-start.3
  128.4 4.4 %fusion.30 = f32[256,768]{0,1:T(8,128)} fusion(f32[256,256]{1,0:T(8,128)S(1)} %copy-done.9, f32[256,512]{1,0:T(8,128)S(1)} %broadcast_select_fusion.3, f32[256,256]{1,0:T(8,128)S(1)} %get-tuple-element.23, f32[256,256]{1,0:T(8,128)S(1)} %get-tuple-element.22, f32[1,3,256,512]{3,2,1,0:T(8,128)} %param.7), kind=kOutput, calls=%fused_computation.40 | convolution fusion | flops 1209925632 | bytes 2621440 | tf_op jit(solution)/shard_map/dot_general | solution.py:66
  132.7 7.7 %fusion.4 = f32[2048,768]{1,0:T(8,128)S(1)} fusion(f32[768,256]{1,0:T(8,128)} %copy-done.6, f32[2048,256]{1,0:T(8,128)} %param.4, f32[2048,256]{1,0:T(8,128)S(1)} %copy-done.3, pred[]{:T(512)S(6)} %lt.76), kind=kOutput, calls=%fused_computation.16 | convolution fusion | flops 4832362496 | bytes 11272193 | tf_op jit(solution)/shard_map/dot_general | solution.py:83
  140.5 0.0 copy-start.4
  140.5 2.9 %broadcast_select_fusion = f32[256,768]{0,1:T(8,128)} fusion(f32[256,768]{0,1:T(8,128)} %collective-permute-done.12, f32[256,768]{0,1:T(8,128)} %fusion.30, pred[]{:T(512)S(6)} %ne.93), kind=kLoop, calls=%fused_computation.79 | loop fusion | flops 196608 | bytes 2359297 | tf_op jit(solution)/shard_map/jit(_where)/select_n | solution.py:20
  143.4 0.0 collective-permute-start.13
  143.4 1.1 copy-done.4
  144.5 6.1 %fusion.2 = f32[2048,768]{1,0:T(8,128)S(1)} fusion(f32[256,768]{0,1:T(8,128)S(1)} %broadcast_select_fusion.1, pred[]{:T(512)S(6)} %lt.74, f32[2048,256]{1,0:T(8,128)S(1)} %copy-done.5, f32[2048,768]{1,0:T(8,128)S(1)} %fusion.4, pred[]{:T(512)S(6)} %lt.76, f32[2048,256]{1,0:T(8,128)S(1)} %copy-done.4), kind=kOutput, calls=%fused_computation.12 | convolution fusion | flops 4835508224 | bytes 15466498 | tf_op jit(solution)/shard_map/dot_general | solution.py:83
  150.5 0.8 negate_select_fusion.1
  151.4 1.8 copy-done.2
  153.2 9.8 %collective-permute-done.13 = f32[256,768]{0,1:T(8,128)} collective-permute-done((f32[256,768]{0,1:T(8,128)}, f32[256,768]{0,1:T(8,128)}, u32[]{:S(2)}, u32[]{:S(2)}) %collective-permute-start.13) | collective-permute-done | bytes 786464 | tf_op jit(solution)/shard_map/ppermute | solution.py:12
  163.0 7.0 %fusion = f32[2048,768]{1,0:T(8,128)S(1)} fusion(f32[2048,256]{1,0:T(8,128)S(1)} %get-tuple-element.10, f32[2048,256]{1,0:T(8,128)S(1)} %get-tuple-element.9, pred[]{:T(512)S(6)} %lt.72, f32[256,768]{0,1:T(8,128)} %collective-permute-done.13, f32[256,768]{0,1:T(8,128)} %broadcast_select_fusion, pred[]{:T(512)S(6)} %ne.92), kind=kOutput, calls=%fused_computation.8 | convolution fusion | flops 4832559104 | bytes 12058626 | tf_op jit(solution)/shard_map/dot_general | solution.py:83
  170.0 6.6 %slice_subtract_fusion = (f32[2048,256]{1,0:T(8,128)}, f32[2048,256]{1,0:T(8,128)}, f32[2048,256]{1,0:T(8,128)}) fusion(f32[2048,768]{1,0:T(8,128)S(1)} %fusion, f32[2048,768]{1,0:T(8,128)} %copy-done.2, f32[2048,256]{1,0:T(8,128)} %param.6, f32[2048,768]{1,0:T(8,128)} %copy-done, f32[2048,256]{1,0:T(8,128)S(1)} %get-tuple-element.9, pred[]{:T(512)S(6)} %lt.72, ...), kind=kLoop, calls=%fused_computation.3 | loop fusion | flops 4718592 | bytes 23068672 | tf_op jit(solution)/shard_map/sub | solution.py:86
  (26 shorter events, 0.2 us)
Async XLA Ops:
  3.7 0.7 collective-permute-start
  4.7 0.7 collective-permute-start.1
  5.6 1.5 collective-permute-start.2
  8.3 61.5 %collective-permute-start.3 = (f32[256,512]{1,0:T(8,128)S(1)}, f32[256,512]{1,0:T(8,128)S(1)}, u32[]{:S(2)}, u32[]{:S(2)}) collective-permute-start(f32[256,512]{1,0:T(8,128)S(1)} %get-tuple-element.3), channel_id=1, source_target_pairs={{0,2},{4,6},{8,10},{12,14},{16,18},{20,22},{24,26},{28,30},{3,1},{... | collective-permute-start | bytes 1572872 | tf_op jit(solution)/shard_map/ppermute | solution.py:30
  70.0 9.3 %collective-permute-start.4 = (f32[256,512]{1,0:T(8,128)S(1)}, f32[256,512]{1,0:T(8,128)S(1)}, u32[]{:S(2)}, u32[]{:S(2)}) collective-permute-start(f32[256,512]{1,0:T(8,128)S(1)} %broadcast_select_fusion.17), channel_id=1, source_target_pairs={{0,1},{2,3},{4,5},{6,7},{8,9},{10,11},{12,13},{14,15},{16,17},{18,... | collective-permute-start | bytes 1572872 | tf_op jit(solution)/shard_map/ppermute | solution.py:30
  79.5 4.4 %collective-permute-start.6 = (f32[256,512]{1,0:T(8,128)S(1)}, f32[256,512]{1,0:T(8,128)S(1)}, u32[]{:S(2)}, u32[]{:S(2)}) collective-permute-start(f32[256,512]{1,0:T(8,128)S(1)} %get-tuple-element.16), channel_id=1, source_target_pairs={{32,0},{96,64},{160,128},{224,192},{33,1},{97,65},{161,129},{225,1... | collective-permute-start | bytes 1572872 | tf_op jit(solution)/shard_map/ppermute | solution.py:59
  80.8 4.6 %collective-permute-start.5 = (f32[256,512]{1,0:T(8,128)S(1)}, f32[256,512]{1,0:T(8,128)S(1)}, u32[]{:S(2)}, u32[]{:S(2)}) collective-permute-start(f32[256,512]{1,0:T(8,128)S(1)} %get-tuple-element.17), channel_id=1, source_target_pairs={{0,32},{64,96},{128,160},{192,224},{1,33},{65,97},{129,161},{193,2... | collective-permute-start | bytes 1572872 | tf_op jit(solution)/shard_map/ppermute | solution.py:60
  85.5 3.4 %copy-start.7 = (f32[256,256]{1,0:T(8,128)}, f32[256,256]{1,0:T(8,128)S(1)}, u32[]{:S(2)}) copy-start(f32[256,256]{1,0:T(8,128)S(1)} %broadcast_in_dim.3) | copy-start | bytes 786436
  89.0 1.5 copy-start.6
  91.3 2.2 %collective-permute-start.8 = (f32[256,512]{1,0:T(8,128)}, f32[256,512]{1,0:T(8,128)}, u32[]{:S(2)}, u32[]{:S(2)}) collective-permute-start(f32[256,512]{1,0:T(8,128)} %pad_maximum_fusion.6), channel_id=1, source_target_pairs={{64,32},{192,160},{65,33},{193,161},{66,34},{194,162},{67,35},{195... | collective-permute-start | bytes 1572872 | tf_op jit(solution)/shard_map/ppermute | solution.py:59
  92.8 1.9 %collective-permute-start.7 = (f32[256,512]{1,0:T(8,128)S(1)}, f32[256,512]{1,0:T(8,128)S(1)}, u32[]{:S(2)}, u32[]{:S(2)}) collective-permute-start(f32[256,512]{1,0:T(8,128)S(1)} %pad_maximum_fusion.5), channel_id=1, source_target_pairs={{32,64},{160,192},{33,65},{161,193},{34,66},{162,194},{35,67},{163... | collective-permute-start | bytes 1572872 | tf_op jit(solution)/shard_map/ppermute | solution.py:60
  93.5 1.3 copy-start.8
  98.1 11.6 %collective-permute-start.9 = (f32[256,768]{0,1:T(8,128)S(1)}, f32[256,768]{0,1:T(8,128)}, u32[]{:S(2)}, u32[]{:S(2)}) collective-permute-start(f32[256,768]{0,1:T(8,128)S(1)} %fusion.33), channel_id=1, source_target_pairs={{0,32},{32,0},{64,96},{96,64},{128,160},{160,128},{192,224},{224,1... | collective-permute-start | bytes 2359304 | tf_op jit(solution)/shard_map/ppermute | solution.py:12
  112.5 10.4 %collective-permute-start.11 = (f32[256,512]{1,0:T(8,128)}, f32[256,512]{1,0:T(8,128)S(1)}, u32[]{:S(2)}, u32[]{:S(2)}) collective-permute-start(f32[256,512]{1,0:T(8,128)} %pad_maximum_fusion.8), channel_id=1, source_target_pairs={{128,96},{129,97},{130,98},{131,99},{132,100},{133,101},{134,102},... | collective-permute-start | bytes 1572872 | tf_op jit(solution)/shard_map/ppermute | solution.py:59
  117.6 10.7 %collective-permute-start.10 = (f32[256,512]{1,0:T(8,128)}, f32[256,512]{1,0:T(8,128)S(1)}, u32[]{:S(2)}, u32[]{:S(2)}) collective-permute-start(f32[256,512]{1,0:T(8,128)} %pad_maximum_fusion.7), channel_id=1, source_target_pairs={{96,128},{97,129},{98,130},{99,131},{100,132},{101,133},{102,134},... | collective-permute-start | bytes 1572872 | tf_op jit(solution)/shard_map/ppermute | solution.py:60
  119.1 9.3 %copy-start.9 = (f32[256,256]{1,0:T(8,128)S(1)}, f32[256,256]{1,0:T(8,128)}, u32[]{:S(2)}) copy-start(f32[256,256]{1,0:T(8,128)} %copy-done.7) | copy-start | bytes 786436
  128.3 4.4 %copy-start.3 = (f32[2048,256]{1,0:T(8,128)S(1)}, f32[2048,256]{1,0:T(8,128)}, u32[]{:S(2)}) copy-start(f32[2048,256]{1,0:T(8,128)} %param.5) | copy-start | bytes 6291460
  132.7 7.8 %collective-permute-start.12 = (f32[256,768]{0,1:T(8,128)}, f32[256,768]{0,1:T(8,128)}, u32[]{:S(2)}, u32[]{:S(2)}) collective-permute-start(f32[256,768]{0,1:T(8,128)} %fusion.30), channel_id=1, source_target_pairs={{0,32},{32,0},{64,96},{96,64},{128,160},{160,128},{192,224},{224,1... | collective-permute-start | bytes 2359304 | tf_op jit(solution)/shard_map/ppermute | solution.py:12
  132.7 10.7 %copy-start.5 = (f32[2048,256]{1,0:T(8,128)S(1)}, f32[2048,256]{1,0:T(8,128)}, u32[]{:S(2)}) copy-start(f32[2048,256]{1,0:T(8,128)} %param.4) | copy-start | bytes 6291460
  140.5 10.0 %copy-start = (f32[2048,768]{1,0:T(8,128)}, f32[2048,768]{1,0:T(8,128)S(1)}, u32[]{:S(2)}) copy-start(f32[2048,768]{1,0:T(8,128)S(1)} %fusion.4) | copy-start | bytes 18874372
  140.5 4.0 %copy-start.4 = (f32[2048,256]{1,0:T(8,128)S(1)}, f32[2048,256]{1,0:T(8,128)}, u32[]{:S(2)}) copy-start(f32[2048,256]{1,0:T(8,128)} %param.5) | copy-start | bytes 6291460
  143.4 19.6 %collective-permute-start.13 = (f32[256,768]{0,1:T(8,128)}, f32[256,768]{0,1:T(8,128)}, u32[]{:S(2)}, u32[]{:S(2)}) collective-permute-start(f32[256,768]{0,1:T(8,128)} %broadcast_select_fusion), channel_id=1, source_target_pairs={{0,64},{32,96},{64,0},{96,32},{128,192},{160,224},{192,128},{224,1... | collective-permute-start | bytes 2359304 | tf_op jit(solution)/shard_map/ppermute | solution.py:12
  150.5 2.6 %copy-start.2 = (f32[2048,768]{1,0:T(8,128)}, f32[2048,768]{1,0:T(8,128)S(1)}, u32[]{:S(2)}) copy-start(f32[2048,768]{1,0:T(8,128)S(1)} %fusion.2) | copy-start | bytes 18874372
  153.2 9.9 %copy-start.1 = (f32[2048,256]{1,0:T(8,128)}, f32[2048,256]{1,0:T(8,128)S(1)}, u32[]{:S(2)}) copy-start(f32[2048,256]{1,0:T(8,128)S(1)} %get-tuple-element.10) | copy-start | bytes 6291460

commit v2 on v1

--- a/solution.py
+++ b/solution.py
@@ -8,30 +8,33 @@
 LEVELS = 3
 
 
-def partner_2(x, axis, distance):
-    return lax.ppermute(x, axis, [(i, i ^ 1 << distance) for i in range(lax.axis_size(axis))])
+def spread_tips(top, bottom, row_pos, count, fanouts):
+    stride = count
+    for fanout in fanouts:
+        step = stride // fanout
+        got_top = top
+        got_bottom = bottom
+        for k in range(1, fanout):
+            offset = k * step
+            pairs = [(s, s + offset) for s in range(0, count, stride)]
+            pairs += [(s, s - offset) for s in range(stride - 1, count, stride)]
+            sent = jnp.where(row_pos % stride == 0, top, bottom)
+            got = lax.ppermute(sent, "rows", pairs)
+            got_top = jnp.where(row_pos % stride == offset, got, got_top)
+            got_bottom = jnp.where(row_pos % stride == stride - 1 - offset, got, got_bottom)
+        top = got_top
+        bottom = got_bottom
+        stride = step
+    return top, bottom
 
 
-def spread_block(block, level, chain_pos, side_low):
-    source_bit = jnp.where(side_low, 1, 0)
-    for bit in range(level):
-        partner = partner_2(block, "chain", bit)
-        own_bit = chain_pos // 2**bit % 2
-        block = jnp.where(own_bit != source_bit, partner, block)
-    return block
-
-
-def spread_tips(top, bottom, row_pos, count):
-    step = count // 2
-    while step >= 1:
-        pairs = [(s, s + step) for s in range(0, count, 2 * step)]
-        pairs += [(s, s - step) for s in range(2 * step - 1, count, 2 * step)]
-        sent = jnp.where(row_pos % (2 * step) == 0, top, bottom)
-        got = lax.ppermute(sent, "rows", pairs)
-        top = jnp.where(row_pos % (2 * step) == step, got, top)
-        bottom = jnp.where(row_pos % (2 * step) == step - 1, got, bottom)
-        step //= 2
-    return top, bottom
+def row_fanouts(count):
+    fanouts = []
+    while count > 1:
+        fanout = 4 if count % 4 == 0 else 2
+        fanouts.append(fanout)
+        count //= fanout
+    return fanouts
 
 
 def on_device(right_spike, left_spike, loads, tip_inverse):
@@ -41,14 +44,27 @@
     chain_pos = lax.axis_index("chain")
     row_pos = lax.axis_index("rows")
     chain_count = lax.axis_size("chain")
+    row_count = lax.axis_size("rows")
     spike_right = right_spike
     spike_left = left_spike
     load_block = loads
+    inverses = [tip_inverse[0, 0]]
+    for level in range(1, LEVELS):
+        half = 2**level
+        place = chain_pos % (2 * half)
+        lasts = list(range(half - 1, chain_count - 1, 2 * half))
+        mine = tip_inverse[0, level]
+        for k in range(1, half):
+            pairs = [(a, a - k) for a in lasts] + [(a + 1, a + 1 + k) for a in lasts]
+            got = lax.ppermute(mine, "chain", pairs)
+            mine = jnp.where((place == half - 1 - k) | (place == half + k), got, mine)
+        inverses.append(mine)
     top, bottom = spread_tips(
         jnp.concatenate([load_block[:band], spike_right[:band]], 1),
         jnp.concatenate([load_block[-band:], spike_left[-band:]], 1),
         row_pos,
-        lax.axis_size("rows"),
+        row_count,
+        row_fanouts(row_count),
     )
     blank_block = jnp.zeros((band, band), jnp.float32)
     for level in range(LEVELS):
@@ -56,17 +72,18 @@
         place = chain_pos % (2 * half)
         side_low = place < half
         lasts = list(range(half - 1, chain_count - 1, 2 * half))
-        next_top = lax.ppermute(top, "chain", [(a + 1, a) for a in lasts])
-        prev_bottom = lax.ppermute(bottom, "chain", [(a, a + 1) for a in lasts])
-        lower_tip = jnp.where(side_low, bottom, prev_bottom)
-        upper_tip = jnp.where(side_low, next_top, top)
+        lower_tip = bottom
+        upper_tip = top
+        sent = jnp.where(place == half - 1, bottom, top)
+        for offset in list(range(-(half - 1), 0)) + list(range(1, half + 1)):
+            pairs = [(a, a + offset) for a in lasts] + [(a + 1, a + 1 - offset) for a in lasts]
+            got = lax.ppermute(sent, "chain", pairs)
+            lower_tip = jnp.where(place == half - 1 + offset, got, lower_tip)
+            upper_tip = jnp.where(place == half - offset, got, upper_tip)
         upper_rows = jnp.concatenate([lower_tip[:, :band], lower_tip[:, band:], blank_block], 1)
         lower_rows = jnp.concatenate([upper_tip[:, :band], blank_block, upper_tip[:, band:]], 1)
         tip_rhs = jnp.concatenate([upper_rows, lower_rows], 0)
-        solved = jnp.dot(
-            tip_inverse[0, level], tip_rhs, precision=precise, preferred_element_type=jnp.float32
-        )
-        solved = spread_block(solved, level, chain_pos, side_low)
+        solved = jnp.dot(inverses[level], tip_rhs, precision=precise, preferred_element_type=jnp.float32)
         if level + 1 < LEVELS:
             bottom_prod = jnp.dot(
                 bottom[:, band:], solved[:, : 2 * band], precision=precise, preferred_element_type=jnp.float32

time: 177 us -> 169 us (0.955)
  the two profiles are of different devices: /device:TPU:12 before, /device:TPU:72 now
where the time goes in v2:
time: 169 us; the launch traced here: 168 us
  waiting for transfers between devices  90.2 us (53%)
  matrix products  26.8 us (16%)
  starting transfers between devices  24.3 us (14%)
  other arithmetic  18.1 us (11%)
  local copies, waits for them, and re-layouts  7.41 us (4%)
    ppermute x7, waiting for transfers between devices, spread_tips(): got = lax.ppermute(sent, 'rows', pairs)  63.3 us
    ppermute x11, waiting for transfers between devices, on_device(): got = lax.ppermute(sent, 'chain', pairs)  24.5 us
    dot_general x3, matrix products, on_device(): jnp.dot(driver, solved, precision=precise, preferred_element_type=jnp.flo...  19 us
    ppermute x11, starting transfers between devices, on_device(): got = lax.ppermute(sent, 'chain', pairs)  13.5 us
    sub x1, other arithmetic, on_device(): load_block = load_block - product[:, :width]  7.82 us
    ppermute x7, starting transfers between devices, spread_tips(): got = lax.ppermute(sent, 'rows', pairs)  5.63 us
    dot_general x3, matrix products, on_device(): jnp.dot(inverses[level], tip_rhs, precision=precise, preferred_element_ty...  5.26 us
    ppermute x4, starting transfers between devices, on_device(): got = lax.ppermute(mine, 'chain', pairs)  5.26 us
  transfers between devices with their start and end apart: 22, of which 5 were waited for; matrix products, arithmetic and copies ran while one was open for 13% of the time, Pallas kernels for 0%

profile of v2, /device:TPU:72, one launch (start us, length us, event | category | flops | bytes accessed | tf_op | source)
XLA Modules:
  0.0 168.1 jit_solution(10409456423188688011)
XLA Ops:
  0.6 1.0 slice.130
  1.6 1.0 slice.132
  2.6 1.1 fusion.73
  3.7 0.1 fusion.57
  3.7 0.7 collective-permute-start.2
  4.4 0.7 collective-permute-start.1
  5.1 1.5 collective-permute-start
  6.6 0.8 copy-done.8
  7.4 1.5 broadcast_select_fusion.3
  8.9 0.7 collective-permute-start.5
  9.6 0.7 collective-permute-start.4
  10.3 1.3 collective-permute-start.3
  11.7 0.0 copy-start.9
  11.7 53.7 %collective-permute-done.3 = f32[256,512]{1,0:T(8,128)S(1)} collective-permute-done((f32[256,512]{1,0:T(8,128)S(1)}, f32[256,512]{1,0:T(8,128)S(1)}, u32[]{:S(2)}, u32[]{:S(2)}) %collective-permute-start.3) | collective-permute-done | bytes 524320 | tf_op jit(solution)/shard_map/ppermute | solution.py:22
  65.4 0.8 copy-done.10
  66.2 1.6 broadcast_select_fusion.5
  67.8 0.1 collective-permute-start.6
  68.0 1.0 slice_bitcast_fusion
  69.0 1.5 collective-permute-start.12
  70.4 9.6 %collective-permute-done.6 = f32[256,512]{1,0:T(8,128)S(1)} collective-permute-done((f32[256,512]{1,0:T(8,128)S(1)}, f32[256,512]{1,0:T(8,128)S(1)}, u32[]{:S(2)}, u32[]{:S(2)}) %collective-permute-start.6) | collective-permute-done | bytes 524320 | tf_op jit(solution)/shard_map/ppermute | solution.py:22
  80.0 0.2 broadcast_select_fusion.7
  80.2 0.1 collective-permute-start.7
  80.3 1.3 collective-permute-start.8
  81.7 1.1 broadcast_select_fusion
  82.8 0.0 copy-start.5
  82.8 0.8 collective-permute-start.13
  83.7 0.1 broadcast_select_fusion.6
  83.9 0.3 copy-done.5
  84.2 2.2 %fusion.8 = f32[768,256]{1,0:T(8,128)S(1)} fusion(f32[256,256]{1,0:T(8,128)S(1)} %broadcast_in_dim.3, f32[256,512]{1,0:T(8,128)S(1)} %get-tuple-element.44, f32[256,256]{1,0:T(8,128)S(1)} %get-tuple-element.42, f32[256,256]{1,0:T(8,128)S(1)} %get-tuple-element.41, f32[1,3,256,512]{3,2,1,0:T(8,128)S(1)} %copy-done.5), kind=kOutput, calls=%fused_computation.20 | convolution fusion | flops 1209925632 | bytes 2621440 | tf_op jit(solution)/shard_map/dot_general | solution.py:86
  86.5 0.6 fusion.41
  87.2 0.1 slice_subtract_fusion.6
  87.2 0.6 fusion.43
  87.9 0.0 copy-start.1
  87.9 0.1 slice_subtract_fusion.5
  87.9 0.1 fusion.56
  88.0 1.6 collective-permute-start.11
  89.6 0.7 collective-permute-start.10
  90.3 1.5 collective-permute-start.9
  91.8 0.9 broadcast_select_fusion.1
  92.7 5.8 %fusion.4 = f32[2048,768]{1,0:T(8,128)S(1)} fusion(f32[768,256]{1,0:T(8,128)S(1)} %fusion.8, f32[2048,256]{1,0:T(8,128)S(1)} %copy-done.2, f32[2048,256]{1,0:T(8,128)S(1)} %copy-done.1, pred[]{:T(512)S(6)} %lt.80), kind=kOutput, calls=%fused_computation.16 | convolution fusion | flops 4832362496 | bytes 11272193 | tf_op jit(solution)/shard_map/dot_general | solution.py:100
  98.5 10.2 %collective-permute-done.9 = f32[256,512]{1,0:T(8,128)S(1)} collective-permute-done((f32[256,512]{1,0:T(8,128)S(1)}, f32[256,512]{1,0:T(8,128)S(1)}, u32[]{:S(2)}, u32[]{:S(2)}) %collective-permute-start.9) | collective-permute-done | bytes 524320 | tf_op jit(solution)/shard_map/ppermute | solution.py:80
  108.7 0.3 select_select_fusion.2
  109.1 1.5 fusion.12
  110.6 0.6 fusion.39
  111.3 0.6 fusion.47
  111.9 0.1 slice_subtract_fusion.3
  112.0 0.9 fusion.55
  112.9 1.3 collective-permute-start.21
  114.1 0.7 collective-permute-start.20
  114.8 1.5 collective-permute-start.19
  116.4 1.5 collective-permute-start.18
  117.9 1.5 collective-permute-start.17
  119.3 6.1 %fusion.2 = f32[2048,768]{1,0:T(8,128)S(1)} fusion(f32[256,768]{1,0:T(8,128)S(1)} %fusion.12, pred[]{:T(512)S(6)} %lt.78, f32[2048,256]{1,0:T(8,128)S(1)} %copy-done.2, f32[2048,768]{1,0:T(8,128)S(1)} %fusion.4, pred[]{:T(512)S(6)} %lt.80, f32[2048,256]{1,0:T(8,128)S(1)} %copy-done.1), kind=kOutput, calls=%fused_computation.12 | convolution fusion | flops 4835508224 | bytes 15466498 | tf_op jit(solution)/shard_map/dot_general | solution.py:100
  125.4 1.9 %collective-permute-start.16 = (f32[256,512]{1,0:T(8,128)}, f32[256,512]{1,0:T(8,128)}, u32[]{:S(2)}, u32[]{:S(2)}) collective-permute-start(f32[256,512]{1,0:T(8,128)} %fusion.55), channel_id=1, source_target_pairs={{96,192},{128,32},{97,193},{129,33},{98,194},{130,34},{99,195},{13... | collective-permute-start | bytes 1572872 | tf_op jit(solution)/shard_map/ppermute | solution.py:80
  127.3 1.2 copy-done.7
  128.5 1.3 collective-permute-start.15
  129.8 0.8 negate_select_fusion.1
  130.7 1.7 %collective-permute-start.14 = (f32[256,512]{1,0:T(8,128)}, f32[256,512]{1,0:T(8,128)S(1)}, u32[]{:S(2)}, u32[]{:S(2)}) collective-permute-start(f32[256,512]{1,0:T(8,128)} %broadcast_select_fusion.1), channel_id=1, source_target_pairs={{96,0},{128,224},{97,1},{129,225},{98,2},{130,226},{99,3},{131,227... | collective-permute-start | bytes 1572872 | tf_op jit(solution)/shard_map/ppermute | solution.py:59
  132.4 14.3 %collective-permute-done.15 = f32[256,512]{1,0:T(8,128)} collective-permute-done((f32[256,512]{1,0:T(8,128)}, f32[256,512]{1,0:T(8,128)}, u32[]{:S(2)}, u32[]{:S(2)}) %collective-permute-start.15) | collective-permute-done | bytes 524320 | tf_op jit(solution)/shard_map/ppermute | solution.py:80
  146.7 2.5 %select_select_fusion = (f32[256,512]{1,0:T(8,128)S(1)}, f32[256,512]{1,0:T(8,128)S(1)}) fusion(f32[256,512]{1,0:T(8,128)} %collective-permute-done.15, f32[256,512]{1,0:T(8,128)} %collective-permute-done.16, f32[256,512]{1,0:T(8,128)} %collective-permute-done.17, f32[256,512]{1,0:T(8,128)} %collective-permute-done.18, ...), kind=kLoop, calls=%fused_computation.68 | loop fusion | flops 2097152 | bytes 5767176 | tf_op jit(solution)/shard_map/jit(_where)/select_n | solution.py:82
  149.3 2.3 %collective-permute-done.14 = f32[256,512]{1,0:T(8,128)S(1)} collective-permute-done((f32[256,512]{1,0:T(8,128)}, f32[256,512]{1,0:T(8,128)S(1)}, u32[]{:S(2)}, u32[]{:S(2)}) %collective-permute-start.14) | collective-permute-done | bytes 524320 | tf_op jit(solution)/shard_map/ppermute | solution.py:59
  151.6 1.5 fusion.16
  153.1 7.1 %fusion = f32[2048,768]{1,0:T(8,128)} fusion(f32[256,768]{1,0:T(8,128)S(1)} %fusion.16, f32[2048,256]{1,0:T(8,128)S(1)} %get-tuple-element.13, f32[2048,256]{1,0:T(8,128)S(1)} %get-tuple-element.12, pred[]{:T(512)S(6)} %lt.76), kind=kOutput, calls=%fused_computation.8 | convolution fusion | flops 4832362496 | bytes 11272193 | tf_op jit(solution)/shard_map/dot_general | solution.py:100
  160.3 7.8 %slice_subtract_fusion = (f32[2048,256]{1,0:T(8,128)}, f32[2048,256]{1,0:T(8,128)}, f32[2048,256]{1,0:T(8,128)}) fusion(f32[2048,768]{1,0:T(8,128)} %fusion, f32[2048,768]{1,0:T(8,128)} %copy-done, f32[2048,256]{1,0:T(8,128)} %param.6, f32[2048,768]{1,0:T(8,128)S(1)} %fusion.4, f32[2048,256]{1,0:T(8,128)S(1)} %get-tuple-element.12, pred[]{:T(512)S(6)} %lt.76, ...), kind=kLoop, calls=%fused_computation.3 | loop fusion | flops 4718592 | bytes 23068672 | tf_op jit(solution)/shard_map/sub | solution.py:103
  (40 shorter events, 0.3 us)
Async XLA Ops:
  3.7 2.9 %collective-permute-start.2 = (f32[256,512]{1,0:T(8,128)S(1)}, f32[256,512]{1,0:T(8,128)S(1)}, u32[]{:S(2)}, u32[]{:S(2)}) collective-permute-start(f32[256,512]{1,0:T(8,128)S(1)} %fusion.57), channel_id=1, source_target_pairs={{0,8},{31,23},{32,40},{63,55},{64,72},{95,87},{96,104},{127,119},{... | collective-permute-start | bytes 1572872 | tf_op jit(solution)/shard_map/ppermute | solution.py:22
  4.4 2.2 %collective-permute-start.1 = (f32[256,512]{1,0:T(8,128)S(1)}, f32[256,512]{1,0:T(8,128)S(1)}, u32[]{:S(2)}, u32[]{:S(2)}) collective-permute-start(f32[256,512]{1,0:T(8,128)S(1)} %fusion.57), channel_id=1, source_target_pairs={{0,16},{31,15},{32,48},{63,47},{64,80},{95,79},{96,112},{127,111},... | collective-permute-start | bytes 1572872 | tf_op jit(solution)/shard_map/ppermute | solution.py:22
  5.1 2.3 %collective-permute-start = (f32[256,512]{1,0:T(8,128)S(1)}, f32[256,512]{1,0:T(8,128)}, u32[]{:S(2)}, u32[]{:S(2)}) collective-permute-start(f32[256,512]{1,0:T(8,128)S(1)} %fusion.57), channel_id=1, source_target_pairs={{0,24},{31,7},{32,56},{63,39},{64,88},{95,71},{96,120},{127,103},{... | collective-permute-start | bytes 1572872 | tf_op jit(solution)/shard_map/ppermute | solution.py:22
  6.6 0.8 copy-start.8
  8.9 2.7 %collective-permute-start.5 = (f32[256,512]{1,0:T(8,128)S(1)}, f32[256,512]{1,0:T(8,128)S(1)}, u32[]{:S(2)}, u32[]{:S(2)}) collective-permute-start(f32[256,512]{1,0:T(8,128)S(1)} %get-tuple-element.9), channel_id=1, source_target_pairs={{0,2},{8,10},{16,18},{24,26},{7,5},{15,13},{23,21},{31,29},{32,34}... | collective-permute-start | bytes 1572872 | tf_op jit(solution)/shard_map/ppermute | solution.py:22
  9.6 2.0 %collective-permute-start.4 = (f32[256,512]{1,0:T(8,128)S(1)}, f32[256,512]{1,0:T(8,128)S(1)}, u32[]{:S(2)}, u32[]{:S(2)}) collective-permute-start(f32[256,512]{1,0:T(8,128)S(1)} %get-tuple-element.9), channel_id=1, source_target_pairs={{0,4},{8,12},{16,20},{24,28},{7,3},{15,11},{23,19},{31,27},{32,36}... | collective-permute-start | bytes 1572872 | tf_op jit(solution)/shard_map/ppermute | solution.py:22
  10.3 55.1 %collective-permute-start.3 = (f32[256,512]{1,0:T(8,128)S(1)}, f32[256,512]{1,0:T(8,128)S(1)}, u32[]{:S(2)}, u32[]{:S(2)}) collective-permute-start(f32[256,512]{1,0:T(8,128)S(1)} %get-tuple-element.9), channel_id=1, source_target_pairs={{0,6},{8,14},{16,22},{24,30},{7,1},{15,9},{23,17},{31,25},{32,38},... | collective-permute-start | bytes 1572872 | tf_op jit(solution)/shard_map/ppermute | solution.py:22
  11.7 53.7 %copy-start.9 = (f32[256,512]{1,0:T(8,128)}, f32[256,512]{1,0:T(8,128)S(1)}, u32[]{:S(2)}) copy-start(f32[256,512]{1,0:T(8,128)S(1)} %collective-permute-done.4) | copy-start | bytes 1572868
  65.4 0.8 copy-start.10
  66.2 1.7 %copy-start.4 = (f32[1,3,256,512]{3,2,1,0:T(8,128)S(1)}, f32[1,3,256,512]{3,2,1,0:T(8,128)}, u32[]{:S(2)}) copy-start(f32[1,3,256,512]{3,2,1,0:T(8,128)} %param.7) | copy-start | bytes 4718596
  67.8 12.2 %collective-permute-start.6 = (f32[256,512]{1,0:T(8,128)S(1)}, f32[256,512]{1,0:T(8,128)S(1)}, u32[]{:S(2)}, u32[]{:S(2)}) collective-permute-start(f32[256,512]{1,0:T(8,128)S(1)} %get-tuple-element.6), channel_id=1, source_target_pairs={{0,1},{2,3},{4,5},{6,7},{8,9},{10,11},{12,13},{14,15},{16,17},{18,... | collective-permute-start | bytes 1572872 | tf_op jit(solution)/shard_map/ppermute | solution.py:22
  69.0 12.7 %collective-permute-start.12 = (f32[256,512]{1,0:T(8,128)}, f32[256,512]{1,0:T(8,128)}, u32[]{:S(2)}, u32[]{:S(2)}) collective-permute-start(f32[256,512]{1,0:T(8,128)} %get-tuple-element.21), channel_id=1, source_target_pairs={{96,64},{128,160},{97,65},{129,161},{98,66},{130,162},{99,67},{131... | collective-permute-start | bytes 1572872 | tf_op jit(solution)/shard_map/ppermute | solution.py:59
  80.2 3.5 %collective-permute-start.7 = (f32[256,512]{1,0:T(8,128)S(1)}, f32[256,512]{1,0:T(8,128)S(1)}, u32[]{:S(2)}, u32[]{:S(2)}) collective-permute-start(f32[256,512]{1,0:T(8,128)S(1)} %get-tuple-element.3), channel_id=1, source_target_pairs={{0,32},{64,96},{128,160},{192,224},{32,0},{96,64},{160,128},{224,1... | collective-permute-start | bytes 1572872 | tf_op jit(solution)/shard_map/ppermute | solution.py:80
  80.3 28.7 %collective-permute-start.8 = (f32[256,512]{1,0:T(8,128)}, f32[256,512]{1,0:T(8,128)S(1)}, u32[]{:S(2)}, u32[]{:S(2)}) collective-permute-start(f32[256,512]{1,0:T(8,128)} %get-tuple-element.22), channel_id=1, source_target_pairs={{32,0},{160,128},{64,96},{192,224},{33,1},{161,129},{65,97},{193,2... | collective-permute-start | bytes 1572872 | tf_op jit(solution)/shard_map/ppermute | solution.py:59
  82.8 1.4 copy-start.5
  82.8 8.9 %collective-permute-start.13 = (f32[256,512]{1,0:T(8,128)S(1)}, f32[256,512]{1,0:T(8,128)S(1)}, u32[]{:S(2)}, u32[]{:S(2)}) collective-permute-start(f32[256,512]{1,0:T(8,128)S(1)} %broadcast_select_fusion), channel_id=1, source_target_pairs={{96,32},{128,192},{97,33},{129,193},{98,34},{130,194},{99,35},{131... | collective-permute-start | bytes 1572872 | tf_op jit(solution)/shard_map/ppermute | solution.py:59
  87.9 4.8 %copy-start.1 = (f32[2048,256]{1,0:T(8,128)S(1)}, f32[2048,256]{1,0:T(8,128)}, u32[]{:S(2)}) copy-start(f32[2048,256]{1,0:T(8,128)} %param.5) | copy-start | bytes 6291460
  87.9 4.8 %copy-start.2 = (f32[2048,256]{1,0:T(8,128)S(1)}, f32[2048,256]{1,0:T(8,128)}, u32[]{:S(2)}) copy-start(f32[2048,256]{1,0:T(8,128)} %param.4) | copy-start | bytes 6291460
  88.0 10.5 %collective-permute-start.11 = (f32[256,512]{1,0:T(8,128)S(1)}, f32[256,512]{1,0:T(8,128)S(1)}, u32[]{:S(2)}, u32[]{:S(2)}) collective-permute-start(f32[256,512]{1,0:T(8,128)S(1)} %fusion.56), channel_id=1, source_target_pairs={{32,0},{160,128},{64,96},{192,224},{33,1},{161,129},{65,97},{193,2... | collective-permute-start | bytes 1572872 | tf_op jit(solution)/shard_map/ppermute | solution.py:80
  89.6 8.9 %collective-permute-start.10 = (f32[256,512]{1,0:T(8,128)S(1)}, f32[256,512]{1,0:T(8,128)S(1)}, u32[]{:S(2)}, u32[]{:S(2)}) collective-permute-start(f32[256,512]{1,0:T(8,128)S(1)} %fusion.56), channel_id=1, source_target_pairs={{32,64},{160,192},{64,32},{192,160},{33,65},{161,193},{65,33},{193... | collective-permute-start | bytes 1572872 | tf_op jit(solution)/shard_map/ppermute | solution.py:80
  90.3 18.4 %collective-permute-start.9 = (f32[256,512]{1,0:T(8,128)S(1)}, f32[256,512]{1,0:T(8,128)S(1)}, u32[]{:S(2)}, u32[]{:S(2)}) collective-permute-start(f32[256,512]{1,0:T(8,128)S(1)} %fusion.56), channel_id=1, source_target_pairs={{32,96},{160,224},{64,0},{192,128},{33,97},{161,225},{65,1},{193,1... | collective-permute-start | bytes 1572872 | tf_op jit(solution)/shard_map/ppermute | solution.py:80
  112.9 12.5 %collective-permute-start.21 = (f32[256,512]{1,0:T(8,128)}, f32[256,512]{1,0:T(8,128)S(1)}, u32[]{:S(2)}, u32[]{:S(2)}) collective-permute-start(f32[256,512]{1,0:T(8,128)} %fusion.55), channel_id=1, source_target_pairs={{96,0},{128,224},{97,1},{129,225},{98,2},{130,226},{99,3},{131,227... | collective-permute-start | bytes 1572872 | tf_op jit(solution)/shard_map/ppermute | solution.py:80
  114.1 13.2 %collective-permute-start.20 = (f32[256,512]{1,0:T(8,128)}, f32[256,512]{1,0:T(8,128)S(1)}, u32[]{:S(2)}, u32[]{:S(2)}) collective-permute-start(f32[256,512]{1,0:T(8,128)} %fusion.55), channel_id=1, source_target_pairs={{96,32},{128,192},{97,33},{129,193},{98,34},{130,194},{99,35},{131... | collective-permute-start | bytes 1572872 | tf_op jit(solution)/shard_map/ppermute | solution.py:80
  114.8 15.8 %collective-permute-start.19 = (f32[256,512]{1,0:T(8,128)}, f32[256,512]{1,0:T(8,128)}, u32[]{:S(2)}, u32[]{:S(2)}) collective-permute-start(f32[256,512]{1,0:T(8,128)} %fusion.55), channel_id=1, source_target_pairs={{96,64},{128,160},{97,65},{129,161},{98,66},{130,162},{99,67},{131... | collective-permute-start | bytes 1572872 | tf_op jit(solution)/shard_map/ppermute | solution.py:80
  116.4 16.0 %collective-permute-start.18 = (f32[256,512]{1,0:T(8,128)}, f32[256,512]{1,0:T(8,128)}, u32[]{:S(2)}, u32[]{:S(2)}) collective-permute-start(f32[256,512]{1,0:T(8,128)} %fusion.55), channel_id=1, source_target_pairs={{96,128},{128,96},{97,129},{129,97},{98,130},{130,98},{99,131},{13... | collective-permute-start | bytes 1572872 | tf_op jit(solution)/shard_map/ppermute | solution.py:80
  117.9 14.6 %collective-permute-start.17 = (f32[256,512]{1,0:T(8,128)}, f32[256,512]{1,0:T(8,128)}, u32[]{:S(2)}, u32[]{:S(2)}) collective-permute-start(f32[256,512]{1,0:T(8,128)} %fusion.55), channel_id=1, source_target_pairs={{96,160},{128,64},{97,161},{129,65},{98,162},{130,66},{99,163},{13... | collective-permute-start | bytes 1572872 | tf_op jit(solution)/shard_map/ppermute | solution.py:80
  125.4 5.3 %copy-start = (f32[2048,768]{1,0:T(8,128)}, f32[2048,768]{1,0:T(8,128)S(1)}, u32[]{:S(2)}) copy-start(f32[2048,768]{1,0:T(8,128)S(1)} %fusion.2) | copy-start | bytes 18874372
  125.4 1.9 %copy-start.6 = (f32[256,512]{1,0:T(8,128)}, f32[256,512]{1,0:T(8,128)S(1)}, u32[]{:S(2)}) copy-start(f32[256,512]{1,0:T(8,128)S(1)} %collective-permute-done.21) | copy-start | bytes 1572868
  125.4 7.0 %collective-permute-start.16 = (f32[256,512]{1,0:T(8,128)}, f32[256,512]{1,0:T(8,128)}, u32[]{:S(2)}, u32[]{:S(2)}) collective-permute-start(f32[256,512]{1,0:T(8,128)} %fusion.55), channel_id=1, source_target_pairs={{96,192},{128,32},{97,193},{129,33},{98,194},{130,34},{99,195},{13... | collective-permute-start | bytes 1572872 | tf_op jit(solution)/shard_map/ppermute | solution.py:80
  127.3 1.2 copy-start.7
  128.5 18.2 %collective-permute-start.15 = (f32[256,512]{1,0:T(8,128)}, f32[256,512]{1,0:T(8,128)}, u32[]{:S(2)}, u32[]{:S(2)}) collective-permute-start(f32[256,512]{1,0:T(8,128)} %fusion.55), channel_id=1, source_target_pairs={{96,224},{128,0},{97,225},{129,1},{98,226},{130,2},{99,227},{131,3... | collective-permute-start | bytes 1572872 | tf_op jit(solution)/shard_map/ppermute | solution.py:80
  130.7 22.4 %copy-start.3 = (f32[2048,256]{1,0:T(8,128)}, f32[2048,256]{1,0:T(8,128)S(1)}, u32[]{:S(2)}) copy-start(f32[2048,256]{1,0:T(8,128)S(1)} %get-tuple-element.13) | copy-start | bytes 6291460
  130.7 20.9 %copy-start.11 = (f32[256,512]{1,0:T(8,128)S(1)}, f32[256,512]{1,0:T(8,128)}, u32[]{:S(2)}) copy-start(f32[256,512]{1,0:T(8,128)} %broadcast_select_fusion.1) | copy-start | bytes 1572868
  130.7 20.9 %collective-permute-start.14 = (f32[256,512]{1,0:T(8,128)}, f32[256,512]{1,0:T(8,128)S(1)}, u32[]{:S(2)}, u32[]{:S(2)}) collective-permute-start(f32[256,512]{1,0:T(8,128)} %broadcast_select_fusion.1), channel_id=1, source_target_pairs={{96,0},{128,224},{97,1},{129,225},{98,2},{130,226},{99,3},{131,227... | collective-permute-start | bytes 1572872 | tf_op jit(solution)/shard_map/ppermute | solution.py:59

commit v3 on v2

--- a/solution.py
+++ b/solution.py
@@ -1,4 +1,5 @@
 import jax
+import numpy as np
 import jax.numpy as jnp
 from jax import lax
 from jax.sharding import PartitionSpec as P
@@ -37,8 +38,57 @@
     return fanouts
 
 
+CORE_PLANS = (
+    (((2, 0), (4, 0), (6, 0)), ((0, 1), (0, 2), (0, 3)), ((1, 0),)),
+    (((0, 1), (0, 2), (0, 3)), ((2, 0), (4, 0), (6, 0)), ((7, 0),)),
+)
+
+
+def core_tree(top, bottom, chain_pos, row_pos, chain_count, z_count, y_count):
+    row_count = z_count * y_count
+
+    def moved(r, off, sign):
+        z, y = divmod(r, y_count)
+        return ((z + sign * off[0]) % z_count) * y_count + (y + sign * off[1]) % y_count
+
+    holders = [({0}, {row_count - 1}) for _ in CORE_PLANS]
+    for step in range(len(CORE_PLANS[0])):
+        got_top = top
+        got_bottom = bottom
+        new_holders = [(set(t), set(b)) for t, b in holders]
+        for slot in range(len(CORE_PLANS[0][step])):
+            pairs = []
+            sends_top = np.zeros((len(CORE_PLANS), row_count), bool)
+            takes_top = np.zeros((len(CORE_PLANS), row_count), bool)
+            takes_bottom = np.zeros((len(CORE_PLANS), row_count), bool)
+            for kind, plan in enumerate(CORE_PLANS):
+                off = plan[step][slot]
+                tops, bottoms = holders[kind]
+                for s in tops:
+                    sends_top[kind, s] = True
+                    d = moved(s, off, 1)
+                    takes_top[kind, d] = True
+                    new_holders[kind][0].add(d)
+                for s in bottoms:
+                    d = moved(s, off, -1)
+                    takes_bottom[kind, d] = True
+                    new_holders[kind][1].add(d)
+                for c in range(kind, chain_count, len(CORE_PLANS)):
+                    pairs += [(c * row_count + s, c * row_count + moved(s, off, 1)) for s in tops]
+                    pairs += [(c * row_count + s, c * row_count + moved(s, off, -1)) for s in bottoms]
+            kind_pos = chain_pos % len(CORE_PLANS)
+            sent = jnp.where(jnp.asarray(sends_top)[kind_pos, row_pos], top, bottom)
+            got = lax.ppermute(sent, ("chain", "rows"), pairs)
+            got_top = jnp.where(jnp.asarray(takes_top)[kind_pos, row_pos], got, got_top)
+            got_bottom = jnp.where(jnp.asarray(takes_bottom)[kind_pos, row_pos], got, got_bottom)
+        holders = new_holders
+        top = got_top
+        bottom = got_bottom
+    return top, bottom
+
+
 def on_device(right_spike, left_spike, loads, tip_inverse):
-    precise = lax.Precision.HIGHEST
+    precise = lax.Precision.HIGH
     band = HALF_BAND
     width = LOAD_COLS
     chain_pos = lax.axis_index("chain")
@@ -59,13 +109,12 @@
             got = lax.ppermute(mine, "chain", pairs)
             mine = jnp.where((place == half - 1 - k) | (place == half + k), got, mine)
         inverses.append(mine)
-    top, bottom = spread_tips(
-        jnp.concatenate([load_block[:band], spike_right[:band]], 1),
-        jnp.concatenate([load_block[-band:], spike_left[-band:]], 1),
-        row_pos,
-        row_count,
-        row_fanouts(row_count),
-    )
+    first_tip = jnp.concatenate([load_block[:band], spike_right[:band]], 1)
+    last_tip = jnp.concatenate([load_block[-band:], spike_left[-band:]], 1)
+    if row_count == 32 and chain_count % 2 == 0:
+        top, bottom = core_tree(first_tip, last_tip, chain_pos, row_pos, chain_count, 8, 4)
+    else:
+        top, bottom = spread_tips(first_tip, last_tip, row_pos, row_count, row_fanouts(row_count))
     blank_block = jnp.zeros((band, band), jnp.float32)
     for level in range(LEVELS):
         half = 2**level

time: 169 us -> 145 us (0.86)
  the two profiles are of different devices: /device:TPU:72 before, /device:TPU:96 now
where the time goes in v3:
time: 145 us; the launch traced here: 144 us
  waiting for transfers between devices  58.2 us (40%)
  other arithmetic  26.3 us (18%)
  starting transfers between devices  26.3 us (18%)
  matrix products  16.5 us (11%)
  local copies, waits for them, and re-layouts  15.1 us (10%)
    ppermute x11, waiting for transfers between devices, on_device(): got = lax.ppermute(sent, 'chain', pairs)  28.6 us
    ppermute x7, waiting for transfers between devices, core_tree(): got = lax.ppermute(sent, ('chain', 'rows'), pairs)  27.5 us
    ppermute x11, starting transfers between devices, on_device(): got = lax.ppermute(sent, 'chain', pairs)  16.5 us
    dot_general x3, matrix products, on_device(): jnp.dot(driver, solved, precision=precise, preferred_element_type=jnp.flo...  10.8 us
    select_n x3, other arithmetic, core_tree(): sent = jnp.where(jnp.asarray(sends_top)[kind_pos, row_pos], top, bottom)  10.1 us
    sub x1, other arithmetic, on_device(): load_block = load_block - product[:, :width]  7.82 us
    ppermute x4, starting transfers between devices, on_device(): got = lax.ppermute(mine, 'chain', pairs)  5 us
    ppermute x7, starting transfers between devices, core_tree(): got = lax.ppermute(sent, ('chain', 'rows'), pairs)  4.86 us
  transfers between devices with their start and end apart: 22, of which 6 were waited for; matrix products, arithmetic and copies ran while one was open for 18% of the time, Pallas kernels for 0%

profile of v3, /device:TPU:96, one launch (start us, length us, event | category | flops | bytes accessed | tf_op | source)
XLA Modules:
  0.0 143.7 jit_solution(9117348315847274684)
XLA Ops:
  0.7 1.0 slice.130
  1.7 1.0 slice.132
  2.7 1.1 fusion.73
  3.8 0.6 dynamic_slice.68
  4.4 0.7 fusion.57
  5.1 0.7 collective-permute-start.2
  5.8 0.7 collective-permute-start.1
  6.5 0.7 collective-permute-start
  7.2 0.6 dynamic_slice.66
  7.8 0.6 dynamic_slice.73
  8.4 0.6 dynamic_slice.67
  9.0 0.6 dynamic_slice.74
  9.5 0.6 dynamic_slice.69
  10.2 0.6 dynamic_slice.75
  10.8 0.6 dynamic_slice.71
  11.5 4.6 %broadcast_select_fusion.3 = (f32[256,512]{1,0:T(8,128)S(1)}, f32[256,512]{1,0:T(8,128)S(1)}, f32[256,512]{1,0:T(8,128)S(1)}) fusion(pred[]{:T(512)} %bitcast.2, f32[256,512]{1,0:T(8,128)S(1)} %collective-permute-done, f32[256,512]{1,0:T(8,128)S(1)} %collective-permute-done.1, f32[256,512]{1,0:T(8,128)S(1)} %collective-permute-done.2, ...), kind=kLoop, calls=%fused_computation.99 | loop fusion | flops 1179648 | bytes 4194311 | tf_op jit(solution)/shard_map/jit(_where)/select_n | solution.py:80
  16.1 0.7 collective-permute-start.5
  16.8 0.7 collective-permute-start.4
  17.5 1.3 collective-permute-start.3
  18.9 0.6 dynamic_slice.63
  19.4 0.6 dynamic_slice.80
  20.0 0.6 dynamic_slice.65
  20.6 0.6 dynamic_slice.81
  21.2 0.6 dynamic_slice.76
  21.8 0.6 dynamic_slice.82
  22.4 0.6 dynamic_slice.78
  23.0 21.5 %collective-permute-done.3 = f32[256,512]{1,0:T(8,128)S(1)} collective-permute-done((f32[256,512]{1,0:T(8,128)S(1)}, f32[256,512]{1,0:T(8,128)S(1)}, u32[]{:S(2)}, u32[]{:S(2)}) %collective-permute-start.3) | collective-permute-done | bytes 524320 | tf_op jit(solution)/shard_map/ppermute | solution.py:81
  44.6 4.7 %broadcast_select_fusion.4 = (f32[256,512]{1,0:T(8,128)S(1)}, f32[256,512]{1,0:T(8,128)S(1)}, f32[256,512]{1,0:T(8,128)S(1)}) fusion(pred[]{:T(512)} %bitcast, f32[256,512]{1,0:T(8,128)S(1)} %collective-permute-done.3, f32[256,512]{1,0:T(8,128)S(1)} %collective-permute-done.4, f32[256,512]{1,0:T(8,128)S(1)} %collective-permute-done.5, ...), kind=kLoop, calls=%fused_computation.100 | loop fusion | flops 917504 | bytes 4194311 | tf_op jit(solution)/shard_map/jit(_where)/select_n | solution.py:80
  49.4 1.0 slice_bitcast_fusion
  50.5 1.5 %collective-permute-start.12 = (f32[256,512]{1,0:T(8,128)}, f32[256,512]{1,0:T(8,128)}, u32[]{:S(2)}, u32[]{:S(2)}) collective-permute-start(f32[256,512]{1,0:T(8,128)} %get-tuple-element.21), channel_id=1, source_target_pairs={{96,64},{128,160},{97,65},{129,161},{98,66},{130,162},{99,67},{131... | collective-permute-start | bytes 1572872 | tf_op jit(solution)/shard_map/ppermute | solution.py:109
  51.9 0.7 dynamic_slice.83
  52.6 6.0 %collective-permute-done.6 = f32[256,512]{1,0:T(8,128)S(1)} collective-permute-done((f32[256,512]{1,0:T(8,128)S(1)}, f32[256,512]{1,0:T(8,128)S(1)}, u32[]{:S(2)}, u32[]{:S(2)}) %collective-permute-start.6) | collective-permute-done | bytes 524320 | tf_op jit(solution)/shard_map/ppermute | solution.py:81
  58.6 1.5 %broadcast_select_fusion.7 = (f32[256,512]{1,0:T(8,128)S(1)}, f32[256,512]{1,0:T(8,128)S(1)}, f32[256,512]{1,0:T(8,128)S(1)}) fusion(pred[]{:T(512)S(6)} %eq.75, f32[256,512]{1,0:T(8,128)S(1)} %collective-permute-done.6, f32[256,512]{1,0:T(8,128)S(1)} %get-tuple-element.8, pred[]{:T(512)} %bitcast.15, f32[256,512]{1,0:T(8,128)S(1)} %get-tuple-element.7, ...), kind=kLoop, calls=%fused_computation.103 | loop fusion | flops 393216 | bytes 3145731 | tf_op jit(solution)/shard_map/jit(_where)/select_n | solution.py:126
  60.1 2.9 %collective-permute-start.7 = (f32[256,512]{1,0:T(8,128)S(1)}, f32[256,512]{1,0:T(8,128)S(1)}, u32[]{:S(2)}, u32[]{:S(2)}) collective-permute-start(f32[256,512]{1,0:T(8,128)S(1)} %get-tuple-element.3), channel_id=1, source_target_pairs={{0,32},{64,96},{128,160},{192,224},{32,0},{96,64},{160,128},{224,1... | collective-permute-start | bytes 1572872 | tf_op jit(solution)/shard_map/ppermute | solution.py:129
  63.0 1.3 collective-permute-start.8
  64.3 1.1 broadcast_select_fusion
  65.5 0.8 collective-permute-start.13
  66.9 1.2 fusion.8
  69.2 1.6 %collective-permute-start.11 = (f32[256,512]{1,0:T(8,128)S(1)}, f32[256,512]{1,0:T(8,128)S(1)}, u32[]{:S(2)}, u32[]{:S(2)}) collective-permute-start(f32[256,512]{1,0:T(8,128)S(1)} %fusion.56), channel_id=1, source_target_pairs={{32,0},{160,128},{64,96},{192,224},{33,1},{161,129},{65,97},{193,2... | collective-permute-start | bytes 1572872 | tf_op jit(solution)/shard_map/ppermute | solution.py:129
  70.8 0.7 collective-permute-start.10
  71.5 1.3 collective-permute-start.9
  72.8 0.9 broadcast_select_fusion.1
  73.7 2.9 %fusion.4 = f32[2048,768]{1,0:T(8,128)S(1)} fusion(f32[768,256]{1,0:T(8,128)S(1)} %fusion.8, f32[2048,256]{1,0:T(8,128)S(1)} %copy-done.2, f32[2048,256]{1,0:T(8,128)S(1)} %copy-done.1, pred[]{:T(512)S(6)} %lt.47), kind=kOutput, calls=%fused_computation.16 | convolution fusion | flops 2416443392 | bytes 11272193 | tf_op jit(solution)/shard_map/dot_general | solution.py:149
  76.6 14.0 %collective-permute-done.9 = f32[256,512]{1,0:T(8,128)S(1)} collective-permute-done((f32[256,512]{1,0:T(8,128)S(1)}, f32[256,512]{1,0:T(8,128)S(1)}, u32[]{:S(2)}, u32[]{:S(2)}) %collective-permute-start.9) | collective-permute-done | bytes 524320 | tf_op jit(solution)/shard_map/ppermute | solution.py:129
  90.9 2.0 %fusion.12 = f32[256,768]{1,0:T(8,128)S(1)} fusion(f32[256,256]{1,0:T(8,128)S(1)} %broadcast_in_dim.3, f32[256,512]{1,0:T(8,128)S(1)} %get-tuple-element.24, f32[256,256]{1,0:T(8,128)S(1)} %get-tuple-element.36, f32[256,256]{1,0:T(8,128)S(1)} %get-tuple-element.35, f32[256,512]{1,0:T(8,128)} %collective-permute-done.8, pred[]{:T(512)S(6)} %or.12, ...), kind=kOutput, calls=%fused_computation.23 | convolution fusion | flops 606076928 | bytes 3145729 | tf_op jit(solution)/shard_map/dot_general | solution.py:135
  93.9 0.9 fusion.55
  94.7 1.3 collective-permute-start.21
  96.0 0.7 collective-permute-start.20
  96.7 1.7 %collective-permute-start.19 = (f32[256,512]{1,0:T(8,128)}, f32[256,512]{1,0:T(8,128)}, u32[]{:S(2)}, u32[]{:S(2)}) collective-permute-start(f32[256,512]{1,0:T(8,128)} %fusion.55), channel_id=1, source_target_pairs={{96,64},{128,160},{97,65},{129,161},{98,66},{130,162},{99,67},{131... | collective-permute-start | bytes 1572872 | tf_op jit(solution)/shard_map/ppermute | solution.py:129
  98.4 1.5 %collective-permute-start.18 = (f32[256,512]{1,0:T(8,128)}, f32[256,512]{1,0:T(8,128)}, u32[]{:S(2)}, u32[]{:S(2)}) collective-permute-start(f32[256,512]{1,0:T(8,128)} %fusion.55), channel_id=1, source_target_pairs={{96,128},{128,96},{97,129},{129,97},{98,130},{130,98},{99,131},{13... | collective-permute-start | bytes 1572872 | tf_op jit(solution)/shard_map/ppermute | solution.py:129
  99.9 1.5 %collective-permute-start.17 = (f32[256,512]{1,0:T(8,128)}, f32[256,512]{1,0:T(8,128)}, u32[]{:S(2)}, u32[]{:S(2)}) collective-permute-start(f32[256,512]{1,0:T(8,128)} %fusion.55), channel_id=1, source_target_pairs={{96,160},{128,64},{97,161},{129,65},{98,162},{130,66},{99,163},{13... | collective-permute-start | bytes 1572872 | tf_op jit(solution)/shard_map/ppermute | solution.py:129
  101.4 3.2 %fusion.2 = f32[2048,768]{1,0:T(8,128)S(1)} fusion(f32[256,768]{1,0:T(8,128)S(1)} %fusion.12, pred[]{:T(512)S(6)} %lt.45, f32[2048,256]{1,0:T(8,128)S(1)} %copy-done.2, f32[2048,768]{1,0:T(8,128)S(1)} %fusion.4, pred[]{:T(512)S(6)} %lt.47, f32[2048,256]{1,0:T(8,128)S(1)} %copy-done.1), kind=kOutput, calls=%fused_computation.12 | convolution fusion | flops 2419589120 | bytes 15466498 | tf_op jit(solution)/shard_map/dot_general | solution.py:149
  104.6 0.8 collective-permute-done.21
  105.4 2.1 %collective-permute-start.16 = (f32[256,512]{1,0:T(8,128)}, f32[256,512]{1,0:T(8,128)}, u32[]{:S(2)}, u32[]{:S(2)}) collective-permute-start(f32[256,512]{1,0:T(8,128)} %fusion.55), channel_id=1, source_target_pairs={{96,192},{128,32},{97,193},{129,33},{98,194},{130,34},{99,195},{13... | collective-permute-start | bytes 1572872 | tf_op jit(solution)/shard_map/ppermute | solution.py:129
  107.5 0.8 copy-done.7
  108.3 1.3 collective-permute-start.15
  109.6 0.8 negate_select_fusion.1
  110.5 1.4 collective-permute-start.14
  111.9 13.8 %collective-permute-done.15 = f32[256,512]{1,0:T(8,128)} collective-permute-done((f32[256,512]{1,0:T(8,128)}, f32[256,512]{1,0:T(8,128)}, u32[]{:S(2)}, u32[]{:S(2)}) %collective-permute-start.15) | collective-permute-done | bytes 524320 | tf_op jit(solution)/shard_map/ppermute | solution.py:129
  125.7 2.5 %select_select_fusion = (f32[256,512]{1,0:T(8,128)S(1)}, f32[256,512]{1,0:T(8,128)S(1)}) fusion(f32[256,512]{1,0:T(8,128)} %collective-permute-done.15, f32[256,512]{1,0:T(8,128)} %collective-permute-done.16, f32[256,512]{1,0:T(8,128)} %collective-permute-done.17, f32[256,512]{1,0:T(8,128)} %collective-permute-done.18, ...), kind=kLoop, calls=%fused_computation.68 | loop fusion | flops 2097152 | bytes 5767176 | tf_op jit(solution)/shard_map/jit(_where)/select_n | solution.py:131
  128.3 2.0 %collective-permute-done.14 = f32[256,512]{1,0:T(8,128)S(1)} collective-permute-done((f32[256,512]{1,0:T(8,128)}, f32[256,512]{1,0:T(8,128)S(1)}, u32[]{:S(2)}, u32[]{:S(2)}) %collective-permute-start.14) | collective-permute-done | bytes 524320 | tf_op jit(solution)/shard_map/ppermute | solution.py:109
  130.3 0.9 fusion.16
  131.3 4.7 %fusion = f32[2048,768]{1,0:T(8,128)} fusion(f32[256,768]{1,0:T(8,128)S(1)} %fusion.16, f32[2048,256]{1,0:T(8,128)S(1)} %get-tuple-element.13, f32[2048,256]{1,0:T(8,128)S(1)} %get-tuple-element.12, pred[]{:T(512)S(6)} %lt.43), kind=kOutput, calls=%fused_computation.8 | convolution fusion | flops 2416443392 | bytes 11272193 | tf_op jit(solution)/shard_map/dot_general | solution.py:149
  135.9 7.8 %slice_subtract_fusion = (f32[2048,256]{1,0:T(8,128)}, f32[2048,256]{1,0:T(8,128)}, f32[2048,256]{1,0:T(8,128)}) fusion(f32[2048,768]{1,0:T(8,128)} %fusion, f32[2048,768]{1,0:T(8,128)} %copy-done, f32[2048,256]{1,0:T(8,128)} %param.27, f32[2048,768]{1,0:T(8,128)S(1)} %fusion.4, f32[2048,256]{1,0:T(8,128)S(1)} %get-tuple-element.12, pred[]{:T(512)S(6)} %lt.43, ...), kind=kLoop, calls=%fused_computation.3 | loop fusion | flops 4718592 | bytes 23068672 | tf_op jit(solution)/shard_map/sub | solution.py:152
  (82 shorter events, 3.1 us)
Async XLA Ops:
  0.6 3.2 %copy-start.24 = (pred[2,32]{1,0:T(4,128)(4,1)S(1)}, pred[2,32]{1,0:T(4,128)(4,1)}, u32[]{:S(2)}) copy-start(pred[2,32]{1,0:T(4,128)(4,1)} %constant.104.clone) | copy-start | bytes 196
  0.6 6.6 %copy-start.23 = (pred[2,32]{1,0:T(4,128)(4,1)S(1)}, pred[2,32]{1,0:T(4,128)(4,1)}, u32[]{:S(2)}) copy-start(pred[2,32]{1,0:T(4,128)(4,1)} %constant.111.clone) | copy-start | bytes 196
  0.7 7.2 %copy-start.22 = (pred[2,32]{1,0:T(4,128)(4,1)S(1)}, pred[2,32]{1,0:T(4,128)(4,1)}, u32[]{:S(2)}) copy-start(pred[2,32]{1,0:T(4,128)(4,1)} %constant.110.clone) | copy-start | bytes 196
  0.7 7.7 %copy-start.21 = (pred[2,32]{1,0:T(4,128)(4,1)S(1)}, pred[2,32]{1,0:T(4,128)(4,1)}, u32[]{:S(2)}) copy-start(pred[2,32]{1,0:T(4,128)(4,1)} %constant.109.clone) | copy-start | bytes 196
  0.7 8.3 %copy-start.20 = (pred[2,32]{1,0:T(4,128)(4,1)S(1)}, pred[2,32]{1,0:T(4,128)(4,1)}, u32[]{:S(2)}) copy-start(pred[2,32]{1,0:T(4,128)(4,1)} %constant.108.clone) | copy-start | bytes 196
  0.7 8.8 %copy-start.19 = (pred[2,32]{1,0:T(4,128)(4,1)S(1)}, pred[2,32]{1,0:T(4,128)(4,1)}, u32[]{:S(2)}) copy-start(pred[2,32]{1,0:T(4,128)(4,1)} %constant.107.clone) | copy-start | bytes 196
  0.7 9.5 %copy-start.18 = (pred[2,32]{1,0:T(4,128)(4,1)S(1)}, pred[2,32]{1,0:T(4,128)(4,1)}, u32[]{:S(2)}) copy-start(pred[2,32]{1,0:T(4,128)(4,1)} %constant.106.clone) | copy-start | bytes 196
  0.7 10.1 %copy-start.17 = (pred[2,32]{1,0:T(4,128)(4,1)S(1)}, pred[2,32]{1,0:T(4,128)(4,1)}, u32[]{:S(2)}) copy-start(pred[2,32]{1,0:T(4,128)(4,1)} %constant.105.clone) | copy-start | bytes 196
  5.1 6.3 %collective-permute-start.2 = (f32[256,512]{1,0:T(8,128)S(1)}, f32[256,512]{1,0:T(8,128)S(1)}, u32[]{:S(2)}, u32[]{:S(2)}) collective-permute-start(f32[256,512]{1,0:T(8,128)S(1)} %fusion.57), channel_id=1, source_target_pairs={{0,8},{31,23},{64,72},{95,87},{128,136},{159,151},{192,200},{223,2... | collective-permute-start | bytes 1572872 | tf_op jit(solution)/shard_map/ppermute | solution.py:81
  5.8 5.6 %collective-permute-start.1 = (f32[256,512]{1,0:T(8,128)S(1)}, f32[256,512]{1,0:T(8,128)S(1)}, u32[]{:S(2)}, u32[]{:S(2)}) collective-permute-start(f32[256,512]{1,0:T(8,128)S(1)} %fusion.57), channel_id=1, source_target_pairs={{0,16},{31,15},{64,80},{95,79},{128,144},{159,143},{192,208},{223,... | collective-permute-start | bytes 1572872 | tf_op jit(solution)/shard_map/ppermute | solution.py:81
  6.5 4.9 %collective-permute-start = (f32[256,512]{1,0:T(8,128)S(1)}, f32[256,512]{1,0:T(8,128)S(1)}, u32[]{:S(2)}, u32[]{:S(2)}) collective-permute-start(f32[256,512]{1,0:T(8,128)S(1)} %fusion.57), channel_id=1, source_target_pairs={{0,24},{31,7},{64,88},{95,71},{128,152},{159,135},{192,216},{223,1... | collective-permute-start | bytes 1572872 | tf_op jit(solution)/shard_map/ppermute | solution.py:81
  11.4 7.4 %copy-start.16 = (pred[2,32]{1,0:T(4,128)(4,1)S(1)}, pred[2,32]{1,0:T(4,128)(4,1)}, u32[]{:S(2)}) copy-start(pred[2,32]{1,0:T(4,128)(4,1)} %constant.118.clone) | copy-start | bytes 196
  11.4 8.0 %copy-start.15 = (pred[2,32]{1,0:T(4,128)(4,1)S(1)}, pred[2,32]{1,0:T(4,128)(4,1)}, u32[]{:S(2)}) copy-start(pred[2,32]{1,0:T(4,128)(4,1)} %constant.117.clone) | copy-start | bytes 196
  11.4 8.6 %copy-start.14 = (pred[2,32]{1,0:T(4,128)(4,1)S(1)}, pred[2,32]{1,0:T(4,128)(4,1)}, u32[]{:S(2)}) copy-start(pred[2,32]{1,0:T(4,128)(4,1)} %constant.116.clone) | copy-start | bytes 196
  11.4 9.2 %copy-start.13 = (pred[2,32]{1,0:T(4,128)(4,1)S(1)}, pred[2,32]{1,0:T(4,128)(4,1)}, u32[]{:S(2)}) copy-start(pred[2,32]{1,0:T(4,128)(4,1)} %constant.115.clone) | copy-start | bytes 196
  11.5 9.7 %copy-start.12 = (pred[2,32]{1,0:T(4,128)(4,1)S(1)}, pred[2,32]{1,0:T(4,128)(4,1)}, u32[]{:S(2)}) copy-start(pred[2,32]{1,0:T(4,128)(4,1)} %constant.114.clone) | copy-start | bytes 196
  11.5 10.4 %copy-start.11 = (pred[2,32]{1,0:T(4,128)(4,1)S(1)}, pred[2,32]{1,0:T(4,128)(4,1)}, u32[]{:S(2)}) copy-start(pred[2,32]{1,0:T(4,128)(4,1)} %constant.113.clone) | copy-start | bytes 196
  11.5 10.9 %copy-start.10 = (pred[2,32]{1,0:T(4,128)(4,1)S(1)}, pred[2,32]{1,0:T(4,128)(4,1)}, u32[]{:S(2)}) copy-start(pred[2,32]{1,0:T(4,128)(4,1)} %constant.112.clone) | copy-start | bytes 196
  16.1 6.9 %collective-permute-start.5 = (f32[256,512]{1,0:T(8,128)S(1)}, f32[256,512]{1,0:T(8,128)S(1)}, u32[]{:S(2)}, u32[]{:S(2)}) collective-permute-start(f32[256,512]{1,0:T(8,128)S(1)} %get-tuple-element.9), channel_id=1, source_target_pairs={{0,1},{8,9},{16,17},{24,25},{7,6},{23,22},{15,14},{31,30},{64,65},... | collective-permute-start | bytes 1572872 | tf_op jit(solution)/shard_map/ppermute | solution.py:81
  16.8 6.2 %collective-permute-start.4 = (f32[256,512]{1,0:T(8,128)S(1)}, f32[256,512]{1,0:T(8,128)S(1)}, u32[]{:S(2)}, u32[]{:S(2)}) collective-permute-start(f32[256,512]{1,0:T(8,128)S(1)} %get-tuple-element.9), channel_id=1, source_target_pairs={{0,2},{8,10},{16,18},{24,26},{7,5},{23,21},{15,13},{31,29},{64,66}... | collective-permute-start | bytes 1572872 | tf_op jit(solution)/shard_map/ppermute | solution.py:81
  17.5 27.0 %collective-permute-start.3 = (f32[256,512]{1,0:T(8,128)S(1)}, f32[256,512]{1,0:T(8,128)S(1)}, u32[]{:S(2)}, u32[]{:S(2)}) collective-permute-start(f32[256,512]{1,0:T(8,128)S(1)} %get-tuple-element.9), channel_id=1, source_target_pairs={{0,3},{8,11},{16,19},{24,27},{7,4},{23,20},{15,12},{31,28},{64,67}... | collective-permute-start | bytes 1572872 | tf_op jit(solution)/shard_map/ppermute | solution.py:81
  44.6 4.9 %copy-start.4 = (f32[1,3,256,512]{3,2,1,0:T(8,128)S(1)}, f32[1,3,256,512]{3,2,1,0:T(8,128)}, u32[]{:S(2)}) copy-start(f32[1,3,256,512]{3,2,1,0:T(8,128)} %param.28) | copy-start | bytes 4718596
  49.3 2.6 %copy-start.9 = (pred[2,32]{1,0:T(4,128)(4,1)S(1)}, pred[2,32]{1,0:T(4,128)(4,1)}, u32[]{:S(2)}) copy-start(pred[2,32]{1,0:T(4,128)(4,1)} %constant.119.clone) | copy-start | bytes 196
  49.3 9.3 %collective-permute-start.6 = (f32[256,512]{1,0:T(8,128)S(1)}, f32[256,512]{1,0:T(8,128)S(1)}, u32[]{:S(2)}, u32[]{:S(2)}) collective-permute-start(f32[256,512]{1,0:T(8,128)S(1)} %get-tuple-element.6), channel_id=1, source_target_pairs={{0,4},{1,5},{2,6},{3,7},{8,12},{9,13},{10,14},{11,15},{16,20},{17,... | collective-permute-start | bytes 1572872 | tf_op jit(solution)/shard_map/ppermute | solution.py:81
  50.5 13.8 %collective-permute-start.12 = (f32[256,512]{1,0:T(8,128)}, f32[256,512]{1,0:T(8,128)}, u32[]{:S(2)}, u32[]{:S(2)}) collective-permute-start(f32[256,512]{1,0:T(8,128)} %get-tuple-element.21), channel_id=1, source_target_pairs={{96,64},{128,160},{97,65},{129,161},{98,66},{130,162},{99,67},{131... | collective-permute-start | bytes 1572872 | tf_op jit(solution)/shard_map/ppermute | solution.py:109
  60.1 6.2 %collective-permute-start.7 = (f32[256,512]{1,0:T(8,128)S(1)}, f32[256,512]{1,0:T(8,128)S(1)}, u32[]{:S(2)}, u32[]{:S(2)}) collective-permute-start(f32[256,512]{1,0:T(8,128)S(1)} %get-tuple-element.3), channel_id=1, source_target_pairs={{0,32},{64,96},{128,160},{192,224},{32,0},{96,64},{160,128},{224,1... | collective-permute-start | bytes 1572872 | tf_op jit(solution)/shard_map/ppermute | solution.py:129
  63.0 28.0 %collective-permute-start.8 = (f32[256,512]{1,0:T(8,128)}, f32[256,512]{1,0:T(8,128)}, u32[]{:S(2)}, u32[]{:S(2)}) collective-permute-start(f32[256,512]{1,0:T(8,128)} %get-tuple-element.22), channel_id=1, source_target_pairs={{32,0},{160,128},{64,96},{192,224},{33,1},{161,129},{65,97},{193,2... | collective-permute-start | bytes 1572872 | tf_op jit(solution)/shard_map/ppermute | solution.py:109
  65.5 1.4 copy-start.5
  65.5 7.3 %collective-permute-start.13 = (f32[256,512]{1,0:T(8,128)S(1)}, f32[256,512]{1,0:T(8,128)S(1)}, u32[]{:S(2)}, u32[]{:S(2)}) collective-permute-start(f32[256,512]{1,0:T(8,128)S(1)} %broadcast_select_fusion), channel_id=1, source_target_pairs={{96,32},{128,192},{97,33},{129,193},{98,34},{130,194},{99,35},{131... | collective-permute-start | bytes 1572872 | tf_op jit(solution)/shard_map/ppermute | solution.py:109
  69.1 4.6 %copy-start.1 = (f32[2048,256]{1,0:T(8,128)S(1)}, f32[2048,256]{1,0:T(8,128)}, u32[]{:S(2)}) copy-start(f32[2048,256]{1,0:T(8,128)} %param.26) | copy-start | bytes 6291460
  69.1 4.6 %copy-start.2 = (f32[2048,256]{1,0:T(8,128)S(1)}, f32[2048,256]{1,0:T(8,128)}, u32[]{:S(2)}) copy-start(f32[2048,256]{1,0:T(8,128)} %param.25) | copy-start | bytes 6291460
  69.2 7.4 %collective-permute-start.11 = (f32[256,512]{1,0:T(8,128)S(1)}, f32[256,512]{1,0:T(8,128)S(1)}, u32[]{:S(2)}, u32[]{:S(2)}) collective-permute-start(f32[256,512]{1,0:T(8,128)S(1)} %fusion.56), channel_id=1, source_target_pairs={{32,0},{160,128},{64,96},{192,224},{33,1},{161,129},{65,97},{193,2... | collective-permute-start | bytes 1572872 | tf_op jit(solution)/shard_map/ppermute | solution.py:129
  70.8 5.9 %collective-permute-start.10 = (f32[256,512]{1,0:T(8,128)S(1)}, f32[256,512]{1,0:T(8,128)S(1)}, u32[]{:S(2)}, u32[]{:S(2)}) collective-permute-start(f32[256,512]{1,0:T(8,128)S(1)} %fusion.56), channel_id=1, source_target_pairs={{32,64},{160,192},{64,32},{192,160},{33,65},{161,193},{65,33},{193... | collective-permute-start | bytes 1572872 | tf_op jit(solution)/shard_map/ppermute | solution.py:129
  71.5 19.1 %collective-permute-start.9 = (f32[256,512]{1,0:T(8,128)S(1)}, f32[256,512]{1,0:T(8,128)S(1)}, u32[]{:S(2)}, u32[]{:S(2)}) collective-permute-start(f32[256,512]{1,0:T(8,128)S(1)} %fusion.56), channel_id=1, source_target_pairs={{32,96},{160,224},{64,0},{192,128},{33,97},{161,225},{65,1},{193,1... | collective-permute-start | bytes 1572872 | tf_op jit(solution)/shard_map/ppermute | solution.py:129
  94.7 10.7 %collective-permute-start.21 = (f32[256,512]{1,0:T(8,128)}, f32[256,512]{1,0:T(8,128)S(1)}, u32[]{:S(2)}, u32[]{:S(2)}) collective-permute-start(f32[256,512]{1,0:T(8,128)} %fusion.55), channel_id=1, source_target_pairs={{96,0},{128,224},{97,1},{129,225},{98,2},{130,226},{99,3},{131,227... | collective-permute-start | bytes 1572872 | tf_op jit(solution)/shard_map/ppermute | solution.py:129
  96.0 11.5 %collective-permute-start.20 = (f32[256,512]{1,0:T(8,128)}, f32[256,512]{1,0:T(8,128)S(1)}, u32[]{:S(2)}, u32[]{:S(2)}) collective-permute-start(f32[256,512]{1,0:T(8,128)} %fusion.55), channel_id=1, source_target_pairs={{96,32},{128,192},{97,33},{129,193},{98,34},{130,194},{99,35},{131... | collective-permute-start | bytes 1572872 | tf_op jit(solution)/shard_map/ppermute | solution.py:129
  96.7 13.8 %collective-permute-start.19 = (f32[256,512]{1,0:T(8,128)}, f32[256,512]{1,0:T(8,128)}, u32[]{:S(2)}, u32[]{:S(2)}) collective-permute-start(f32[256,512]{1,0:T(8,128)} %fusion.55), channel_id=1, source_target_pairs={{96,64},{128,160},{97,65},{129,161},{98,66},{130,162},{99,67},{131... | collective-permute-start | bytes 1572872 | tf_op jit(solution)/shard_map/ppermute | solution.py:129
  98.4 13.5 %collective-permute-start.18 = (f32[256,512]{1,0:T(8,128)}, f32[256,512]{1,0:T(8,128)}, u32[]{:S(2)}, u32[]{:S(2)}) collective-permute-start(f32[256,512]{1,0:T(8,128)} %fusion.55), channel_id=1, source_target_pairs={{96,128},{128,96},{97,129},{129,97},{98,130},{130,98},{99,131},{13... | collective-permute-start | bytes 1572872 | tf_op jit(solution)/shard_map/ppermute | solution.py:129
  99.9 12.0 %collective-permute-start.17 = (f32[256,512]{1,0:T(8,128)}, f32[256,512]{1,0:T(8,128)}, u32[]{:S(2)}, u32[]{:S(2)}) collective-permute-start(f32[256,512]{1,0:T(8,128)} %fusion.55), channel_id=1, source_target_pairs={{96,160},{128,64},{97,161},{129,65},{98,162},{130,66},{99,163},{13... | collective-permute-start | bytes 1572872 | tf_op jit(solution)/shard_map/ppermute | solution.py:129
  104.6 5.9 %copy-start = (f32[2048,768]{1,0:T(8,128)}, f32[2048,768]{1,0:T(8,128)S(1)}, u32[]{:S(2)}) copy-start(f32[2048,768]{1,0:T(8,128)S(1)} %fusion.2) | copy-start | bytes 18874372
  105.4 2.1 %copy-start.6 = (f32[256,512]{1,0:T(8,128)}, f32[256,512]{1,0:T(8,128)S(1)}, u32[]{:S(2)}) copy-start(f32[256,512]{1,0:T(8,128)S(1)} %collective-permute-done.21) | copy-start | bytes 1572868
  105.4 6.5 %collective-permute-start.16 = (f32[256,512]{1,0:T(8,128)}, f32[256,512]{1,0:T(8,128)}, u32[]{:S(2)}, u32[]{:S(2)}) collective-permute-start(f32[256,512]{1,0:T(8,128)} %fusion.55), channel_id=1, source_target_pairs={{96,192},{128,32},{97,193},{129,33},{98,194},{130,34},{99,195},{13... | collective-permute-start | bytes 1572872 | tf_op jit(solution)/shard_map/ppermute | solution.py:129
  107.5 0.8 copy-start.7
  108.3 17.4 %collective-permute-start.15 = (f32[256,512]{1,0:T(8,128)}, f32[256,512]{1,0:T(8,128)}, u32[]{:S(2)}, u32[]{:S(2)}) collective-permute-start(f32[256,512]{1,0:T(8,128)} %fusion.55), channel_id=1, source_target_pairs={{96,224},{128,0},{97,225},{129,1},{98,226},{130,2},{99,227},{131,3... | collective-permute-start | bytes 1572872 | tf_op jit(solution)/shard_map/ppermute | solution.py:129
  110.4 20.8 %copy-start.3 = (f32[2048,256]{1,0:T(8,128)}, f32[2048,256]{1,0:T(8,128)S(1)}, u32[]{:S(2)}) copy-start(f32[2048,256]{1,0:T(8,128)S(1)} %get-tuple-element.13) | copy-start | bytes 6291460
  110.5 19.9 %copy-start.8 = (f32[256,512]{1,0:T(8,128)S(1)}, f32[256,512]{1,0:T(8,128)}, u32[]{:S(2)}) copy-start(f32[256,512]{1,0:T(8,128)} %broadcast_select_fusion.1) | copy-start | bytes 1572868
  110.5 19.9 %collective-permute-start.14 = (f32[256,512]{1,0:T(8,128)}, f32[256,512]{1,0:T(8,128)S(1)}, u32[]{:S(2)}, u32[]{:S(2)}) collective-permute-start(f32[256,512]{1,0:T(8,128)} %broadcast_select_fusion.1), channel_id=1, source_target_pairs={{96,0},{128,224},{97,1},{129,225},{98,2},{130,226},{99,3},{131,227... | collective-permute-start | bytes 1572872 | tf_op jit(solution)/shard_map/ppermute | solution.py:109

commit v4 on v3

--- a/solution.py
+++ b/solution.py
@@ -46,49 +46,51 @@
 
 def core_tree(top, bottom, chain_pos, row_pos, chain_count, z_count, y_count):
     row_count = z_count * y_count
+    kinds = len(CORE_PLANS)
 
     def moved(r, off, sign):
         z, y = divmod(r, y_count)
         return ((z + sign * off[0]) % z_count) * y_count + (y + sign * off[1]) % y_count
 
+    steps = len(CORE_PLANS[0])
+    table = np.zeros((steps, 3, kinds, row_count), np.int32)
+    all_pairs = []
     holders = [({0}, {row_count - 1}) for _ in CORE_PLANS]
-    for step in range(len(CORE_PLANS[0])):
-        got_top = top
-        got_bottom = bottom
+    for step in range(steps):
         new_holders = [(set(t), set(b)) for t, b in holders]
+        step_pairs = []
         for slot in range(len(CORE_PLANS[0][step])):
             pairs = []
-            sends_top = np.zeros((len(CORE_PLANS), row_count), bool)
-            takes_top = np.zeros((len(CORE_PLANS), row_count), bool)
-            takes_bottom = np.zeros((len(CORE_PLANS), row_count), bool)
             for kind, plan in enumerate(CORE_PLANS):
                 off = plan[step][slot]
                 tops, bottoms = holders[kind]
                 for s in tops:
-                    sends_top[kind, s] = True
+                    table[step, 2, kind, s] = 1
                     d = moved(s, off, 1)
-                    takes_top[kind, d] = True
+                    table[step, 0, kind, d] = slot + 1
                     new_holders[kind][0].add(d)
                 for s in bottoms:
                     d = moved(s, off, -1)
-                    takes_bottom[kind, d] = True
+                    table[step, 1, kind, d] = slot + 1
                     new_holders[kind][1].add(d)
-                for c in range(kind, chain_count, len(CORE_PLANS)):
+                for c in range(kind, chain_count, kinds):
                     pairs += [(c * row_count + s, c * row_count + moved(s, off, 1)) for s in tops]
                     pairs += [(c * row_count + s, c * row_count + moved(s, off, -1)) for s in bottoms]
-            kind_pos = chain_pos % len(CORE_PLANS)
-            sent = jnp.where(jnp.asarray(sends_top)[kind_pos, row_pos], top, bottom)
-            got = lax.ppermute(sent, ("chain", "rows"), pairs)
-            got_top = jnp.where(jnp.asarray(takes_top)[kind_pos, row_pos], got, got_top)
-            got_bottom = jnp.where(jnp.asarray(takes_bottom)[kind_pos, row_pos], got, got_bottom)
+            step_pairs.append(pairs)
+        all_pairs.append(step_pairs)
         holders = new_holders
-        top = got_top
-        bottom = got_bottom
+    mine = jnp.asarray(table.reshape(steps * 3, kinds, row_count))[:, chain_pos % kinds, row_pos]
+    for step in range(steps):
+        sent = jnp.where(mine[3 * step + 2] == 1, top, bottom)
+        got = [lax.ppermute(sent, ("chain", "rows"), pairs) for pairs in all_pairs[step]]
+        top = lax.select_n(mine[3 * step], top, *got)
+        bottom = lax.select_n(mine[3 * step + 1], bottom, *got)
     return top, bottom
 
 
 def on_device(right_spike, left_spike, loads, tip_inverse):
-    precise = lax.Precision.HIGH
+    precise = lax.Precision.HIGHEST
+    fast = lax.Precision.HIGH
     band = HALF_BAND
     width = LOAD_COLS
     chain_pos = lax.axis_index("chain")
@@ -146,7 +148,7 @@
             )
             top = jnp.concatenate([top[:, :band] - top_prod[:, :band], -top_prod[:, band:]], 1)
         driver = jnp.where(side_low, spike_right, spike_left)
-        product = jnp.dot(driver, solved, precision=precise, preferred_element_type=jnp.float32)
+        product = jnp.dot(driver, solved, precision=fast, preferred_element_type=jnp.float32)
         left_term = product[:, width : width + band]
         right_term = product[:, width + band :]
         load_block = load_block - product[:, :width]

time: 145 us -> 148 us (1.021)
  the two profiles are of different devices: /device:TPU:96 before, /device:TPU:72 now
where the time goes in v4:
time: 148 us; the launch traced here: 147 us
  waiting for transfers between devices  69.3 us (47%)
  starting transfers between devices  23.6 us (16%)
  matrix products  19.6 us (13%)
  other arithmetic  15.6 us (11%)
  between operations  11.8 us (8%)
  local copies, waits for them, and re-layouts  7.07 us (5%)
    ppermute x7, waiting for transfers between devices, core_tree(): lax.ppermute(sent, ('chain', 'rows'), pairs)  38.4 us
    ppermute x11, waiting for transfers between devices, on_device(): got = lax.ppermute(sent, 'chain', pairs)  28.6 us
    ppermute x11, starting transfers between devices, on_device(): got = lax.ppermute(sent, 'chain', pairs)  13.5 us
    dot_general x3, matrix products, on_device(): jnp.dot(driver, solved, precision=fast, preferred_element_type=jnp.float32)  10.8 us
    sub x1, other arithmetic, on_device(): load_block = load_block - product[:, :width]  7.82 us
    dot_general x3, matrix products, on_device(): jnp.dot(inverses[level], tip_rhs, precision=precise, preferred_element_ty...  6.32 us
    ppermute x4, starting transfers between devices, on_device(): got = lax.ppermute(mine, 'chain', pairs)  5.22 us
    ppermute x7, starting transfers between devices, core_tree(): lax.ppermute(sent, ('chain', 'rows'), pairs)  4.86 us
  transfers between devices with their start and end apart: 22, of which 6 were waited for; matrix products, arithmetic and copies ran while one was open for 12% of the time, Pallas kernels for 0%

profile of v4, /device:TPU:72, one launch (start us, length us, event | category | flops | bytes accessed | tf_op | source)
XLA Modules:
  0.0 146.9 jit_solution(8885095602392547686)
XLA Ops:
  0.6 0.0 copy-start.9
  0.7 1.0 slice.172
  1.6 1.0 slice.169
  2.6 1.1 fusion.73
  3.7 0.7 fusion.79
  5.1 0.1 fusion.57
  5.1 0.7 collective-permute-start.2
  5.8 0.7 collective-permute-start.1
  6.5 0.7 collective-permute-start
  11.4 0.3 broadcast_select_fusion.4
  11.7 0.7 collective-permute-start.5
  12.4 0.7 collective-permute-start.4
  13.1 1.3 collective-permute-start.3
  18.9 33.9 %collective-permute-done.3 = f32[256,512]{1,0:T(8,128)S(1)} collective-permute-done((f32[256,512]{1,0:T(8,128)S(1)}, f32[256,512]{1,0:T(8,128)S(1)}, u32[]{:S(2)}, u32[]{:S(2)}) %collective-permute-start.3) | collective-permute-done | bytes 524320 | tf_op jit(solution)/shard_map/ppermute | solution.py:85
  52.8 0.3 broadcast_select_fusion.3
  53.2 0.1 collective-permute-start.6
  53.3 1.0 copy-done.4
  54.3 1.0 slice_bitcast_fusion
  55.3 1.5 collective-permute-start.12
  58.0 4.5 %collective-permute-done.6 = f32[256,512]{1,0:T(8,128)S(1)} collective-permute-done((f32[256,512]{1,0:T(8,128)S(1)}, f32[256,512]{1,0:T(8,128)S(1)}, u32[]{:S(2)}, u32[]{:S(2)}) %collective-permute-start.6) | collective-permute-done | bytes 524320 | tf_op jit(solution)/shard_map/ppermute | solution.py:85
  62.4 0.2 broadcast_select_fusion.7
  62.6 0.1 collective-permute-start.7
  62.7 1.3 collective-permute-start.8
  64.1 1.1 broadcast_select_fusion
  65.3 0.0 copy-start.5
  65.3 0.8 collective-permute-start.13
  66.1 0.1 broadcast_select_fusion.6
  66.3 0.3 copy-done.5
  66.7 2.3 %fusion.8 = f32[768,256]{1,0:T(8,128)S(1)} fusion(f32[256,256]{1,0:T(8,128)S(1)} %broadcast_in_dim.3, f32[256,512]{1,0:T(8,128)S(1)} %get-tuple-element.44, f32[256,256]{1,0:T(8,128)S(1)} %get-tuple-element.42, f32[256,256]{1,0:T(8,128)S(1)} %get-tuple-element.41, f32[1,3,256,512]{3,2,1,0:T(8,128)S(1)} %copy-done.5), kind=kOutput, calls=%fused_computation.20 | convolution fusion | flops 1209925632 | bytes 2621440 | tf_op jit(solution)/shard_map/dot_general | solution.py:137
  68.9 0.6 fusion.41
  69.6 0.1 slice_subtract_fusion.6
  69.7 0.6 fusion.43
  70.3 0.1 slice_subtract_fusion.5
  70.4 0.1 fusion.56
  70.5 1.6 %collective-permute-start.11 = (f32[256,512]{1,0:T(8,128)S(1)}, f32[256,512]{1,0:T(8,128)S(1)}, u32[]{:S(2)}, u32[]{:S(2)}) collective-permute-start(f32[256,512]{1,0:T(8,128)S(1)} %fusion.56), channel_id=1, source_target_pairs={{32,0},{160,128},{64,96},{192,224},{33,1},{161,129},{65,97},{193,2... | collective-permute-start | bytes 1572872 | tf_op jit(solution)/shard_map/ppermute | solution.py:131
  72.0 0.7 collective-permute-start.10
  72.7 1.5 %collective-permute-start.9 = (f32[256,512]{1,0:T(8,128)S(1)}, f32[256,512]{1,0:T(8,128)S(1)}, u32[]{:S(2)}, u32[]{:S(2)}) collective-permute-start(f32[256,512]{1,0:T(8,128)S(1)} %fusion.56), channel_id=1, source_target_pairs={{32,96},{160,224},{64,0},{192,128},{33,97},{161,225},{65,1},{193,1... | collective-permute-start | bytes 1572872 | tf_op jit(solution)/shard_map/ppermute | solution.py:131
  74.2 0.9 broadcast_select_fusion.1
  75.1 2.9 %fusion.4 = f32[2048,768]{1,0:T(8,128)S(1)} fusion(f32[768,256]{1,0:T(8,128)S(1)} %fusion.8, f32[2048,256]{1,0:T(8,128)S(1)} %copy-done.1, f32[2048,256]{1,0:T(8,128)S(1)} %copy-done.2, pred[]{:T(512)S(6)} %lt.40), kind=kOutput, calls=%fused_computation.16 | convolution fusion | flops 2416443392 | bytes 11272193 | tf_op jit(solution)/shard_map/dot_general | solution.py:151
  78.1 13.8 %collective-permute-done.9 = f32[256,512]{1,0:T(8,128)S(1)} collective-permute-done((f32[256,512]{1,0:T(8,128)S(1)}, f32[256,512]{1,0:T(8,128)S(1)}, u32[]{:S(2)}, u32[]{:S(2)}) %collective-permute-start.9) | collective-permute-done | bytes 524320 | tf_op jit(solution)/shard_map/ppermute | solution.py:131
  91.9 0.3 select_select_fusion.2
  92.2 2.6 %fusion.12 = f32[256,768]{1,0:T(8,128)S(1)} fusion(f32[256,256]{1,0:T(8,128)S(1)} %broadcast_in_dim.3, f32[256,512]{1,0:T(8,128)S(1)} %get-tuple-element.24, f32[256,256]{1,0:T(8,128)S(1)} %get-tuple-element.36, f32[256,256]{1,0:T(8,128)S(1)} %get-tuple-element.35, f32[256,512]{1,0:T(8,128)} %collective-permute-done.8, pred[]{:T(512)S(6)} %or.12, ...), kind=kOutput, calls=%fused_computation.23 | convolution fusion | flops 1210056704 | bytes 3145729 | tf_op jit(solution)/shard_map/dot_general | solution.py:137
  94.8 0.6 fusion.39
  95.4 0.6 fusion.47
  96.1 0.1 slice_subtract_fusion.3
  96.2 0.9 fusion.55
  97.0 1.3 collective-permute-start.21
  98.3 0.7 collective-permute-start.20
  99.0 1.5 %collective-permute-start.19 = (f32[256,512]{1,0:T(8,128)}, f32[256,512]{1,0:T(8,128)}, u32[]{:S(2)}, u32[]{:S(2)}) collective-permute-start(f32[256,512]{1,0:T(8,128)} %fusion.55), channel_id=1, source_target_pairs={{96,64},{128,160},{97,65},{129,161},{98,66},{130,162},{99,67},{131... | collective-permute-start | bytes 1572872 | tf_op jit(solution)/shard_map/ppermute | solution.py:131
  100.5 1.5 %collective-permute-start.18 = (f32[256,512]{1,0:T(8,128)}, f32[256,512]{1,0:T(8,128)}, u32[]{:S(2)}, u32[]{:S(2)}) collective-permute-start(f32[256,512]{1,0:T(8,128)} %fusion.55), channel_id=1, source_target_pairs={{96,128},{128,96},{97,129},{129,97},{98,130},{130,98},{99,131},{13... | collective-permute-start | bytes 1572872 | tf_op jit(solution)/shard_map/ppermute | solution.py:131
  102.0 1.5 collective-permute-start.17
  103.5 3.2 %fusion.2 = f32[2048,768]{1,0:T(8,128)S(1)} fusion(f32[256,768]{1,0:T(8,128)S(1)} %fusion.12, pred[]{:T(512)S(6)} %lt.38, f32[2048,256]{1,0:T(8,128)S(1)} %copy-done.1, f32[2048,768]{1,0:T(8,128)S(1)} %fusion.4, pred[]{:T(512)S(6)} %lt.40, f32[2048,256]{1,0:T(8,128)S(1)} %copy-done.2), kind=kOutput, calls=%fused_computation.12 | convolution fusion | flops 2419589120 | bytes 15466498 | tf_op jit(solution)/shard_map/dot_general | solution.py:151
  106.7 1.1 collective-permute-done.21
  107.7 1.9 %collective-permute-start.16 = (f32[256,512]{1,0:T(8,128)}, f32[256,512]{1,0:T(8,128)}, u32[]{:S(2)}, u32[]{:S(2)}) collective-permute-start(f32[256,512]{1,0:T(8,128)} %fusion.55), channel_id=1, source_target_pairs={{96,192},{128,32},{97,193},{129,33},{98,194},{130,34},{99,195},{13... | collective-permute-start | bytes 1572872 | tf_op jit(solution)/shard_map/ppermute | solution.py:131
  109.7 0.8 copy-done.7
  110.5 1.3 collective-permute-start.15
  111.8 0.8 negate_select_fusion.1
  112.6 1.6 %collective-permute-start.14 = (f32[256,512]{1,0:T(8,128)}, f32[256,512]{1,0:T(8,128)S(1)}, u32[]{:S(2)}, u32[]{:S(2)}) collective-permute-start(f32[256,512]{1,0:T(8,128)} %broadcast_select_fusion.1), channel_id=1, source_target_pairs={{96,0},{128,224},{97,1},{129,225},{98,2},{130,226},{99,3},{131,227... | collective-permute-start | bytes 1572872 | tf_op jit(solution)/shard_map/ppermute | solution.py:111
  114.3 13.7 %collective-permute-done.15 = f32[256,512]{1,0:T(8,128)} collective-permute-done((f32[256,512]{1,0:T(8,128)}, f32[256,512]{1,0:T(8,128)}, u32[]{:S(2)}, u32[]{:S(2)}) %collective-permute-start.15) | collective-permute-done | bytes 524320 | tf_op jit(solution)/shard_map/ppermute | solution.py:131
  128.0 2.5 %select_select_fusion = (f32[256,512]{1,0:T(8,128)S(1)}, f32[256,512]{1,0:T(8,128)S(1)}) fusion(f32[256,512]{1,0:T(8,128)} %collective-permute-done.15, f32[256,512]{1,0:T(8,128)} %collective-permute-done.16, f32[256,512]{1,0:T(8,128)} %collective-permute-done.17, f32[256,512]{1,0:T(8,128)} %collective-permute-done.18, ...), kind=kLoop, calls=%fused_computation.68 | loop fusion | flops 2097152 | bytes 5767176 | tf_op jit(solution)/shard_map/jit(_where)/select_n | solution.py:133
  130.6 2.3 %collective-permute-done.14 = f32[256,512]{1,0:T(8,128)S(1)} collective-permute-done((f32[256,512]{1,0:T(8,128)}, f32[256,512]{1,0:T(8,128)S(1)}, u32[]{:S(2)}, u32[]{:S(2)}) %collective-permute-start.14) | collective-permute-done | bytes 524320 | tf_op jit(solution)/shard_map/ppermute | solution.py:111
  132.9 1.5 %fusion.16 = f32[256,768]{1,0:T(8,128)S(1)} fusion(f32[256,256]{1,0:T(8,128)S(1)} %broadcast_in_dim.3, f32[256,512]{1,0:T(8,128)S(1)} %get-tuple-element.18, f32[256,256]{1,0:T(8,128)S(1)} %get-tuple-element.30, f32[256,256]{1,0:T(8,128)S(1)} %get-tuple-element.29, f32[256,512]{1,0:T(8,128)S(1)} %collective-permute-done.14, f32[256,512]{1,0:T(8,128)S(1)} %copy-done.8, ...), kind=kOutput, calls=%fused_computation.26 | convolution fusion | flops 1210056704 | bytes 3145729 | tf_op jit(solution)/shard_map/dot_general | solution.py:137
  134.4 4.7 %fusion = f32[2048,768]{1,0:T(8,128)} fusion(f32[256,768]{1,0:T(8,128)S(1)} %fusion.16, f32[2048,256]{1,0:T(8,128)S(1)} %get-tuple-element.13, f32[2048,256]{1,0:T(8,128)S(1)} %get-tuple-element.12, pred[]{:T(512)S(6)} %lt.36), kind=kOutput, calls=%fused_computation.8 | convolution fusion | flops 2416443392 | bytes 11272193 | tf_op jit(solution)/shard_map/dot_general | solution.py:151
  139.1 7.8 %slice_subtract_fusion = (f32[2048,256]{1,0:T(8,128)}, f32[2048,256]{1,0:T(8,128)}, f32[2048,256]{1,0:T(8,128)}) fusion(f32[2048,768]{1,0:T(8,128)} %fusion, f32[2048,768]{1,0:T(8,128)} %copy-done, f32[2048,256]{1,0:T(8,128)} %param.7, f32[2048,768]{1,0:T(8,128)S(1)} %fusion.4, f32[2048,256]{1,0:T(8,128)S(1)} %get-tuple-element.12, pred[]{:T(512)S(6)} %lt.36, ...), kind=kLoop, calls=%fused_computation.3 | loop fusion | flops 4718592 | bytes 23068672 | tf_op jit(solution)/shard_map/sub | solution.py:154
  (37 shorter events, 0.3 us)
Async XLA Ops:
  0.6 3.1 %copy-start.9 = (s32[9,2,32]{2,1,0:T(2,128)S(1)}, s32[9,2,32]{2,1,0:T(2,128)}, u32[]{:S(2)}) copy-start(s32[9,2,32]{2,1,0:T(2,128)} %constant.82.clone) | copy-start | bytes 6916
  5.1 6.3 %collective-permute-start.2 = (f32[256,512]{1,0:T(8,128)S(1)}, f32[256,512]{1,0:T(8,128)S(1)}, u32[]{:S(2)}, u32[]{:S(2)}) collective-permute-start(f32[256,512]{1,0:T(8,128)S(1)} %fusion.57), channel_id=1, source_target_pairs={{0,24},{31,7},{64,88},{95,71},{128,152},{159,135},{192,216},{223,1... | collective-permute-start | bytes 1572872 | tf_op jit(solution)/shard_map/ppermute | solution.py:85
  5.8 5.6 %collective-permute-start.1 = (f32[256,512]{1,0:T(8,128)S(1)}, f32[256,512]{1,0:T(8,128)S(1)}, u32[]{:S(2)}, u32[]{:S(2)}) collective-permute-start(f32[256,512]{1,0:T(8,128)S(1)} %fusion.57), channel_id=1, source_target_pairs={{0,16},{31,15},{64,80},{95,79},{128,144},{159,143},{192,208},{223,... | collective-permute-start | bytes 1572872 | tf_op jit(solution)/shard_map/ppermute | solution.py:85
  6.5 4.9 %collective-permute-start = (f32[256,512]{1,0:T(8,128)S(1)}, f32[256,512]{1,0:T(8,128)S(1)}, u32[]{:S(2)}, u32[]{:S(2)}) collective-permute-start(f32[256,512]{1,0:T(8,128)S(1)} %fusion.57), channel_id=1, source_target_pairs={{0,8},{31,23},{64,72},{95,87},{128,136},{159,151},{192,200},{223,2... | collective-permute-start | bytes 1572872 | tf_op jit(solution)/shard_map/ppermute | solution.py:85
  11.7 7.2 %collective-permute-start.5 = (f32[256,512]{1,0:T(8,128)S(1)}, f32[256,512]{1,0:T(8,128)S(1)}, u32[]{:S(2)}, u32[]{:S(2)}) collective-permute-start(f32[256,512]{1,0:T(8,128)S(1)} %get-tuple-element.9), channel_id=1, source_target_pairs={{0,3},{8,11},{16,19},{24,27},{7,4},{23,20},{15,12},{31,28},{64,67}... | collective-permute-start | bytes 1572872 | tf_op jit(solution)/shard_map/ppermute | solution.py:85
  12.4 6.5 %collective-permute-start.4 = (f32[256,512]{1,0:T(8,128)S(1)}, f32[256,512]{1,0:T(8,128)S(1)}, u32[]{:S(2)}, u32[]{:S(2)}) collective-permute-start(f32[256,512]{1,0:T(8,128)S(1)} %get-tuple-element.9), channel_id=1, source_target_pairs={{0,2},{8,10},{16,18},{24,26},{7,5},{23,21},{15,13},{31,29},{64,66}... | collective-permute-start | bytes 1572872 | tf_op jit(solution)/shard_map/ppermute | solution.py:85
  13.1 39.7 %collective-permute-start.3 = (f32[256,512]{1,0:T(8,128)S(1)}, f32[256,512]{1,0:T(8,128)S(1)}, u32[]{:S(2)}, u32[]{:S(2)}) collective-permute-start(f32[256,512]{1,0:T(8,128)S(1)} %get-tuple-element.9), channel_id=1, source_target_pairs={{0,1},{8,9},{16,17},{24,25},{7,6},{23,22},{15,14},{31,30},{64,65},... | collective-permute-start | bytes 1572872 | tf_op jit(solution)/shard_map/ppermute | solution.py:85
  52.8 1.4 copy-start.4
  53.2 9.3 %collective-permute-start.6 = (f32[256,512]{1,0:T(8,128)S(1)}, f32[256,512]{1,0:T(8,128)S(1)}, u32[]{:S(2)}, u32[]{:S(2)}) collective-permute-start(f32[256,512]{1,0:T(8,128)S(1)} %get-tuple-element.6), channel_id=1, source_target_pairs={{0,4},{1,5},{2,6},{3,7},{8,12},{9,13},{10,14},{11,15},{16,20},{17,... | collective-permute-start | bytes 1572872 | tf_op jit(solution)/shard_map/ppermute | solution.py:85
  55.3 8.8 %collective-permute-start.12 = (f32[256,512]{1,0:T(8,128)}, f32[256,512]{1,0:T(8,128)}, u32[]{:S(2)}, u32[]{:S(2)}) collective-permute-start(f32[256,512]{1,0:T(8,128)} %get-tuple-element.21), channel_id=1, source_target_pairs={{96,64},{128,160},{97,65},{129,161},{98,66},{130,162},{99,67},{131... | collective-permute-start | bytes 1572872 | tf_op jit(solution)/shard_map/ppermute | solution.py:111
  62.6 3.5 %collective-permute-start.7 = (f32[256,512]{1,0:T(8,128)S(1)}, f32[256,512]{1,0:T(8,128)S(1)}, u32[]{:S(2)}, u32[]{:S(2)}) collective-permute-start(f32[256,512]{1,0:T(8,128)S(1)} %get-tuple-element.3), channel_id=1, source_target_pairs={{0,32},{64,96},{128,160},{192,224},{32,0},{96,64},{160,128},{224,1... | collective-permute-start | bytes 1572872 | tf_op jit(solution)/shard_map/ppermute | solution.py:131
  62.7 29.5 %collective-permute-start.8 = (f32[256,512]{1,0:T(8,128)}, f32[256,512]{1,0:T(8,128)}, u32[]{:S(2)}, u32[]{:S(2)}) collective-permute-start(f32[256,512]{1,0:T(8,128)} %get-tuple-element.22), channel_id=1, source_target_pairs={{32,0},{160,128},{64,96},{192,224},{33,1},{161,129},{65,97},{193,2... | collective-permute-start | bytes 1572872 | tf_op jit(solution)/shard_map/ppermute | solution.py:111
  65.3 1.4 copy-start.5
  65.3 8.9 %collective-permute-start.13 = (f32[256,512]{1,0:T(8,128)S(1)}, f32[256,512]{1,0:T(8,128)S(1)}, u32[]{:S(2)}, u32[]{:S(2)}) collective-permute-start(f32[256,512]{1,0:T(8,128)S(1)} %broadcast_select_fusion), channel_id=1, source_target_pairs={{96,32},{128,192},{97,33},{129,193},{98,34},{130,194},{99,35},{131... | collective-permute-start | bytes 1572872 | tf_op jit(solution)/shard_map/ppermute | solution.py:111
  70.3 4.8 %copy-start.1 = (f32[2048,256]{1,0:T(8,128)S(1)}, f32[2048,256]{1,0:T(8,128)}, u32[]{:S(2)}) copy-start(f32[2048,256]{1,0:T(8,128)} %param.5) | copy-start | bytes 6291460
  70.3 4.8 %copy-start.2 = (f32[2048,256]{1,0:T(8,128)S(1)}, f32[2048,256]{1,0:T(8,128)}, u32[]{:S(2)}) copy-start(f32[2048,256]{1,0:T(8,128)} %param.6) | copy-start | bytes 6291460
  70.5 7.6 %collective-permute-start.11 = (f32[256,512]{1,0:T(8,128)S(1)}, f32[256,512]{1,0:T(8,128)S(1)}, u32[]{:S(2)}, u32[]{:S(2)}) collective-permute-start(f32[256,512]{1,0:T(8,128)S(1)} %fusion.56), channel_id=1, source_target_pairs={{32,0},{160,128},{64,96},{192,224},{33,1},{161,129},{65,97},{193,2... | collective-permute-start | bytes 1572872 | tf_op jit(solution)/shard_map/ppermute | solution.py:131
  72.0 6.0 %collective-permute-start.10 = (f32[256,512]{1,0:T(8,128)S(1)}, f32[256,512]{1,0:T(8,128)S(1)}, u32[]{:S(2)}, u32[]{:S(2)}) collective-permute-start(f32[256,512]{1,0:T(8,128)S(1)} %fusion.56), channel_id=1, source_target_pairs={{32,64},{160,192},{64,32},{192,160},{33,65},{161,193},{65,33},{193... | collective-permute-start | bytes 1572872 | tf_op jit(solution)/shard_map/ppermute | solution.py:131
  72.7 19.2 %collective-permute-start.9 = (f32[256,512]{1,0:T(8,128)S(1)}, f32[256,512]{1,0:T(8,128)S(1)}, u32[]{:S(2)}, u32[]{:S(2)}) collective-permute-start(f32[256,512]{1,0:T(8,128)S(1)} %fusion.56), channel_id=1, source_target_pairs={{32,96},{160,224},{64,0},{192,128},{33,97},{161,225},{65,1},{193,1... | collective-permute-start | bytes 1572872 | tf_op jit(solution)/shard_map/ppermute | solution.py:131
  97.0 10.7 %collective-permute-start.21 = (f32[256,512]{1,0:T(8,128)}, f32[256,512]{1,0:T(8,128)S(1)}, u32[]{:S(2)}, u32[]{:S(2)}) collective-permute-start(f32[256,512]{1,0:T(8,128)} %fusion.55), channel_id=1, source_target_pairs={{96,0},{128,224},{97,1},{129,225},{98,2},{130,226},{99,3},{131,227... | collective-permute-start | bytes 1572872 | tf_op jit(solution)/shard_map/ppermute | solution.py:131
  98.3 11.4 %collective-permute-start.20 = (f32[256,512]{1,0:T(8,128)}, f32[256,512]{1,0:T(8,128)S(1)}, u32[]{:S(2)}, u32[]{:S(2)}) collective-permute-start(f32[256,512]{1,0:T(8,128)} %fusion.55), channel_id=1, source_target_pairs={{96,32},{128,192},{97,33},{129,193},{98,34},{130,194},{99,35},{131... | collective-permute-start | bytes 1572872 | tf_op jit(solution)/shard_map/ppermute | solution.py:131
  99.0 13.6 %collective-permute-start.19 = (f32[256,512]{1,0:T(8,128)}, f32[256,512]{1,0:T(8,128)}, u32[]{:S(2)}, u32[]{:S(2)}) collective-permute-start(f32[256,512]{1,0:T(8,128)} %fusion.55), channel_id=1, source_target_pairs={{96,64},{128,160},{97,65},{129,161},{98,66},{130,162},{99,67},{131... | collective-permute-start | bytes 1572872 | tf_op jit(solution)/shard_map/ppermute | solution.py:131
  100.5 13.8 %collective-permute-start.18 = (f32[256,512]{1,0:T(8,128)}, f32[256,512]{1,0:T(8,128)}, u32[]{:S(2)}, u32[]{:S(2)}) collective-permute-start(f32[256,512]{1,0:T(8,128)} %fusion.55), channel_id=1, source_target_pairs={{96,128},{128,96},{97,129},{129,97},{98,130},{130,98},{99,131},{13... | collective-permute-start | bytes 1572872 | tf_op jit(solution)/shard_map/ppermute | solution.py:131
  102.0 12.3 %collective-permute-start.17 = (f32[256,512]{1,0:T(8,128)}, f32[256,512]{1,0:T(8,128)}, u32[]{:S(2)}, u32[]{:S(2)}) collective-permute-start(f32[256,512]{1,0:T(8,128)} %fusion.55), channel_id=1, source_target_pairs={{96,160},{128,64},{97,161},{129,65},{98,162},{130,66},{99,163},{13... | collective-permute-start | bytes 1572872 | tf_op jit(solution)/shard_map/ppermute | solution.py:131
  106.7 5.9 %copy-start = (f32[2048,768]{1,0:T(8,128)}, f32[2048,768]{1,0:T(8,128)S(1)}, u32[]{:S(2)}) copy-start(f32[2048,768]{1,0:T(8,128)S(1)} %fusion.2) | copy-start | bytes 18874372
  107.7 1.9 %copy-start.6 = (f32[256,512]{1,0:T(8,128)}, f32[256,512]{1,0:T(8,128)S(1)}, u32[]{:S(2)}) copy-start(f32[256,512]{1,0:T(8,128)S(1)} %collective-permute-done.21) | copy-start | bytes 1572868
  107.7 6.6 %collective-permute-start.16 = (f32[256,512]{1,0:T(8,128)}, f32[256,512]{1,0:T(8,128)}, u32[]{:S(2)}, u32[]{:S(2)}) collective-permute-start(f32[256,512]{1,0:T(8,128)} %fusion.55), channel_id=1, source_target_pairs={{96,192},{128,32},{97,193},{129,33},{98,194},{130,34},{99,195},{13... | collective-permute-start | bytes 1572872 | tf_op jit(solution)/shard_map/ppermute | solution.py:131
  109.7 0.8 copy-start.7
  110.5 17.5 %collective-permute-start.15 = (f32[256,512]{1,0:T(8,128)}, f32[256,512]{1,0:T(8,128)}, u32[]{:S(2)}, u32[]{:S(2)}) collective-permute-start(f32[256,512]{1,0:T(8,128)} %fusion.55), channel_id=1, source_target_pairs={{96,224},{128,0},{97,225},{129,1},{98,226},{130,2},{99,227},{131,3... | collective-permute-start | bytes 1572872 | tf_op jit(solution)/shard_map/ppermute | solution.py:131
  112.6 21.8 %copy-start.3 = (f32[2048,256]{1,0:T(8,128)}, f32[2048,256]{1,0:T(8,128)S(1)}, u32[]{:S(2)}) copy-start(f32[2048,256]{1,0:T(8,128)S(1)} %get-tuple-element.13) | copy-start | bytes 6291460
  112.6 20.3 %copy-start.8 = (f32[256,512]{1,0:T(8,128)S(1)}, f32[256,512]{1,0:T(8,128)}, u32[]{:S(2)}) copy-start(f32[256,512]{1,0:T(8,128)} %broadcast_select_fusion.1) | copy-start | bytes 1572868
  112.6 20.2 %collective-permute-start.14 = (f32[256,512]{1,0:T(8,128)}, f32[256,512]{1,0:T(8,128)S(1)}, u32[]{:S(2)}, u32[]{:S(2)}) collective-permute-start(f32[256,512]{1,0:T(8,128)} %broadcast_select_fusion.1), channel_id=1, source_target_pairs={{96,0},{128,224},{97,1},{129,225},{98,2},{130,226},{99,3},{131,227... | collective-permute-start | bytes 1572872 | tf_op jit(solution)/shard_map/ppermute | solution.py:111

commit v5 on v4

--- a/solution.py
+++ b/solution.py
@@ -2,6 +2,8 @@
 import numpy as np
 import jax.numpy as jnp
 from jax import lax
+from jax.experimental import pallas as pl
+from jax.experimental.pallas import tpu as pltpu
 from jax.sharding import PartitionSpec as P
 
 HALF_BAND = 256
@@ -36,6 +38,34 @@
         fanouts.append(fanout)
         count //= fanout
     return fanouts
+
+
+def bulk_kernel(flag_ref, x_ref, v_ref, w_ref, g_ref, vo_ref, wo_ref, go_ref):
+    low = flag_ref[0] == 1
+    v = v_ref[...]
+    w = w_ref[...]
+    prod = jnp.dot(jnp.where(low, v, w), x_ref[...], precision=lax.Precision.HIGHEST,
+                   preferred_element_type=jnp.float32)
+    go_ref[...] = g_ref[...] - prod[:, :LOAD_COLS]
+    left_term = prod[:, LOAD_COLS:LOAD_COLS + HALF_BAND]
+    right_term = prod[:, LOAD_COLS + HALF_BAND:]
+    wo_ref[...] = jnp.where(low, w - left_term, -left_term)
+    vo_ref[...] = jnp.where(low, -right_term, v - right_term)
+
+def bulk_update(flag, x, v, w, g, tile=512):
+    rows = v.shape[0]
+    block = pl.BlockSpec((tile, HALF_BAND), lambda i, f: (i, 0))
+    out = jax.ShapeDtypeStruct((rows, HALF_BAND), jnp.float32)
+    return pl.pallas_call(
+        bulk_kernel,
+        grid_spec=pltpu.PrefetchScalarGridSpec(
+            num_scalar_prefetch=1,
+            grid=(rows // tile,),
+            in_specs=[pl.BlockSpec(x.shape, lambda i, f: (0, 0)), block, block, block],
+            out_specs=[block, block, block],
+        ),
+        out_shape=[out, out, out],
+    )(flag, x, v, w, g)
 
 
 CORE_PLANS = (
@@ -90,7 +120,6 @@
 
 def on_device(right_spike, left_spike, loads, tip_inverse):
     precise = lax.Precision.HIGHEST
-    fast = lax.Precision.HIGH
     band = HALF_BAND
     width = LOAD_COLS
     chain_pos = lax.axis_index("chain")
@@ -147,15 +176,8 @@
                 preferred_element_type=jnp.float32,
             )
             top = jnp.concatenate([top[:, :band] - top_prod[:, :band], -top_prod[:, band:]], 1)
-        driver = jnp.where(side_low, spike_right, spike_left)
-        product = jnp.dot(driver, solved, precision=fast, preferred_element_type=jnp.float32)
-        left_term = product[:, width : width + band]
-        right_term = product[:, width + band :]
-        load_block = load_block - product[:, :width]
-        new_left = jnp.where(side_low, spike_left - left_term, -left_term)
-        new_right = jnp.where(side_low, -right_term, spike_right - right_term)
-        spike_left = new_left
-        spike_right = new_right
+        flag = jnp.where(side_low, 1, 0).astype(jnp.int32).reshape(1)
+        spike_right, spike_left, load_block = bulk_update(flag, solved, spike_right, spike_left, load_block)
     return (spike_right, spike_left, load_block)
 
 

time: 148 us -> 160 us (1.081)
  Pallas kernels: 0 us -> 28 us
  matrix products: 19.6 us -> 10.2 us
  other arithmetic: 15.6 us -> 8.51 us
  waiting for transfers between devices: 69.3 us -> 71.9 us
    pallas_call x0 -> x3, Pallas kernels: none -> 28 us  [bulk_update(): pl.pallas_call(bulk_kernel, grid_spec=pltpu.PrefetchScalarGridSpec(num_sc...]
    dot_general x3 -> x0, matrix products: 10.8 us -> none  [on_device(): jnp.dot(driver, solved, precision=fast, preferred_element_type=jnp.float32)]
    sub x1 -> x0, other arithmetic: 7.82 us -> none  [on_device(): load_block = load_block - product[:, :width]]
    ppermute x11, waiting for transfers between devices: 28.6 us -> 21.1 us  [on_device(): got = lax.ppermute(sent, 'chain', pairs)]
    ppermute x4, waiting for transfers between devices: 2.34 us -> 9.01 us  [on_device(): got = lax.ppermute(mine, 'chain', pairs)]
    ppermute x7, waiting for transfers between devices: 38.4 us -> 41.8 us  [core_tree(): lax.ppermute(sent, ('chain', 'rows'), pairs)]
  transfers between devices with their start and end apart: 22 -> 22, of which waited for: 6 -> 5; matrix products, arithmetic and copies ran while one was open for 12% -> 11% of each run, Pallas kernels for 0% -> 12%
where the time goes in v5:
time: 160 us; the launch traced here: 159 us
  waiting for transfers between devices  71.9 us (45%)
  Pallas kernels  28 us (18%)
  starting transfers between devices  22.4 us (14%)
  between operations  11.8 us (7%)
  matrix products  10.2 us (6%)
  other arithmetic  8.51 us (5%)
  local copies, waits for them, and re-layouts  6.24 us (4%)
    ppermute x7, waiting for transfers between devices, core_tree(): lax.ppermute(sent, ('chain', 'rows'), pairs)  41.8 us
    pallas_call x3, Pallas kernels, bulk_update(): pl.pallas_call(bulk_kernel, grid_spec=pltpu.PrefetchScalarGridSpec(num_sc...  28 us
    ppermute x11, waiting for transfers between devices, on_device(): got = lax.ppermute(sent, 'chain', pairs)  21.1 us
    ppermute x11, starting transfers between devices, on_device(): got = lax.ppermute(sent, 'chain', pairs)  12.7 us
    ppermute x4, waiting for transfers between devices, on_device(): got = lax.ppermute(mine, 'chain', pairs)  9.01 us
    dot_general x3, matrix products, on_device(): jnp.dot(inverses[level], tip_rhs, precision=precise, preferred_element_ty...  7.73 us
    ppermute x4, starting transfers between devices, on_device(): got = lax.ppermute(mine, 'chain', pairs)  4.88 us
    ppermute x7, starting transfers between devices, core_tree(): lax.ppermute(sent, ('chain', 'rows'), pairs)  4.86 us
  transfers between devices with their start and end apart: 22, of which 5 were waited for; matrix products, arithmetic and copies ran while one was open for 11% of the time, Pallas kernels for 12%

profile of v5, /device:TPU:72, one launch (start us, length us, event | category | flops | bytes accessed | tf_op | source)
XLA Modules:
  0.0 159.0 jit_solution(17142038885451594162)
XLA Ops:
  0.6 0.0 copy-start.6
  0.7 1.0 slice.146
  1.6 1.0 slice.143
  2.6 1.1 fusion.67
  3.7 0.7 fusion.73
  5.0 0.1 fusion.51
  5.1 0.7 collective-permute-start.5
  5.8 0.7 collective-permute-start.4
  6.5 0.7 collective-permute-start.3
  11.6 0.0 collective-permute-done.5
  11.6 0.0 collective-permute-done.4
  11.6 0.3 broadcast_select_fusion.5
  11.9 0.7 collective-permute-start.8
  12.7 0.7 collective-permute-start.7
  13.4 1.3 collective-permute-start.6
  18.9 33.9 %collective-permute-done.6 = f32[256,512]{1,0:T(8,128)S(1)} collective-permute-done((f32[256,512]{1,0:T(8,128)S(1)}, f32[256,512]{1,0:T(8,128)S(1)}, u32[]{:S(2)}, u32[]{:S(2)}) %collective-permute-start.6) | collective-permute-done | bytes 524320 | tf_op jit(solution)/shard_map/ppermute | solution.py:115
  52.8 0.3 broadcast_select_fusion.4
  53.1 0.1 collective-permute-start.9
  54.5 7.9 %collective-permute-done.9 = f32[256,512]{1,0:T(8,128)S(1)} collective-permute-done((f32[256,512]{1,0:T(8,128)S(1)}, f32[256,512]{1,0:T(8,128)S(1)}, u32[]{:S(2)}, u32[]{:S(2)}) %collective-permute-start.9) | collective-permute-done | bytes 524320 | tf_op jit(solution)/shard_map/ppermute | solution.py:115
  62.4 0.2 broadcast_select_fusion.2
  62.6 0.1 collective-permute-start.10
  62.7 1.1 copy-done.2
  63.8 1.0 slice_bitcast_fusion.1
  64.8 1.5 collective-permute-start
  66.3 0.0 collective-permute-done.10
  66.3 0.1 broadcast_select_fusion.1
  66.5 2.7 %fusion.24.x_ref = f32[256,768]{1,0:T(8,128)S(1)} fusion(f32[256,256]{1,0:T(8,128)S(1)} %broadcast_in_dim.3, f32[256,512]{1,0:T(8,128)S(1)} %get-tuple-element.51, f32[256,256]{1,0:T(8,128)S(1)} %get-tuple-element.49, f32[256,256]{1,0:T(8,128)S(1)} %get-tuple-element.48, f32[1,3,256,512]{3,2,1,0:T(8,128)} %param.8), kind=kOutput, calls=%fused_computation.25 | convolution fusion | flops 1209925632 | bytes 2621440 | tf_op jit(solution)/shard_map/dot_general | solution.py:166
  69.2 0.6 fusion.35
  69.9 0.1 slice_subtract_fusion.3
  69.9 0.2 copy-done
  70.1 0.6 fusion.37
  70.7 0.1 slice_subtract_fusion.2
  70.8 0.9 fusion.50
  71.7 1.3 collective-permute-start.14
  72.9 1.5 collective-permute-start.13
  74.4 1.3 collective-permute-start.12
  75.7 1.3 collective-permute-start.11
  77.0 0.0 collective-permute-done
  77.1 1.1 broadcast_select_fusion.7
  78.2 0.7 collective-permute-start.1
  78.9 16.0 %collective-permute-done.12 = f32[256,512]{1,0:T(8,128)} collective-permute-done((f32[256,512]{1,0:T(8,128)}, f32[256,512]{1,0:T(8,128)}, u32[]{:S(2)}, u32[]{:S(2)}) %collective-permute-start.12) | collective-permute-done | bytes 524320 | tf_op jit(solution)/shard_map/ppermute | solution.py:160
  94.9 1.4 select_select_fusion.2
  96.4 0.0 collective-permute-done.11
  96.4 2.7 %fusion.6.x_ref = f32[256,768]{1,0:T(8,128)S(1)} fusion(f32[256,256]{1,0:T(8,128)S(1)} %broadcast_in_dim.3, f32[256,512]{1,0:T(8,128)S(1)} %get-tuple-element.31, f32[256,256]{1,0:T(8,128)S(1)} %get-tuple-element.43, f32[256,256]{1,0:T(8,128)S(1)} %get-tuple-element.42, f32[256,512]{1,0:T(8,128)} %collective-permute-done.11, pred[]{:T(512)S(6)} %or.15, ...), kind=kOutput, calls=%fused_computation.8 | convolution fusion | flops 1210056704 | bytes 3145729 | tf_op jit(solution)/shard_map/dot_general | solution.py:166
  99.1 0.6 fusion.33
  99.8 0.6 fusion.41
  100.4 0.1 slice_subtract_fusion
  100.6 0.9 fusion.49
  101.5 1.3 collective-permute-start.21
  102.7 0.7 collective-permute-start.20
  103.4 0.7 collective-permute-start.19
  104.1 1.5 collective-permute-start.18
  105.6 1.5 collective-permute-start.17
  107.1 5.1 %collective-permute-done.21 = f32[256,512]{1,0:T(8,128)S(1)} collective-permute-done((f32[256,512]{1,0:T(8,128)}, f32[256,512]{1,0:T(8,128)S(1)}, u32[]{:S(2)}, u32[]{:S(2)}) %collective-permute-start.21) | collective-permute-done | bytes 524320 | tf_op jit(solution)/shard_map/ppermute | solution.py:160
  112.2 1.5 collective-permute-start.16
  113.7 1.5 collective-permute-start.15
  115.2 0.9 broadcast_select_fusion.8
  116.1 9.3 %shard_map.76 = (f32[2048,256]{1,0:T(8,128)}, f32[2048,256]{1,0:T(8,128)}, f32[2048,256]{1,0:T(8,128)}) custom-call(s32[1]{0:T(128)} %bitcast.23.flag_ref, f32[256,768]{1,0:T(8,128)} %copy-done, f32[2048,256]{1,0:T(8,128)} %v_ref.1, f32[2048,256]{1,0:T(8,128)} %w_ref.1, f32[2048,256]{1,0:T(8,128)} %g_ref.1), custom_call_target="tpu_custom_call" | custom-call | tf_op jit(solution)/shard_map/pallas_call | solution.py:59
  125.4 9.3 %shard_map.77 = (f32[2048,256]{1,0:T(8,128)}, f32[2048,256]{1,0:T(8,128)}, f32[2048,256]{1,0:T(8,128)}) custom-call(s32[1]{0:T(128)} %bitcast.22.flag_ref, f32[256,768]{1,0:T(8,128)} %copy-done.1, f32[2048,256]{1,0:T(8,128)} %get-tuple-element.9.v_ref, f32[2048,256]{1,0:T(8,128)} %get-tuple-element.10.w_ref, f32[2048,256]{1,0:T(8,128)} %get-tuple-element.11.g_ref), custom_call_target="tpu_custom_call" | custom-call | tf_op jit(solution)/shard_map/pallas_call | solution.py:59
  134.8 1.4 collective-permute-start.2
  136.2 2.0 %select_select_fusion = (f32[256,512]{1,0:T(8,128)S(1)}, f32[256,512]{1,0:T(8,128)S(1)}) fusion(f32[256,512]{1,0:T(8,128)} %collective-permute-done.15, f32[256,512]{1,0:T(8,128)} %collective-permute-done.16, f32[256,512]{1,0:T(8,128)} %collective-permute-done.17, f32[256,512]{1,0:T(8,128)} %collective-permute-done.18, ...), kind=kLoop, calls=%fused_computation.51 | loop fusion | flops 2097152 | bytes 5767176 | tf_op jit(solution)/shard_map/jit(_where)/select_n | solution.py:162
  138.3 9.0 %collective-permute-done.2 = f32[256,512]{1,0:T(8,128)S(1)} collective-permute-done((f32[256,512]{1,0:T(8,128)}, f32[256,512]{1,0:T(8,128)S(1)}, u32[]{:S(2)}, u32[]{:S(2)}) %collective-permute-start.2) | collective-permute-done | bytes 524320 | tf_op jit(solution)/shard_map/ppermute | solution.py:140
  147.3 2.4 %fusion.10.x_ref = f32[256,768]{1,0:T(8,128)} fusion(f32[256,256]{1,0:T(8,128)S(1)} %copy-done.5, f32[256,512]{1,0:T(8,128)S(1)} %get-tuple-element.25, f32[256,256]{1,0:T(8,128)S(1)} %get-tuple-element.37, f32[256,256]{1,0:T(8,128)S(1)} %get-tuple-element.36, f32[256,512]{1,0:T(8,128)S(1)} %collective-permute-done.2, ...), kind=kOutput, calls=%fused_computation.11 | convolution fusion | flops 1210056704 | bytes 3145729 | tf_op jit(solution)/shard_map/dot_general | solution.py:166
  149.7 9.3 %shard_map.78 = (f32[2048,256]{1,0:T(8,128)}, f32[2048,256]{1,0:T(8,128)}, f32[2048,256]{1,0:T(8,128)}) custom-call(s32[1]{0:T(128)} %bitcast.flag_ref, f32[256,768]{1,0:T(8,128)} %fusion.10.x_ref, f32[2048,256]{1,0:T(8,128)} %get-tuple-element.12.v_ref, f32[2048,256]{1,0:T(8,128)} %get-tuple-element.13.w_ref, f32[2048,256]{1,0:T(8,128)} %get-tuple-element.14.g_ref), custom_call_target="tpu_custom_call" | custom-call | tf_op jit(solution)/shard_map/pallas_call | solution.py:59
  (29 shorter events, 0.3 us)
Async XLA Ops:
  0.6 3.1 %copy-start.6 = (s32[9,2,32]{2,1,0:T(2,128)S(1)}, s32[9,2,32]{2,1,0:T(2,128)}, u32[]{:S(2)}) copy-start(s32[9,2,32]{2,1,0:T(2,128)} %constant.82.clone) | copy-start | bytes 6916
  5.1 6.5 %collective-permute-start.5 = (f32[256,512]{1,0:T(8,128)S(1)}, f32[256,512]{1,0:T(8,128)S(1)}, u32[]{:S(2)}, u32[]{:S(2)}) collective-permute-start(f32[256,512]{1,0:T(8,128)S(1)} %fusion.51), channel_id=1, source_target_pairs={{0,24},{31,7},{64,88},{95,71},{128,152},{159,135},{192,216},{223,1... | collective-permute-start | bytes 1572872 | tf_op jit(solution)/shard_map/ppermute | solution.py:115
  5.8 5.8 %collective-permute-start.4 = (f32[256,512]{1,0:T(8,128)S(1)}, f32[256,512]{1,0:T(8,128)S(1)}, u32[]{:S(2)}, u32[]{:S(2)}) collective-permute-start(f32[256,512]{1,0:T(8,128)S(1)} %fusion.51), channel_id=1, source_target_pairs={{0,16},{31,15},{64,80},{95,79},{128,144},{159,143},{192,208},{223,... | collective-permute-start | bytes 1572872 | tf_op jit(solution)/shard_map/ppermute | solution.py:115
  6.5 5.1 %collective-permute-start.3 = (f32[256,512]{1,0:T(8,128)S(1)}, f32[256,512]{1,0:T(8,128)S(1)}, u32[]{:S(2)}, u32[]{:S(2)}) collective-permute-start(f32[256,512]{1,0:T(8,128)S(1)} %fusion.51), channel_id=1, source_target_pairs={{0,8},{31,23},{64,72},{95,87},{128,136},{159,151},{192,200},{223,2... | collective-permute-start | bytes 1572872 | tf_op jit(solution)/shard_map/ppermute | solution.py:115
  11.9 6.9 %collective-permute-start.8 = (f32[256,512]{1,0:T(8,128)S(1)}, f32[256,512]{1,0:T(8,128)S(1)}, u32[]{:S(2)}, u32[]{:S(2)}) collective-permute-start(f32[256,512]{1,0:T(8,128)S(1)} %get-tuple-element.21), channel_id=1, source_target_pairs={{0,3},{8,11},{16,19},{24,27},{7,4},{23,20},{15,12},{31,28},{64,67}... | collective-permute-start | bytes 1572872 | tf_op jit(solution)/shard_map/ppermute | solution.py:115
  12.7 6.2 %collective-permute-start.7 = (f32[256,512]{1,0:T(8,128)S(1)}, f32[256,512]{1,0:T(8,128)S(1)}, u32[]{:S(2)}, u32[]{:S(2)}) collective-permute-start(f32[256,512]{1,0:T(8,128)S(1)} %get-tuple-element.21), channel_id=1, source_target_pairs={{0,2},{8,10},{16,18},{24,26},{7,5},{23,21},{15,13},{31,29},{64,66}... | collective-permute-start | bytes 1572872 | tf_op jit(solution)/shard_map/ppermute | solution.py:115
  13.4 39.5 %collective-permute-start.6 = (f32[256,512]{1,0:T(8,128)S(1)}, f32[256,512]{1,0:T(8,128)S(1)}, u32[]{:S(2)}, u32[]{:S(2)}) collective-permute-start(f32[256,512]{1,0:T(8,128)S(1)} %get-tuple-element.21), channel_id=1, source_target_pairs={{0,1},{8,9},{16,17},{24,25},{7,6},{23,22},{15,14},{31,30},{64,65},... | collective-permute-start | bytes 1572872 | tf_op jit(solution)/shard_map/ppermute | solution.py:115
  53.1 9.3 %collective-permute-start.9 = (f32[256,512]{1,0:T(8,128)S(1)}, f32[256,512]{1,0:T(8,128)S(1)}, u32[]{:S(2)}, u32[]{:S(2)}) collective-permute-start(f32[256,512]{1,0:T(8,128)S(1)} %get-tuple-element.18), channel_id=1, source_target_pairs={{0,4},{1,5},{2,6},{3,7},{8,12},{9,13},{10,14},{11,15},{16,20},{17,... | collective-permute-start | bytes 1572872 | tf_op jit(solution)/shard_map/ppermute | solution.py:115
  62.4 1.4 copy-start.2
  62.6 3.7 %collective-permute-start.10 = (f32[256,512]{1,0:T(8,128)S(1)}, f32[256,512]{1,0:T(8,128)S(1)}, u32[]{:S(2)}, u32[]{:S(2)}) collective-permute-start(f32[256,512]{1,0:T(8,128)S(1)} %get-tuple-element.15), channel_id=1, source_target_pairs={{0,32},{64,96},{128,160},{192,224},{32,0},{96,64},{160,128},{224,1... | collective-permute-start | bytes 1572872 | tf_op jit(solution)/shard_map/ppermute | solution.py:160
  64.8 12.2 %collective-permute-start = (f32[256,512]{1,0:T(8,128)}, f32[256,512]{1,0:T(8,128)}, u32[]{:S(2)}, u32[]{:S(2)}) collective-permute-start(f32[256,512]{1,0:T(8,128)} %get-tuple-element.28), channel_id=1, source_target_pairs={{96,64},{128,160},{97,65},{129,161},{98,66},{130,162},{99,67},{131... | collective-permute-start | bytes 1572872 | tf_op jit(solution)/shard_map/ppermute | solution.py:140
  66.5 29.9 %copy-start.4 = (f32[256,256]{1,0:T(8,128)}, f32[256,256]{1,0:T(8,128)S(1)}, u32[]{:S(2)}) copy-start(f32[256,256]{1,0:T(8,128)S(1)} %broadcast_in_dim.3) | copy-start | bytes 786436
  69.2 0.9 copy-start
  71.7 7.2 %collective-permute-start.14 = (f32[256,512]{1,0:T(8,128)}, f32[256,512]{1,0:T(8,128)S(1)}, u32[]{:S(2)}, u32[]{:S(2)}) collective-permute-start(f32[256,512]{1,0:T(8,128)} %fusion.50), channel_id=1, source_target_pairs={{32,0},{160,128},{64,96},{192,224},{33,1},{161,129},{65,97},{193,2... | collective-permute-start | bytes 1572872 | tf_op jit(solution)/shard_map/ppermute | solution.py:160
  72.9 6.0 %collective-permute-start.13 = (f32[256,512]{1,0:T(8,128)}, f32[256,512]{1,0:T(8,128)}, u32[]{:S(2)}, u32[]{:S(2)}) collective-permute-start(f32[256,512]{1,0:T(8,128)} %fusion.50), channel_id=1, source_target_pairs={{32,64},{160,192},{64,32},{192,160},{33,65},{161,193},{65,33},{193... | collective-permute-start | bytes 1572872 | tf_op jit(solution)/shard_map/ppermute | solution.py:160
  74.4 20.5 %collective-permute-start.12 = (f32[256,512]{1,0:T(8,128)}, f32[256,512]{1,0:T(8,128)}, u32[]{:S(2)}, u32[]{:S(2)}) collective-permute-start(f32[256,512]{1,0:T(8,128)} %fusion.50), channel_id=1, source_target_pairs={{32,96},{160,224},{64,0},{192,128},{33,97},{161,225},{65,1},{193,1... | collective-permute-start | bytes 1572872 | tf_op jit(solution)/shard_map/ppermute | solution.py:160
  75.7 20.7 %collective-permute-start.11 = (f32[256,512]{1,0:T(8,128)}, f32[256,512]{1,0:T(8,128)}, u32[]{:S(2)}, u32[]{:S(2)}) collective-permute-start(f32[256,512]{1,0:T(8,128)} %get-tuple-element.29), channel_id=1, source_target_pairs={{32,0},{160,128},{64,96},{192,224},{33,1},{161,129},{65,97},{193,2... | collective-permute-start | bytes 1572872 | tf_op jit(solution)/shard_map/ppermute | solution.py:140
  78.2 27.4 %collective-permute-start.1 = (f32[256,512]{1,0:T(8,128)S(1)}, f32[256,512]{1,0:T(8,128)S(1)}, u32[]{:S(2)}, u32[]{:S(2)}) collective-permute-start(f32[256,512]{1,0:T(8,128)S(1)} %broadcast_select_fusion.7), channel_id=1, source_target_pairs={{96,32},{128,192},{97,33},{129,193},{98,34},{130,194},{99,35},{131... | collective-permute-start | bytes 1572872 | tf_op jit(solution)/shard_map/ppermute | solution.py:140
  99.1 1.3 copy-start.1
  101.5 10.7 %collective-permute-start.21 = (f32[256,512]{1,0:T(8,128)}, f32[256,512]{1,0:T(8,128)S(1)}, u32[]{:S(2)}, u32[]{:S(2)}) collective-permute-start(f32[256,512]{1,0:T(8,128)} %fusion.49), channel_id=1, source_target_pairs={{96,0},{128,224},{97,1},{129,225},{98,2},{130,226},{99,3},{131,227... | collective-permute-start | bytes 1572872 | tf_op jit(solution)/shard_map/ppermute | solution.py:160
  102.7 10.9 %collective-permute-start.20 = (f32[256,512]{1,0:T(8,128)}, f32[256,512]{1,0:T(8,128)S(1)}, u32[]{:S(2)}, u32[]{:S(2)}) collective-permute-start(f32[256,512]{1,0:T(8,128)} %fusion.49), channel_id=1, source_target_pairs={{96,32},{128,192},{97,33},{129,193},{98,34},{130,194},{99,35},{131... | collective-permute-start | bytes 1572872 | tf_op jit(solution)/shard_map/ppermute | solution.py:160
  103.4 31.3 %collective-permute-start.19 = (f32[256,512]{1,0:T(8,128)}, f32[256,512]{1,0:T(8,128)S(1)}, u32[]{:S(2)}, u32[]{:S(2)}) collective-permute-start(f32[256,512]{1,0:T(8,128)} %fusion.49), channel_id=1, source_target_pairs={{96,64},{128,160},{97,65},{129,161},{98,66},{130,162},{99,67},{131... | collective-permute-start | bytes 1572872 | tf_op jit(solution)/shard_map/ppermute | solution.py:160
  104.1 32.1 %collective-permute-start.18 = (f32[256,512]{1,0:T(8,128)}, f32[256,512]{1,0:T(8,128)}, u32[]{:S(2)}, u32[]{:S(2)}) collective-permute-start(f32[256,512]{1,0:T(8,128)} %fusion.49), channel_id=1, source_target_pairs={{96,128},{128,96},{97,129},{129,97},{98,130},{130,98},{99,131},{13... | collective-permute-start | bytes 1572872 | tf_op jit(solution)/shard_map/ppermute | solution.py:160
  105.6 8.1 %copy-start.3 = (f32[256,512]{1,0:T(8,128)}, f32[256,512]{1,0:T(8,128)S(1)}, u32[]{:S(2)}) copy-start(f32[256,512]{1,0:T(8,128)S(1)} %collective-permute-done.1) | copy-start | bytes 1572868
  105.6 30.6 %collective-permute-start.17 = (f32[256,512]{1,0:T(8,128)}, f32[256,512]{1,0:T(8,128)}, u32[]{:S(2)}, u32[]{:S(2)}) collective-permute-start(f32[256,512]{1,0:T(8,128)} %fusion.49), channel_id=1, source_target_pairs={{96,160},{128,64},{97,161},{129,65},{98,162},{130,66},{99,163},{13... | collective-permute-start | bytes 1572872 | tf_op jit(solution)/shard_map/ppermute | solution.py:160
  112.2 24.1 %collective-permute-start.16 = (f32[256,512]{1,0:T(8,128)}, f32[256,512]{1,0:T(8,128)}, u32[]{:S(2)}, u32[]{:S(2)}) collective-permute-start(f32[256,512]{1,0:T(8,128)} %fusion.49), channel_id=1, source_target_pairs={{96,192},{128,32},{97,193},{129,33},{98,194},{130,34},{99,195},{13... | collective-permute-start | bytes 1572872 | tf_op jit(solution)/shard_map/ppermute | solution.py:160
  113.7 22.5 %collective-permute-start.15 = (f32[256,512]{1,0:T(8,128)}, f32[256,512]{1,0:T(8,128)}, u32[]{:S(2)}, u32[]{:S(2)}) collective-permute-start(f32[256,512]{1,0:T(8,128)} %fusion.49), channel_id=1, source_target_pairs={{96,224},{128,0},{97,225},{129,1},{98,226},{130,2},{99,227},{131,3... | collective-permute-start | bytes 1572872 | tf_op jit(solution)/shard_map/ppermute | solution.py:160
  134.8 12.6 %copy-start.5 = (f32[256,256]{1,0:T(8,128)S(1)}, f32[256,256]{1,0:T(8,128)}, u32[]{:S(2)}) copy-start(f32[256,256]{1,0:T(8,128)} %copy-done.4) | copy-start | bytes 786436
  134.8 12.6 %collective-permute-start.2 = (f32[256,512]{1,0:T(8,128)}, f32[256,512]{1,0:T(8,128)S(1)}, u32[]{:S(2)}, u32[]{:S(2)}) collective-permute-start(f32[256,512]{1,0:T(8,128)} %broadcast_select_fusion.8), channel_id=1, source_target_pairs={{96,0},{128,224},{97,1},{129,225},{98,2},{130,226},{99,3},{131,227... | collective-permute-start | bytes 1572872 | tf_op jit(solution)/shard_map/ppermute | solution.py:140

commit v6 on v5

--- a/solution.py
+++ b/solution.py
@@ -44,13 +44,21 @@
     low = flag_ref[0] == 1
     v = v_ref[...]
     w = w_ref[...]
-    prod = jnp.dot(jnp.where(low, v, w), x_ref[...], precision=lax.Precision.HIGHEST,
-                   preferred_element_type=jnp.float32)
+    driver = jnp.where(low, v, w)
+    d_hi = driver.astype(jnp.bfloat16)
+    d_lo = (driver - d_hi.astype(jnp.float32)).astype(jnp.bfloat16)
+    x = x_ref[...]
+    x_hi = x.astype(jnp.bfloat16)
+    x_lo = (x - x_hi.astype(jnp.float32)).astype(jnp.bfloat16)
+    prod = jnp.dot(d_hi, x_hi, preferred_element_type=jnp.float32)
+    prod += jnp.dot(d_hi, x_lo, preferred_element_type=jnp.float32)
+    prod += jnp.dot(d_lo, x_hi, preferred_element_type=jnp.float32)
     go_ref[...] = g_ref[...] - prod[:, :LOAD_COLS]
     left_term = prod[:, LOAD_COLS:LOAD_COLS + HALF_BAND]
     right_term = prod[:, LOAD_COLS + HALF_BAND:]
     wo_ref[...] = jnp.where(low, w - left_term, -left_term)
     vo_ref[...] = jnp.where(low, -right_term, v - right_term)
+
 
 def bulk_update(flag, x, v, w, g, tile=512):
     rows = v.shape[0]
@@ -146,6 +154,7 @@
         top, bottom = core_tree(first_tip, last_tip, chain_pos, row_pos, chain_count, 8, 4)
     else:
         top, bottom = spread_tips(first_tip, last_tip, row_pos, row_count, row_fanouts(row_count))
+    inverses, top, bottom = lax.optimization_barrier((inverses, top, bottom))
     blank_block = jnp.zeros((band, band), jnp.float32)
     for level in range(LEVELS):
         half = 2**level

time: 160 us -> 152 us (0.950)
  the two profiles are of different devices: /device:TPU:72 before, /device:TPU:73 now
where the time goes in v6:
time: 152 us; the launch traced here: 151 us
  waiting for transfers between devices  43.8 us (29%)
  starting transfers between devices  40.7 us (27%)
  Pallas kernels  23.9 us (16%)
  other arithmetic  14.8 us (10%)
  between operations  11.2 us (7%)
  local copies, waits for them, and re-layouts  9.09 us (6%)
  matrix products  7.75 us (5%)
    ppermute x11, starting transfers between devices, on_device(): got = lax.ppermute(sent, 'chain', pairs)  26.7 us
    pallas_call x3, Pallas kernels, bulk_update(): pl.pallas_call(bulk_kernel, grid_spec=pltpu.PrefetchScalarGridSpec(num_sc...  23.9 us
    ppermute x7, waiting for transfers between devices, core_tree(): lax.ppermute(sent, ('chain', 'rows'), pairs)  22.2 us
    ppermute x11, waiting for transfers between devices, on_device(): got = lax.ppermute(sent, 'chain', pairs)  21.6 us
    ppermute x7, starting transfers between devices, core_tree(): lax.ppermute(sent, ('chain', 'rows'), pairs)  7.14 us
    ppermute x4, starting transfers between devices, on_device(): got = lax.ppermute(mine, 'chain', pairs)  6.8 us
    dot_general x3, matrix products, on_device(): jnp.dot(inverses[level], tip_rhs, precision=precise, preferred_element_ty...  5.28 us
    select_n x3, other arithmetic, core_tree(): sent = jnp.where(mine[3 * step + 2] == 1, top, bottom)  4.97 us
  transfers between devices with their start and end apart: 22, of which 6 were waited for; matrix products, arithmetic and copies ran while one was open for 8% of the time, Pallas kernels for 11%

profile of v6, /device:TPU:73, one launch (start us, length us, event | category | flops | bytes accessed | tf_op | source)
XLA Modules:
  0.0 151.3 jit_solution(9469596597494757336)
XLA Ops:
  0.6 0.0 copy-start.11
  0.6 2.5 %slice_bitcast_fusion = (f32[256,512]{1,0:T(8,128)}, f32[256,512]{1,0:T(8,128)}, f32[256,512]{1,0:T(8,128)}) fusion(f32[1,3,256,512]{3,2,1,0:T(8,128)} %param.8), kind=kLoop, calls=%fused_computation.57 | loop fusion | bytes 3145728 | tf_op jit(solution)/shard_map/squeeze | solution.py:145
  3.2 0.7 collective-permute-start.1
  3.9 3.4 %collective-permute-start = (f32[256,512]{1,0:T(8,128)}, f32[256,512]{1,0:T(8,128)}, u32[]{:S(2)}, u32[]{:S(2)}) collective-permute-start(f32[256,512]{1,0:T(8,128)} %get-tuple-element.41), channel_id=1, source_target_pairs={{32,0},{160,128},{64,96},{192,224},{33,1},{161,129},{65,97},{193,2... | collective-permute-start | bytes 1572872 | tf_op jit(solution)/shard_map/ppermute | solution.py:148
  7.2 1.0 slice.145
  8.2 1.1 slice.148
  9.3 0.7 fusion.64
  10.6 1.1 fusion.58
  11.7 0.9 fusion.44
  12.5 1.4 collective-permute-start.6
  14.0 1.5 collective-permute-start.5
  15.4 1.5 collective-permute-start.4
  21.3 0.8 copy-done.10
  22.1 1.0 broadcast_select_fusion.7
  23.1 1.3 collective-permute-start.2
  24.4 2.4 %broadcast_select_fusion.5 = (f32[256,512]{1,0:T(8,128)}, f32[256,512]{1,0:T(8,128)S(1)}, f32[256,512]{1,0:T(8,128)S(1)}) fusion(pred[]{:T(512)} %bitcast.11, f32[256,512]{1,0:T(8,128)} %collective-permute-done.5, f32[256,512]{1,0:T(8,128)} %collective-permute-done.6, pred[]{:T(512)} %bitcast.14, f32[256,512]{1,0:T(8,128)} %collective-permute-done.4, ...), kind=kLoop, calls=%fused_computation.78 | loop fusion | flops 1179648 | bytes 4194311 | tf_op jit(solution)/shard_map/jit(_where)/select_n | solution.py:122
  26.9 0.7 collective-permute-start.9
  27.6 0.7 collective-permute-start.8
  28.3 1.3 collective-permute-start.7
  33.5 1.1 broadcast_select_fusion.8
  34.6 1.5 collective-permute-start.3
  36.1 16.1 %collective-permute-done.7 = f32[256,512]{1,0:T(8,128)} collective-permute-done((f32[256,512]{1,0:T(8,128)}, f32[256,512]{1,0:T(8,128)}, u32[]{:S(2)}, u32[]{:S(2)}) %collective-permute-start.7) | collective-permute-done | bytes 524320 | tf_op jit(solution)/shard_map/ppermute | solution.py:123
  52.2 1.7 %broadcast_select_fusion.4 = (f32[256,512]{1,0:T(8,128)S(1)}, f32[256,512]{1,0:T(8,128)S(1)}, f32[256,512]{1,0:T(8,128)S(1)}) fusion(pred[]{:T(512)} %bitcast.16, f32[256,512]{1,0:T(8,128)} %copy-done.4, f32[256,512]{1,0:T(8,128)} %copy-done.3, pred[]{:T(512)} %bitcast.19, f32[256,512]{1,0:T(8,128)S(1)} %get-tuple-element.29, ...), kind=kLoop, calls=%fused_computation.77 | loop fusion | flops 917504 | bytes 4194311 | tf_op jit(solution)/shard_map/jit(_where)/select_n | solution.py:122
  53.9 0.1 collective-permute-start.10
  55.2 0.9 broadcast_select_fusion.9
  56.2 6.1 %collective-permute-done.10 = f32[256,512]{1,0:T(8,128)S(1)} collective-permute-done((f32[256,512]{1,0:T(8,128)S(1)}, f32[256,512]{1,0:T(8,128)S(1)}, u32[]{:S(2)}, u32[]{:S(2)}) %collective-permute-start.10) | collective-permute-done | bytes 524320 | tf_op jit(solution)/shard_map/ppermute | solution.py:123
  62.3 0.8 copy-done.5
  63.1 1.2 broadcast_select_fusion.3
  64.3 0.1 broadcast_select_fusion.1
  64.4 1.7 %collective-permute-start.11 = (f32[256,512]{1,0:T(8,128)S(1)}, f32[256,512]{1,0:T(8,128)S(1)}, u32[]{:S(2)}, u32[]{:S(2)}) collective-permute-start(f32[256,512]{1,0:T(8,128)S(1)} %broadcast_select_fusion.1), channel_id=1, source_target_pairs={{0,32},{64,96},{128,160},{192,224},{32,0},{96,64},{160,128},{224,1... | collective-permute-start | bytes 1572872 | tf_op jit(solution)/shard_map/ppermute | solution.py:169
  66.1 1.5 %collective-permute-done.11 = f32[256,512]{1,0:T(8,128)S(1)} collective-permute-done((f32[256,512]{1,0:T(8,128)S(1)}, f32[256,512]{1,0:T(8,128)S(1)}, u32[]{:S(2)}, u32[]{:S(2)}) %collective-permute-start.11) | collective-permute-done | bytes 524320 | tf_op jit(solution)/shard_map/ppermute | solution.py:169
  67.6 0.1 broadcast_select_fusion
  67.8 1.5 fusion.2.x_ref
  69.3 0.6 fusion.32
  70.0 0.6 fusion.34
  70.6 0.1 slice_subtract_fusion.2
  70.8 0.9 fusion.43
  71.6 2.3 %collective-permute-start.14 = (f32[256,512]{1,0:T(8,128)}, f32[256,512]{1,0:T(8,128)S(1)}, u32[]{:S(2)}, u32[]{:S(2)}) collective-permute-start(f32[256,512]{1,0:T(8,128)} %fusion.43), channel_id=1, source_target_pairs={{32,0},{160,128},{64,96},{192,224},{33,1},{161,129},{65,97},{193,2... | collective-permute-start | bytes 1572872 | tf_op jit(solution)/shard_map/ppermute | solution.py:169
  74.0 13.0 %collective-permute-start.13 = (f32[256,512]{1,0:T(8,128)}, f32[256,512]{1,0:T(8,128)S(1)}, u32[]{:S(2)}, u32[]{:S(2)}) collective-permute-start(f32[256,512]{1,0:T(8,128)} %fusion.43), channel_id=1, source_target_pairs={{32,64},{160,192},{64,32},{192,160},{33,65},{161,193},{65,33},{193... | collective-permute-start | bytes 1572872 | tf_op jit(solution)/shard_map/ppermute | solution.py:169
  87.0 2.1 %collective-permute-start.12 = (f32[256,512]{1,0:T(8,128)}, f32[256,512]{1,0:T(8,128)}, u32[]{:S(2)}, u32[]{:S(2)}) collective-permute-start(f32[256,512]{1,0:T(8,128)} %fusion.43), channel_id=1, source_target_pairs={{32,96},{160,224},{64,0},{192,128},{33,97},{161,225},{65,1},{193,1... | collective-permute-start | bytes 1572872 | tf_op jit(solution)/shard_map/ppermute | solution.py:169
  89.1 5.0 %collective-permute-done.13 = f32[256,512]{1,0:T(8,128)S(1)} collective-permute-done((f32[256,512]{1,0:T(8,128)}, f32[256,512]{1,0:T(8,128)S(1)}, u32[]{:S(2)}, u32[]{:S(2)}) %collective-permute-start.13) | collective-permute-done | bytes 524320 | tf_op jit(solution)/shard_map/ppermute | solution.py:169
  94.1 0.8 copy-done.6
  94.9 4.2 %collective-permute-done.12 = f32[256,512]{1,0:T(8,128)} collective-permute-done((f32[256,512]{1,0:T(8,128)}, f32[256,512]{1,0:T(8,128)}, u32[]{:S(2)}, u32[]{:S(2)}) %collective-permute-start.12) | collective-permute-done | bytes 524320 | tf_op jit(solution)/shard_map/ppermute | solution.py:169
  99.0 1.4 select_select_fusion.2
  100.5 1.5 fusion.6.x_ref
  102.0 0.6 fusion.30
  102.7 0.1 slice_subtract_fusion.1
  102.8 0.1 copy-done.2
  102.9 0.6 fusion.38
  103.5 0.1 slice_subtract_fusion
  103.6 0.9 fusion.42
  104.5 0.7 collective-permute-start.21
  105.2 1.3 collective-permute-start.20
  106.5 0.7 collective-permute-start.19
  107.2 0.7 collective-permute-start.18
  107.9 1.4 collective-permute-start.17
  109.3 1.3 collective-permute-start.16
  110.6 10.9 %collective-permute-done.20 = f32[256,512]{1,0:T(8,128)S(1)} collective-permute-done((f32[256,512]{1,0:T(8,128)}, f32[256,512]{1,0:T(8,128)S(1)}, u32[]{:S(2)}, u32[]{:S(2)}) %collective-permute-start.20) | collective-permute-done | bytes 524320 | tf_op jit(solution)/shard_map/ppermute | solution.py:169
  121.5 1.5 collective-permute-start.15
  123.0 8.0 %shard_map.76 = (f32[2048,256]{1,0:T(8,128)}, f32[2048,256]{1,0:T(8,128)}, f32[2048,256]{1,0:T(8,128)}) custom-call(s32[1]{0:T(128)} %bitcast.22.flag_ref, f32[256,768]{1,0:T(8,128)} %copy-done.1, f32[2048,256]{1,0:T(8,128)} %v_ref.1, f32[2048,256]{1,0:T(8,128)} %w_ref.1, f32[2048,256]{1,0:T(8,128)} %g_ref.1), custom_call_target="tpu_custom_call" | custom-call | tf_op jit(solution)/shard_map/pallas_call | solution.py:67
  131.0 8.0 %shard_map.77 = (f32[2048,256]{1,0:T(8,128)}, f32[2048,256]{1,0:T(8,128)}, f32[2048,256]{1,0:T(8,128)}) custom-call(s32[1]{0:T(128)} %bitcast.21.flag_ref, f32[256,768]{1,0:T(8,128)} %copy-done.2, f32[2048,256]{1,0:T(8,128)} %get-tuple-element.19.v_ref, f32[2048,256]{1,0:T(8,128)} %get-tuple-element.20.w_ref, f32[2048,256]{1,0:T(8,128)} %get-tuple-element.21.g_ref), custom_call_target="tpu_custom_call" | custom-call | tf_op jit(solution)/shard_map/pallas_call | solution.py:67
  139.0 1.9 %select_select_fusion = (f32[256,512]{1,0:T(8,128)S(1)}, f32[256,512]{1,0:T(8,128)S(1)}) fusion(f32[256,512]{1,0:T(8,128)} %collective-permute-done.15, f32[256,512]{1,0:T(8,128)} %collective-permute-done.16, f32[256,512]{1,0:T(8,128)} %collective-permute-done.17, f32[256,512]{1,0:T(8,128)S(1)} %collective-permute-done.18, ...), kind=kLoop, calls=%fused_computation.49 | loop fusion | flops 2097152 | bytes 5767176 | tf_op jit(solution)/shard_map/jit(_where)/select_n | solution.py:171
  141.0 2.3 %fusion.10.x_ref = f32[256,768]{1,0:T(8,128)} fusion(f32[256,512]{1,0:T(8,128)S(1)} %copy-done.7, f32[256,256]{1,0:T(8,128)S(1)} %broadcast_in_dim.3, f32[256,512]{1,0:T(8,128)S(1)} %get-tuple-element.32, f32[256,256]{1,0:T(8,128)S(1)} %get-tuple-element.47, f32[256,256]{1,0:T(8,128)S(1)} %get-tuple-element.46), kind=kOutput, calls=%fused_computation.11 | convolution fusion | flops 1209925632 | bytes 2621440 | tf_op jit(solution)/shard_map/dot_general | solution.py:175
  143.4 8.0 %shard_map.78 = (f32[2048,256]{1,0:T(8,128)}, f32[2048,256]{1,0:T(8,128)}, f32[2048,256]{1,0:T(8,128)}) custom-call(s32[1]{0:T(128)} %bitcast.flag_ref, f32[256,768]{1,0:T(8,128)} %fusion.10.x_ref, f32[2048,256]{1,0:T(8,128)} %get-tuple-element.22.v_ref, f32[2048,256]{1,0:T(8,128)} %get-tuple-element.23.w_ref, f32[2048,256]{1,0:T(8,128)} %get-tuple-element.24.g_ref), custom_call_target="tpu_custom_call" | custom-call | tf_op jit(solution)/shard_map/pallas_call | solution.py:67
  (41 shorter events, 0.3 us)
Async XLA Ops:
  0.6 8.7 %copy-start.11 = (s32[9,2,32]{2,1,0:T(2,128)S(1)}, s32[9,2,32]{2,1,0:T(2,128)}, u32[]{:S(2)}) copy-start(s32[9,2,32]{2,1,0:T(2,128)} %constant.82.clone) | copy-start | bytes 6916
  3.2 18.1 %collective-permute-start.1 = (f32[256,512]{1,0:T(8,128)}, f32[256,512]{1,0:T(8,128)S(1)}, u32[]{:S(2)}, u32[]{:S(2)}) collective-permute-start(f32[256,512]{1,0:T(8,128)} %get-tuple-element.39), channel_id=1, source_target_pairs={{96,64},{128,160},{97,65},{129,161},{98,66},{130,162},{99,67},{131... | collective-permute-start | bytes 1572872 | tf_op jit(solution)/shard_map/ppermute | solution.py:148
  3.9 18.2 %collective-permute-start = (f32[256,512]{1,0:T(8,128)}, f32[256,512]{1,0:T(8,128)}, u32[]{:S(2)}, u32[]{:S(2)}) collective-permute-start(f32[256,512]{1,0:T(8,128)} %get-tuple-element.41), channel_id=1, source_target_pairs={{32,0},{160,128},{64,96},{192,224},{33,1},{161,129},{65,97},{193,2... | collective-permute-start | bytes 1572872 | tf_op jit(solution)/shard_map/ppermute | solution.py:148
  8.2 13.9 %copy-start = (f32[1,3,256,512]{3,2,1,0:T(8,128)S(1)}, f32[1,3,256,512]{3,2,1,0:T(8,128)}, u32[]{:S(2)}) copy-start(f32[1,3,256,512]{3,2,1,0:T(8,128)} %param.8) | copy-start | bytes 4718596
  12.5 11.9 %collective-permute-start.6 = (f32[256,512]{1,0:T(8,128)}, f32[256,512]{1,0:T(8,128)}, u32[]{:S(2)}, u32[]{:S(2)}) collective-permute-start(f32[256,512]{1,0:T(8,128)} %fusion.44), channel_id=1, source_target_pairs={{0,24},{31,7},{64,88},{95,71},{128,152},{159,135},{192,216},{223,1... | collective-permute-start | bytes 1572872 | tf_op jit(solution)/shard_map/ppermute | solution.py:123
  14.0 10.4 %collective-permute-start.5 = (f32[256,512]{1,0:T(8,128)}, f32[256,512]{1,0:T(8,128)}, u32[]{:S(2)}, u32[]{:S(2)}) collective-permute-start(f32[256,512]{1,0:T(8,128)} %fusion.44), channel_id=1, source_target_pairs={{0,16},{31,15},{64,80},{95,79},{128,144},{159,143},{192,208},{223,... | collective-permute-start | bytes 1572872 | tf_op jit(solution)/shard_map/ppermute | solution.py:123
  15.4 9.0 %collective-permute-start.4 = (f32[256,512]{1,0:T(8,128)}, f32[256,512]{1,0:T(8,128)}, u32[]{:S(2)}, u32[]{:S(2)}) collective-permute-start(f32[256,512]{1,0:T(8,128)} %fusion.44), channel_id=1, source_target_pairs={{0,8},{31,23},{64,72},{95,87},{128,136},{159,151},{192,200},{223,2... | collective-permute-start | bytes 1572872 | tf_op jit(solution)/shard_map/ppermute | solution.py:123
  21.3 0.8 copy-start.10
  23.1 10.4 %collective-permute-start.2 = (f32[256,512]{1,0:T(8,128)S(1)}, f32[256,512]{1,0:T(8,128)}, u32[]{:S(2)}, u32[]{:S(2)}) collective-permute-start(f32[256,512]{1,0:T(8,128)S(1)} %get-tuple-element.37), channel_id=1, source_target_pairs={{96,32},{128,192},{97,33},{129,193},{98,34},{130,194},{99,35},{131... | collective-permute-start | bytes 1572872 | tf_op jit(solution)/shard_map/ppermute | solution.py:148
  26.9 9.2 %collective-permute-start.9 = (f32[256,512]{1,0:T(8,128)}, f32[256,512]{1,0:T(8,128)S(1)}, u32[]{:S(2)}, u32[]{:S(2)}) collective-permute-start(f32[256,512]{1,0:T(8,128)} %get-tuple-element.28), channel_id=1, source_target_pairs={{0,3},{8,11},{16,19},{24,27},{7,4},{23,20},{15,12},{31,28},{64,67}... | collective-permute-start | bytes 1572872 | tf_op jit(solution)/shard_map/ppermute | solution.py:123
  27.6 8.5 %collective-permute-start.8 = (f32[256,512]{1,0:T(8,128)}, f32[256,512]{1,0:T(8,128)S(1)}, u32[]{:S(2)}, u32[]{:S(2)}) collective-permute-start(f32[256,512]{1,0:T(8,128)} %get-tuple-element.28), channel_id=1, source_target_pairs={{0,2},{8,10},{16,18},{24,26},{7,5},{23,21},{15,13},{31,29},{64,66}... | collective-permute-start | bytes 1572872 | tf_op jit(solution)/shard_map/ppermute | solution.py:123
  28.3 23.9 %collective-permute-start.7 = (f32[256,512]{1,0:T(8,128)}, f32[256,512]{1,0:T(8,128)}, u32[]{:S(2)}, u32[]{:S(2)}) collective-permute-start(f32[256,512]{1,0:T(8,128)} %get-tuple-element.28), channel_id=1, source_target_pairs={{0,1},{8,9},{16,17},{24,25},{7,6},{23,22},{15,14},{31,30},{64,65},... | collective-permute-start | bytes 1572872 | tf_op jit(solution)/shard_map/ppermute | solution.py:123
  34.6 20.6 %collective-permute-start.3 = (f32[256,512]{1,0:T(8,128)S(1)}, f32[256,512]{1,0:T(8,128)}, u32[]{:S(2)}, u32[]{:S(2)}) collective-permute-start(f32[256,512]{1,0:T(8,128)S(1)} %broadcast_select_fusion.8), channel_id=1, source_target_pairs={{96,0},{128,224},{97,1},{129,225},{98,2},{130,226},{99,3},{131,227... | collective-permute-start | bytes 1572872 | tf_op jit(solution)/shard_map/ppermute | solution.py:148
  36.1 16.1 %copy-start.3 = (f32[256,512]{1,0:T(8,128)}, f32[256,512]{1,0:T(8,128)S(1)}, u32[]{:S(2)}) copy-start(f32[256,512]{1,0:T(8,128)S(1)} %collective-permute-done.9) | copy-start | bytes 1572868
  36.1 16.1 %copy-start.4 = (f32[256,512]{1,0:T(8,128)}, f32[256,512]{1,0:T(8,128)S(1)}, u32[]{:S(2)}) copy-start(f32[256,512]{1,0:T(8,128)S(1)} %collective-permute-done.8) | copy-start | bytes 1572868
  53.9 8.4 %collective-permute-start.10 = (f32[256,512]{1,0:T(8,128)S(1)}, f32[256,512]{1,0:T(8,128)S(1)}, u32[]{:S(2)}, u32[]{:S(2)}) collective-permute-start(f32[256,512]{1,0:T(8,128)S(1)} %get-tuple-element.25), channel_id=1, source_target_pairs={{0,4},{1,5},{2,6},{3,7},{8,12},{9,13},{10,14},{11,15},{16,20},{17,... | collective-permute-start | bytes 1572872 | tf_op jit(solution)/shard_map/ppermute | solution.py:123
  62.3 0.8 copy-start.5
  64.4 3.3 %collective-permute-start.11 = (f32[256,512]{1,0:T(8,128)S(1)}, f32[256,512]{1,0:T(8,128)S(1)}, u32[]{:S(2)}, u32[]{:S(2)}) collective-permute-start(f32[256,512]{1,0:T(8,128)S(1)} %broadcast_select_fusion.1), channel_id=1, source_target_pairs={{0,32},{64,96},{128,160},{192,224},{32,0},{96,64},{160,128},{224,1... | collective-permute-start | bytes 1572872 | tf_op jit(solution)/shard_map/ppermute | solution.py:169
  66.1 1.8 %copy-start.8 = (f32[256,512]{1,0:T(8,128)S(1)}, f32[256,512]{1,0:T(8,128)}, u32[]{:S(2)}) copy-start(f32[256,512]{1,0:T(8,128)} %get-tuple-element.16) | copy-start | bytes 1572868
  69.3 1.3 copy-start.1
  71.6 17.5 %collective-permute-start.14 = (f32[256,512]{1,0:T(8,128)}, f32[256,512]{1,0:T(8,128)S(1)}, u32[]{:S(2)}, u32[]{:S(2)}) collective-permute-start(f32[256,512]{1,0:T(8,128)} %fusion.43), channel_id=1, source_target_pairs={{32,0},{160,128},{64,96},{192,224},{33,1},{161,129},{65,97},{193,2... | collective-permute-start | bytes 1572872 | tf_op jit(solution)/shard_map/ppermute | solution.py:169
  74.0 20.1 %collective-permute-start.13 = (f32[256,512]{1,0:T(8,128)}, f32[256,512]{1,0:T(8,128)S(1)}, u32[]{:S(2)}, u32[]{:S(2)}) collective-permute-start(f32[256,512]{1,0:T(8,128)} %fusion.43), channel_id=1, source_target_pairs={{32,64},{160,192},{64,32},{192,160},{33,65},{161,193},{65,33},{193... | collective-permute-start | bytes 1572872 | tf_op jit(solution)/shard_map/ppermute | solution.py:169
  87.0 12.0 %collective-permute-start.12 = (f32[256,512]{1,0:T(8,128)}, f32[256,512]{1,0:T(8,128)}, u32[]{:S(2)}, u32[]{:S(2)}) collective-permute-start(f32[256,512]{1,0:T(8,128)} %fusion.43), channel_id=1, source_target_pairs={{32,96},{160,224},{64,0},{192,128},{33,97},{161,225},{65,1},{193,1... | collective-permute-start | bytes 1572872 | tf_op jit(solution)/shard_map/ppermute | solution.py:169
  89.1 11.4 %copy-start.9 = (f32[256,512]{1,0:T(8,128)S(1)}, f32[256,512]{1,0:T(8,128)}, u32[]{:S(2)}) copy-start(f32[256,512]{1,0:T(8,128)} %get-tuple-element.18) | copy-start | bytes 1572868
  94.1 0.8 copy-start.6
  102.0 0.9 copy-start.2
  104.5 4.8 %collective-permute-start.21 = (f32[256,512]{1,0:T(8,128)}, f32[256,512]{1,0:T(8,128)S(1)}, u32[]{:S(2)}, u32[]{:S(2)}) collective-permute-start(f32[256,512]{1,0:T(8,128)} %fusion.42), channel_id=1, source_target_pairs={{96,0},{128,224},{97,1},{129,225},{98,2},{130,226},{99,3},{131,227... | collective-permute-start | bytes 1572872 | tf_op jit(solution)/shard_map/ppermute | solution.py:169
  105.2 16.4 %collective-permute-start.20 = (f32[256,512]{1,0:T(8,128)}, f32[256,512]{1,0:T(8,128)S(1)}, u32[]{:S(2)}, u32[]{:S(2)}) collective-permute-start(f32[256,512]{1,0:T(8,128)} %fusion.42), channel_id=1, source_target_pairs={{96,32},{128,192},{97,33},{129,193},{98,34},{130,194},{99,35},{131... | collective-permute-start | bytes 1572872 | tf_op jit(solution)/shard_map/ppermute | solution.py:169
  106.5 32.5 %collective-permute-start.19 = (f32[256,512]{1,0:T(8,128)}, f32[256,512]{1,0:T(8,128)S(1)}, u32[]{:S(2)}, u32[]{:S(2)}) collective-permute-start(f32[256,512]{1,0:T(8,128)} %fusion.42), channel_id=1, source_target_pairs={{96,64},{128,160},{97,65},{129,161},{98,66},{130,162},{99,67},{131... | collective-permute-start | bytes 1572872 | tf_op jit(solution)/shard_map/ppermute | solution.py:169
  107.2 31.8 %collective-permute-start.18 = (f32[256,512]{1,0:T(8,128)}, f32[256,512]{1,0:T(8,128)S(1)}, u32[]{:S(2)}, u32[]{:S(2)}) collective-permute-start(f32[256,512]{1,0:T(8,128)} %fusion.42), channel_id=1, source_target_pairs={{96,128},{128,96},{97,129},{129,97},{98,130},{130,98},{99,131},{13... | collective-permute-start | bytes 1572872 | tf_op jit(solution)/shard_map/ppermute | solution.py:169
  107.9 31.1 %collective-permute-start.17 = (f32[256,512]{1,0:T(8,128)}, f32[256,512]{1,0:T(8,128)}, u32[]{:S(2)}, u32[]{:S(2)}) collective-permute-start(f32[256,512]{1,0:T(8,128)} %fusion.42), channel_id=1, source_target_pairs={{96,160},{128,64},{97,161},{129,65},{98,162},{130,66},{99,163},{13... | collective-permute-start | bytes 1572872 | tf_op jit(solution)/shard_map/ppermute | solution.py:169
  109.3 29.7 %collective-permute-start.16 = (f32[256,512]{1,0:T(8,128)}, f32[256,512]{1,0:T(8,128)}, u32[]{:S(2)}, u32[]{:S(2)}) collective-permute-start(f32[256,512]{1,0:T(8,128)} %fusion.42), channel_id=1, source_target_pairs={{96,192},{128,32},{97,193},{129,33},{98,194},{130,34},{99,195},{13... | collective-permute-start | bytes 1572872 | tf_op jit(solution)/shard_map/ppermute | solution.py:169
  121.5 17.5 %collective-permute-start.15 = (f32[256,512]{1,0:T(8,128)}, f32[256,512]{1,0:T(8,128)}, u32[]{:S(2)}, u32[]{:S(2)}) collective-permute-start(f32[256,512]{1,0:T(8,128)} %fusion.42), channel_id=1, source_target_pairs={{96,224},{128,0},{97,225},{129,1},{98,226},{130,2},{99,227},{131,3... | collective-permute-start | bytes 1572872 | tf_op jit(solution)/shard_map/ppermute | solution.py:169
  139.0 2.0 %copy-start.7 = (f32[256,512]{1,0:T(8,128)S(1)}, f32[256,512]{1,0:T(8,128)}, u32[]{:S(2)}) copy-start(f32[256,512]{1,0:T(8,128)} %broadcast_select_fusion.9) | copy-start | bytes 1572868

commit v7 on v6

--- a/solution.py
+++ b/solution.py
@@ -169,6 +169,10 @@
             got = lax.ppermute(sent, "chain", pairs)
             lower_tip = jnp.where(place == half - 1 + offset, got, lower_tip)
             upper_tip = jnp.where(place == half - offset, got, upper_tip)
+        if level > 0:
+            lower_tip, upper_tip, spike_right, spike_left, load_block = lax.optimization_barrier(
+                (lower_tip, upper_tip, spike_right, spike_left, load_block)
+            )
         upper_rows = jnp.concatenate([lower_tip[:, :band], lower_tip[:, band:], blank_block], 1)
         lower_rows = jnp.concatenate([upper_tip[:, :band], blank_block, upper_tip[:, band:]], 1)
         tip_rhs = jnp.concatenate([upper_rows, lower_rows], 0)

time: 152 us -> 133 us (0.88)
  the two profiles are of different devices: /device:TPU:73 before, /device:TPU:31 now
where the time goes in v7:
time: 133 us; the launch traced here: 132 us
  starting transfers between devices  34.8 us (26%)
  waiting for transfers between devices  33.7 us (25%)
  Pallas kernels  24 us (18%)
  other arithmetic  13.8 us (10%)
  between operations  11.8 us (9%)
  matrix products  7.78 us (6%)
  local copies, waits for them, and re-layouts  6.51 us (5%)
    pallas_call x3, Pallas kernels, bulk_update(): pl.pallas_call(bulk_kernel, grid_spec=pltpu.PrefetchScalarGridSpec(num_sc...  24 us
    ppermute x11, waiting for transfers between devices, on_device(): got = lax.ppermute(sent, 'chain', pairs)  20 us
    ppermute x7, starting transfers between devices, core_tree(): lax.ppermute(sent, ('chain', 'rows'), pairs)  17.4 us
    ppermute x7, waiting for transfers between devices, core_tree(): lax.ppermute(sent, ('chain', 'rows'), pairs)  13.7 us
    ppermute x11, starting transfers between devices, on_device(): got = lax.ppermute(sent, 'chain', pairs)  11.9 us
    ppermute x4, starting transfers between devices, on_device(): got = lax.ppermute(mine, 'chain', pairs)  5.49 us
    dot_general x3, matrix products, on_device(): jnp.dot(inverses[level], tip_rhs, precision=precise, preferred_element_ty...  5.32 us
    select_n x3, other arithmetic, core_tree(): sent = jnp.where(mine[3 * step + 2] == 1, top, bottom)  4.8 us
  transfers between devices with their start and end apart: 22, of which 8 were waited for; matrix products, arithmetic and copies ran while one was open for 10% of the time, Pallas kernels for 12%

profile of v7, /device:TPU:31, one launch (start us, length us, event | category | flops | bytes accessed | tf_op | source)
XLA Modules:
  0.0 132.4 jit_solution(16102955846848294272)
XLA Ops:
  0.6 0.0 copy-start.8
  0.6 2.4 %slice_bitcast_fusion = (f32[256,512]{1,0:T(8,128)}, f32[256,512]{1,0:T(8,128)}, f32[256,512]{1,0:T(8,128)S(1)}) fusion(f32[1,3,256,512]{3,2,1,0:T(8,128)} %param.8), kind=kLoop, calls=%fused_computation.57 | loop fusion | bytes 3145728 | tf_op jit(solution)/shard_map/squeeze | solution.py:145
  3.1 1.5 %collective-permute-start.1 = (f32[256,512]{1,0:T(8,128)}, f32[256,512]{1,0:T(8,128)}, u32[]{:S(2)}, u32[]{:S(2)}) collective-permute-start(f32[256,512]{1,0:T(8,128)} %get-tuple-element.59), channel_id=1, source_target_pairs={{96,64},{128,160},{97,65},{129,161},{98,66},{130,162},{99,67},{131... | collective-permute-start | bytes 1572872 | tf_op jit(solution)/shard_map/ppermute | solution.py:148
  4.5 1.3 collective-permute-start
  5.9 1.0 slice.148
  6.8 0.0 copy-start
  6.8 1.1 slice.145
  7.9 0.7 fusion.64
  9.3 1.1 fusion.58
  10.4 0.9 fusion.44
  11.2 1.5 %collective-permute-start.5 = (f32[256,512]{1,0:T(8,128)}, f32[256,512]{1,0:T(8,128)}, u32[]{:S(2)}, u32[]{:S(2)}) collective-permute-start(f32[256,512]{1,0:T(8,128)} %fusion.44), channel_id=1, source_target_pairs={{0,16},{31,15},{64,80},{95,79},{128,144},{159,143},{192,208},{223,... | collective-permute-start | bytes 1572872 | tf_op jit(solution)/shard_map/ppermute | solution.py:123
  12.7 1.3 collective-permute-start.6
  14.0 1.5 %collective-permute-start.4 = (f32[256,512]{1,0:T(8,128)}, f32[256,512]{1,0:T(8,128)}, u32[]{:S(2)}, u32[]{:S(2)}) collective-permute-start(f32[256,512]{1,0:T(8,128)} %fusion.44), channel_id=1, source_target_pairs={{0,8},{31,23},{64,72},{95,87},{128,136},{159,151},{192,200},{223,2... | collective-permute-start | bytes 1572872 | tf_op jit(solution)/shard_map/ppermute | solution.py:123
  19.9 2.1 %broadcast_select_fusion.7 = (f32[256,512]{1,0:T(8,128)S(1)}, f32[256,512]{1,0:T(8,128)}) fusion(f32[256,512]{1,0:T(8,128)} %collective-permute-done.1, pred[]{:T(512)S(6)} %or.15, f32[1,3,256,512]{3,2,1,0:T(8,128)S(1)} %copy-done, f32[256,512]{1,0:T(8,128)} %collective-permute-done, pred[]{:T(512)S(6)} %or.12), kind=kLoop, calls=%fused_computation.80 | loop fusion | flops 262144 | bytes 3145730 | tf_op jit(solution)/shard_map/jit(_where)/select_n | solution.py:149
  22.0 1.5 %collective-permute-start.2 = (f32[256,512]{1,0:T(8,128)S(1)}, f32[256,512]{1,0:T(8,128)}, u32[]{:S(2)}, u32[]{:S(2)}) collective-permute-start(f32[256,512]{1,0:T(8,128)S(1)} %get-tuple-element.57), channel_id=1, source_target_pairs={{96,32},{128,192},{97,33},{129,193},{98,34},{130,194},{99,35},{131... | collective-permute-start | bytes 1572872 | tf_op jit(solution)/shard_map/ppermute | solution.py:148
  23.4 1.5 %collective-permute-done.6 = f32[256,512]{1,0:T(8,128)} collective-permute-done((f32[256,512]{1,0:T(8,128)}, f32[256,512]{1,0:T(8,128)}, u32[]{:S(2)}, u32[]{:S(2)}) %collective-permute-start.6) | collective-permute-done | bytes 524320 | tf_op jit(solution)/shard_map/ppermute | solution.py:123
  24.9 1.6 %broadcast_select_fusion.5 = (f32[256,512]{1,0:T(8,128)S(1)}, f32[256,512]{1,0:T(8,128)S(1)}, f32[256,512]{1,0:T(8,128)S(1)}) fusion(pred[]{:T(512)} %bitcast.11, f32[256,512]{1,0:T(8,128)} %collective-permute-done.5, f32[256,512]{1,0:T(8,128)} %collective-permute-done.6, pred[]{:T(512)} %bitcast.14, f32[256,512]{1,0:T(8,128)} %collective-permute-done.4, ...), kind=kLoop, calls=%fused_computation.78 | loop fusion | flops 1179648 | bytes 4194311 | tf_op jit(solution)/shard_map/jit(_where)/select_n | solution.py:122
  26.6 7.5 %collective-permute-start.8 = (f32[256,512]{1,0:T(8,128)S(1)}, f32[256,512]{1,0:T(8,128)S(1)}, u32[]{:S(2)}, u32[]{:S(2)}) collective-permute-start(f32[256,512]{1,0:T(8,128)S(1)} %get-tuple-element.48), channel_id=1, source_target_pairs={{0,2},{8,10},{16,18},{24,26},{7,5},{23,21},{15,13},{31,29},{64,66}... | collective-permute-start | bytes 1572872 | tf_op jit(solution)/shard_map/ppermute | solution.py:123
  34.1 2.1 %collective-permute-start.9 = (f32[256,512]{1,0:T(8,128)S(1)}, f32[256,512]{1,0:T(8,128)}, u32[]{:S(2)}, u32[]{:S(2)}) collective-permute-start(f32[256,512]{1,0:T(8,128)S(1)} %get-tuple-element.48), channel_id=1, source_target_pairs={{0,3},{8,11},{16,19},{24,27},{7,4},{23,20},{15,12},{31,28},{64,67}... | collective-permute-start | bytes 1572872 | tf_op jit(solution)/shard_map/ppermute | solution.py:123
  36.2 2.1 %collective-permute-start.7 = (f32[256,512]{1,0:T(8,128)S(1)}, f32[256,512]{1,0:T(8,128)}, u32[]{:S(2)}, u32[]{:S(2)}) collective-permute-start(f32[256,512]{1,0:T(8,128)S(1)} %get-tuple-element.48), channel_id=1, source_target_pairs={{0,1},{8,9},{16,17},{24,25},{7,6},{23,22},{15,14},{31,30},{64,65},... | collective-permute-start | bytes 1572872 | tf_op jit(solution)/shard_map/ppermute | solution.py:123
  42.6 0.1 broadcast_select_fusion.8
  42.7 1.3 collective-permute-start.3
  44.0 1.8 %collective-permute-done.8 = f32[256,512]{1,0:T(8,128)S(1)} collective-permute-done((f32[256,512]{1,0:T(8,128)S(1)}, f32[256,512]{1,0:T(8,128)S(1)}, u32[]{:S(2)}, u32[]{:S(2)}) %collective-permute-start.8) | collective-permute-done | bytes 524320 | tf_op jit(solution)/shard_map/ppermute | solution.py:123
  45.8 5.6 %collective-permute-done.7 = f32[256,512]{1,0:T(8,128)} collective-permute-done((f32[256,512]{1,0:T(8,128)S(1)}, f32[256,512]{1,0:T(8,128)}, u32[]{:S(2)}, u32[]{:S(2)}) %collective-permute-start.7) | collective-permute-done | bytes 524320 | tf_op jit(solution)/shard_map/ppermute | solution.py:123
  51.4 2.3 %broadcast_select_fusion.4 = (f32[256,512]{1,0:T(8,128)}, f32[256,512]{1,0:T(8,128)S(1)}, f32[256,512]{1,0:T(8,128)S(1)}) fusion(pred[]{:T(512)} %bitcast.16, f32[256,512]{1,0:T(8,128)S(1)} %collective-permute-done.8, f32[256,512]{1,0:T(8,128)} %collective-permute-done.9, pred[]{:T(512)} %bitcast.19, f32[256,512]{1,0:T(8,128)S(1)} %get-tuple-element.49, ...), kind=kLoop, calls=%fused_computation.77 | loop fusion | flops 917504 | bytes 4194311 | tf_op jit(solution)/shard_map/jit(_where)/select_n | solution.py:122
  53.7 1.5 %collective-permute-start.10 = (f32[256,512]{1,0:T(8,128)}, f32[256,512]{1,0:T(8,128)S(1)}, u32[]{:S(2)}, u32[]{:S(2)}) collective-permute-start(f32[256,512]{1,0:T(8,128)} %get-tuple-element.45), channel_id=1, source_target_pairs={{0,4},{1,5},{2,6},{3,7},{8,12},{9,13},{10,14},{11,15},{16,20},{17,... | collective-permute-start | bytes 1572872 | tf_op jit(solution)/shard_map/ppermute | solution.py:123
  56.4 2.0 %broadcast_select_fusion.9 = f32[256,512]{1,0:T(8,128)} fusion(f32[256,512]{1,0:T(8,128)} %collective-permute-done.3, f32[256,512]{1,0:T(8,128)S(1)} %broadcast_select_fusion.8, pred[]{:T(512)S(6)} %or.13), kind=kLoop, calls=%fused_computation.82 | loop fusion | flops 131072 | bytes 1572865 | tf_op jit(solution)/shard_map/jit(_where)/select_n | solution.py:149
  58.4 4.7 %collective-permute-done.10 = f32[256,512]{1,0:T(8,128)S(1)} collective-permute-done((f32[256,512]{1,0:T(8,128)}, f32[256,512]{1,0:T(8,128)S(1)}, u32[]{:S(2)}, u32[]{:S(2)}) %collective-permute-start.10) | collective-permute-done | bytes 524320 | tf_op jit(solution)/shard_map/ppermute | solution.py:123
  63.2 0.1 broadcast_select_fusion.3
  63.3 0.1 broadcast_select_fusion.1
  63.4 0.1 collective-permute-start.11
  63.5 0.0 copy-start.4
  63.5 1.9 %collective-permute-done.11 = f32[256,512]{1,0:T(8,128)S(1)} collective-permute-done((f32[256,512]{1,0:T(8,128)S(1)}, f32[256,512]{1,0:T(8,128)S(1)}, u32[]{:S(2)}, u32[]{:S(2)}) %collective-permute-start.11) | collective-permute-done | bytes 524320 | tf_op jit(solution)/shard_map/ppermute | solution.py:169
  65.4 0.1 broadcast_select_fusion
  65.6 1.5 %fusion.2.x_ref = f32[256,768]{1,0:T(8,128)S(1)} fusion(f32[256,512]{1,0:T(8,128)S(1)} %copy-done.4, f32[256,256]{1,0:T(8,128)S(1)} %broadcast_in_dim.3, f32[256,512]{1,0:T(8,128)S(1)} %get-tuple-element.81, f32[256,256]{1,0:T(8,128)S(1)} %get-tuple-element.79, f32[256,256]{1,0:T(8,128)S(1)} %get-tuple-element.78), kind=kOutput, calls=%fused_computation.5 | convolution fusion | flops 1209925632 | bytes 2621440 | tf_op jit(solution)/shard_map/dot_general | solution.py:179
  67.2 0.6 fusion.32
  67.8 0.6 fusion.34
  68.4 0.1 slice_subtract_fusion.2
  68.6 0.1 fusion.43
  68.6 1.3 collective-permute-start.12
  69.9 1.5 %collective-permute-start.13 = (f32[256,512]{1,0:T(8,128)S(1)}, f32[256,512]{1,0:T(8,128)}, u32[]{:S(2)}, u32[]{:S(2)}) collective-permute-start(f32[256,512]{1,0:T(8,128)S(1)} %fusion.43), channel_id=1, source_target_pairs={{32,64},{160,192},{64,32},{192,160},{33,65},{161,193},{65,33},{193... | collective-permute-start | bytes 1572872 | tf_op jit(solution)/shard_map/ppermute | solution.py:169
  71.4 1.3 collective-permute-start.14
  72.7 8.0 %shard_map.76 = (f32[2048,256]{1,0:T(8,128)}, f32[2048,256]{1,0:T(8,128)}, f32[2048,256]{1,0:T(8,128)}) custom-call(s32[1]{0:T(128)} %bitcast.21.flag_ref, f32[256,768]{1,0:T(8,128)} %copy-done.2, f32[2048,256]{1,0:T(8,128)} %v_ref.1, f32[2048,256]{1,0:T(8,128)} %w_ref.1, f32[2048,256]{1,0:T(8,128)} %g_ref.1), custom_call_target="tpu_custom_call" | custom-call | tf_op jit(solution)/shard_map/pallas_call | solution.py:67
  80.7 2.4 %collective-permute-done.12 = f32[256,512]{1,0:T(8,128)S(1)} collective-permute-done((f32[256,512]{1,0:T(8,128)S(1)}, f32[256,512]{1,0:T(8,128)S(1)}, u32[]{:S(2)}, u32[]{:S(2)}) %collective-permute-start.12) | collective-permute-done | bytes 524320 | tf_op jit(solution)/shard_map/ppermute | solution.py:169
  83.1 1.4 %select_select_fusion.2 = (f32[256,512]{1,0:T(8,128)S(1)}, f32[256,512]{1,0:T(8,128)S(1)}) fusion(f32[256,512]{1,0:T(8,128)S(1)} %collective-permute-done.12, f32[256,512]{1,0:T(8,128)} %collective-permute-done.13, f32[256,512]{1,0:T(8,128)} %collective-permute-done.14, f32[256,256]{1,0:T(8,128)S(1)} %get-tuple-element.77, ...), kind=kLoop, calls=%fused_computation.51 | loop fusion | flops 1048576 | bytes 3670020 | tf_op jit(solution)/shard_map/jit(_where)/select_n | solution.py:171
  84.6 1.5 %fusion.6.x_ref = f32[256,768]{1,0:T(8,128)S(1)} fusion(f32[256,512]{1,0:T(8,128)S(1)} %copy-done.5, f32[256,256]{1,0:T(8,128)S(1)} %broadcast_in_dim.3, f32[256,512]{1,0:T(8,128)S(1)} %get-tuple-element.32, f32[256,256]{1,0:T(8,128)S(1)} %get-tuple-element.73, f32[256,256]{1,0:T(8,128)S(1)} %get-tuple-element.72), kind=kOutput, calls=%fused_computation.8 | convolution fusion | flops 1209925632 | bytes 2621440 | tf_op jit(solution)/shard_map/dot_general | solution.py:179
  86.1 0.6 fusion.30
  86.8 0.6 fusion.38
  87.4 0.1 slice_subtract_fusion
  87.5 0.1 slice_subtract_fusion.1
  87.5 0.9 fusion.42
  88.4 1.3 collective-permute-start.15
  89.7 0.7 collective-permute-start.16
  90.4 0.7 collective-permute-start.17
  91.1 0.7 collective-permute-start.18
  91.8 1.5 %collective-permute-start.19 = (f32[256,512]{1,0:T(8,128)}, f32[256,512]{1,0:T(8,128)}, u32[]{:S(2)}, u32[]{:S(2)}) collective-permute-start(f32[256,512]{1,0:T(8,128)} %fusion.42), channel_id=1, source_target_pairs={{96,64},{128,160},{97,65},{129,161},{98,66},{130,162},{99,67},{131... | collective-permute-start | bytes 1572872 | tf_op jit(solution)/shard_map/ppermute | solution.py:169
  93.3 6.7 %collective-permute-done.15 = f32[256,512]{1,0:T(8,128)S(1)} collective-permute-done((f32[256,512]{1,0:T(8,128)}, f32[256,512]{1,0:T(8,128)S(1)}, u32[]{:S(2)}, u32[]{:S(2)}) %collective-permute-start.15) | collective-permute-done | bytes 524320 | tf_op jit(solution)/shard_map/ppermute | solution.py:169
  100.1 1.5 %collective-permute-start.20 = (f32[256,512]{1,0:T(8,128)}, f32[256,512]{1,0:T(8,128)}, u32[]{:S(2)}, u32[]{:S(2)}) collective-permute-start(f32[256,512]{1,0:T(8,128)} %fusion.42), channel_id=1, source_target_pairs={{96,32},{128,192},{97,33},{129,193},{98,34},{130,194},{99,35},{131... | collective-permute-start | bytes 1572872 | tf_op jit(solution)/shard_map/ppermute | solution.py:169
  101.5 1.5 %collective-permute-start.21 = (f32[256,512]{1,0:T(8,128)}, f32[256,512]{1,0:T(8,128)}, u32[]{:S(2)}, u32[]{:S(2)}) collective-permute-start(f32[256,512]{1,0:T(8,128)} %fusion.42), channel_id=1, source_target_pairs={{96,0},{128,224},{97,1},{129,225},{98,2},{130,226},{99,3},{131,227... | collective-permute-start | bytes 1572872 | tf_op jit(solution)/shard_map/ppermute | solution.py:169
  103.0 8.0 %shard_map.77 = (f32[2048,256]{1,0:T(8,128)}, f32[2048,256]{1,0:T(8,128)}, f32[2048,256]{1,0:T(8,128)}) custom-call(s32[1]{0:T(128)} %bitcast.22.flag_ref, f32[256,768]{1,0:T(8,128)} %copy-done.1, f32[2048,256]{1,0:T(8,128)} %get-tuple-element.34.v_ref, f32[2048,256]{1,0:T(8,128)} %get-tuple-element.35.w_ref, f32[2048,256]{1,0:T(8,128)} %get-tuple-element.36.g_ref), custom_call_target="tpu_custom_call" | custom-call | tf_op jit(solution)/shard_map/pallas_call | solution.py:67
  111.1 9.1 %collective-permute-done.21 = f32[256,512]{1,0:T(8,128)} collective-permute-done((f32[256,512]{1,0:T(8,128)}, f32[256,512]{1,0:T(8,128)}, u32[]{:S(2)}, u32[]{:S(2)}) %collective-permute-start.21) | collective-permute-done | bytes 524320 | tf_op jit(solution)/shard_map/ppermute | solution.py:169
  120.1 1.9 %select_select_fusion = (f32[256,512]{1,0:T(8,128)S(1)}, f32[256,512]{1,0:T(8,128)S(1)}) fusion(f32[256,512]{1,0:T(8,128)S(1)} %collective-permute-done.15, f32[256,512]{1,0:T(8,128)S(1)} %collective-permute-done.16, f32[256,512]{1,0:T(8,128)S(1)} %collective-permute-done.17, f32[256,512]{1,0:T(8,128)S(1)} %collective-permute-done.18, ...), kind=kLoop, calls=%fused_computation.49 | loop fusion | flops 2097152 | bytes 5767176 | tf_op jit(solution)/shard_map/jit(_where)/select_n | solution.py:171
  122.0 2.4 %fusion.10.x_ref = f32[256,768]{1,0:T(8,128)} fusion(f32[256,512]{1,0:T(8,128)S(1)} %copy-done.3, f32[256,256]{1,0:T(8,128)S(1)} %copy-done.7, f32[256,512]{1,0:T(8,128)S(1)} %get-tuple-element.40, f32[256,256]{1,0:T(8,128)S(1)} %get-tuple-element.67, f32[256,256]{1,0:T(8,128)S(1)} %get-tuple-element.66), kind=kOutput, calls=%fused_computation.11 | convolution fusion | flops 1209925632 | bytes 2621440 | tf_op jit(solution)/shard_map/dot_general | solution.py:179
  124.4 8.0 %shard_map.78 = (f32[2048,256]{1,0:T(8,128)}, f32[2048,256]{1,0:T(8,128)}, f32[2048,256]{1,0:T(8,128)}) custom-call(s32[1]{0:T(128)} %bitcast.flag_ref, f32[256,768]{1,0:T(8,128)} %fusion.10.x_ref, f32[2048,256]{1,0:T(8,128)} %get-tuple-element.42.v_ref, f32[2048,256]{1,0:T(8,128)} %get-tuple-element.43.w_ref, f32[2048,256]{1,0:T(8,128)} %get-tuple-element.44.g_ref), custom_call_target="tpu_custom_call" | custom-call | tf_op jit(solution)/shard_map/pallas_call | solution.py:67
  (35 shorter events, 0.3 us)
Async XLA Ops:
  0.6 7.3 %copy-start.8 = (s32[9,2,32]{2,1,0:T(2,128)S(1)}, s32[9,2,32]{2,1,0:T(2,128)}, u32[]{:S(2)}) copy-start(s32[9,2,32]{2,1,0:T(2,128)} %constant.82.clone) | copy-start | bytes 6916
  3.1 16.8 %collective-permute-start.1 = (f32[256,512]{1,0:T(8,128)}, f32[256,512]{1,0:T(8,128)}, u32[]{:S(2)}, u32[]{:S(2)}) collective-permute-start(f32[256,512]{1,0:T(8,128)} %get-tuple-element.59), channel_id=1, source_target_pairs={{96,64},{128,160},{97,65},{129,161},{98,66},{130,162},{99,67},{131... | collective-permute-start | bytes 1572872 | tf_op jit(solution)/shard_map/ppermute | solution.py:148
  4.5 15.3 %collective-permute-start = (f32[256,512]{1,0:T(8,128)S(1)}, f32[256,512]{1,0:T(8,128)}, u32[]{:S(2)}, u32[]{:S(2)}) collective-permute-start(f32[256,512]{1,0:T(8,128)S(1)} %get-tuple-element.61), channel_id=1, source_target_pairs={{32,0},{160,128},{64,96},{192,224},{33,1},{161,129},{65,97},{193,2... | collective-permute-start | bytes 1572872 | tf_op jit(solution)/shard_map/ppermute | solution.py:148
  6.8 13.1 %copy-start = (f32[1,3,256,512]{3,2,1,0:T(8,128)S(1)}, f32[1,3,256,512]{3,2,1,0:T(8,128)}, u32[]{:S(2)}) copy-start(f32[1,3,256,512]{3,2,1,0:T(8,128)} %param.8) | copy-start | bytes 4718596
  11.2 12.2 %collective-permute-start.5 = (f32[256,512]{1,0:T(8,128)}, f32[256,512]{1,0:T(8,128)}, u32[]{:S(2)}, u32[]{:S(2)}) collective-permute-start(f32[256,512]{1,0:T(8,128)} %fusion.44), channel_id=1, source_target_pairs={{0,16},{31,15},{64,80},{95,79},{128,144},{159,143},{192,208},{223,... | collective-permute-start | bytes 1572872 | tf_op jit(solution)/shard_map/ppermute | solution.py:123
  12.7 12.3 %collective-permute-start.6 = (f32[256,512]{1,0:T(8,128)}, f32[256,512]{1,0:T(8,128)}, u32[]{:S(2)}, u32[]{:S(2)}) collective-permute-start(f32[256,512]{1,0:T(8,128)} %fusion.44), channel_id=1, source_target_pairs={{0,24},{31,7},{64,88},{95,71},{128,152},{159,135},{192,216},{223,1... | collective-permute-start | bytes 1572872 | tf_op jit(solution)/shard_map/ppermute | solution.py:123
  14.0 11.0 %collective-permute-start.4 = (f32[256,512]{1,0:T(8,128)}, f32[256,512]{1,0:T(8,128)}, u32[]{:S(2)}, u32[]{:S(2)}) collective-permute-start(f32[256,512]{1,0:T(8,128)} %fusion.44), channel_id=1, source_target_pairs={{0,8},{31,23},{64,72},{95,87},{128,136},{159,151},{192,200},{223,2... | collective-permute-start | bytes 1572872 | tf_op jit(solution)/shard_map/ppermute | solution.py:123
  22.0 20.6 %collective-permute-start.2 = (f32[256,512]{1,0:T(8,128)S(1)}, f32[256,512]{1,0:T(8,128)}, u32[]{:S(2)}, u32[]{:S(2)}) collective-permute-start(f32[256,512]{1,0:T(8,128)S(1)} %get-tuple-element.57), channel_id=1, source_target_pairs={{96,32},{128,192},{97,33},{129,193},{98,34},{130,194},{99,35},{131... | collective-permute-start | bytes 1572872 | tf_op jit(solution)/shard_map/ppermute | solution.py:148
  26.6 19.2 %collective-permute-start.8 = (f32[256,512]{1,0:T(8,128)S(1)}, f32[256,512]{1,0:T(8,128)S(1)}, u32[]{:S(2)}, u32[]{:S(2)}) collective-permute-start(f32[256,512]{1,0:T(8,128)S(1)} %get-tuple-element.48), channel_id=1, source_target_pairs={{0,2},{8,10},{16,18},{24,26},{7,5},{23,21},{15,13},{31,29},{64,66}... | collective-permute-start | bytes 1572872 | tf_op jit(solution)/shard_map/ppermute | solution.py:123
  34.1 11.7 %collective-permute-start.9 = (f32[256,512]{1,0:T(8,128)S(1)}, f32[256,512]{1,0:T(8,128)}, u32[]{:S(2)}, u32[]{:S(2)}) collective-permute-start(f32[256,512]{1,0:T(8,128)S(1)} %get-tuple-element.48), channel_id=1, source_target_pairs={{0,3},{8,11},{16,19},{24,27},{7,4},{23,20},{15,12},{31,28},{64,67}... | collective-permute-start | bytes 1572872 | tf_op jit(solution)/shard_map/ppermute | solution.py:123
  36.2 15.2 %collective-permute-start.7 = (f32[256,512]{1,0:T(8,128)S(1)}, f32[256,512]{1,0:T(8,128)}, u32[]{:S(2)}, u32[]{:S(2)}) collective-permute-start(f32[256,512]{1,0:T(8,128)S(1)} %get-tuple-element.48), channel_id=1, source_target_pairs={{0,1},{8,9},{16,17},{24,25},{7,6},{23,22},{15,14},{31,30},{64,65},... | collective-permute-start | bytes 1572872 | tf_op jit(solution)/shard_map/ppermute | solution.py:123
  42.7 13.8 %collective-permute-start.3 = (f32[256,512]{1,0:T(8,128)S(1)}, f32[256,512]{1,0:T(8,128)}, u32[]{:S(2)}, u32[]{:S(2)}) collective-permute-start(f32[256,512]{1,0:T(8,128)S(1)} %broadcast_select_fusion.8), channel_id=1, source_target_pairs={{96,0},{128,224},{97,1},{129,225},{98,2},{130,226},{99,3},{131,227... | collective-permute-start | bytes 1572872 | tf_op jit(solution)/shard_map/ppermute | solution.py:148
  53.7 9.5 %collective-permute-start.10 = (f32[256,512]{1,0:T(8,128)}, f32[256,512]{1,0:T(8,128)S(1)}, u32[]{:S(2)}, u32[]{:S(2)}) collective-permute-start(f32[256,512]{1,0:T(8,128)} %get-tuple-element.45), channel_id=1, source_target_pairs={{0,4},{1,5},{2,6},{3,7},{8,12},{9,13},{10,14},{11,15},{16,20},{17,... | collective-permute-start | bytes 1572872 | tf_op jit(solution)/shard_map/ppermute | solution.py:123
  63.4 2.0 %collective-permute-start.11 = (f32[256,512]{1,0:T(8,128)S(1)}, f32[256,512]{1,0:T(8,128)S(1)}, u32[]{:S(2)}, u32[]{:S(2)}) collective-permute-start(f32[256,512]{1,0:T(8,128)S(1)} %broadcast_select_fusion.1), channel_id=1, source_target_pairs={{0,32},{64,96},{128,160},{192,224},{32,0},{96,64},{160,128},{224,1... | collective-permute-start | bytes 1572872 | tf_op jit(solution)/shard_map/ppermute | solution.py:169
  63.5 2.1 %copy-start.4 = (f32[256,512]{1,0:T(8,128)S(1)}, f32[256,512]{1,0:T(8,128)}, u32[]{:S(2)}) copy-start(f32[256,512]{1,0:T(8,128)} %get-tuple-element.26) | copy-start | bytes 1572868
  65.6 18.9 %copy-start.6 = (f32[256,256]{1,0:T(8,128)}, f32[256,256]{1,0:T(8,128)S(1)}, u32[]{:S(2)}) copy-start(f32[256,256]{1,0:T(8,128)S(1)} %broadcast_in_dim.3) | copy-start | bytes 786436
  67.1 1.3 copy-start.2
  68.6 14.4 %collective-permute-start.12 = (f32[256,512]{1,0:T(8,128)S(1)}, f32[256,512]{1,0:T(8,128)S(1)}, u32[]{:S(2)}, u32[]{:S(2)}) collective-permute-start(f32[256,512]{1,0:T(8,128)S(1)} %fusion.43), channel_id=1, source_target_pairs={{32,96},{160,224},{64,0},{192,128},{33,97},{161,225},{65,1},{193,1... | collective-permute-start | bytes 1572872 | tf_op jit(solution)/shard_map/ppermute | solution.py:169
  69.9 13.1 %collective-permute-start.13 = (f32[256,512]{1,0:T(8,128)S(1)}, f32[256,512]{1,0:T(8,128)}, u32[]{:S(2)}, u32[]{:S(2)}) collective-permute-start(f32[256,512]{1,0:T(8,128)S(1)} %fusion.43), channel_id=1, source_target_pairs={{32,64},{160,192},{64,32},{192,160},{33,65},{161,193},{65,33},{193... | collective-permute-start | bytes 1572872 | tf_op jit(solution)/shard_map/ppermute | solution.py:169
  71.4 11.7 %collective-permute-start.14 = (f32[256,512]{1,0:T(8,128)S(1)}, f32[256,512]{1,0:T(8,128)}, u32[]{:S(2)}, u32[]{:S(2)}) collective-permute-start(f32[256,512]{1,0:T(8,128)S(1)} %fusion.43), channel_id=1, source_target_pairs={{32,0},{160,128},{64,96},{192,224},{33,1},{161,129},{65,97},{193,2... | collective-permute-start | bytes 1572872 | tf_op jit(solution)/shard_map/ppermute | solution.py:169
  80.7 3.9 %copy-start.5 = (f32[256,512]{1,0:T(8,128)S(1)}, f32[256,512]{1,0:T(8,128)}, u32[]{:S(2)}) copy-start(f32[256,512]{1,0:T(8,128)} %get-tuple-element.28) | copy-start | bytes 1572868
  86.1 1.3 copy-start.1
  88.4 11.6 %collective-permute-start.15 = (f32[256,512]{1,0:T(8,128)}, f32[256,512]{1,0:T(8,128)S(1)}, u32[]{:S(2)}, u32[]{:S(2)}) collective-permute-start(f32[256,512]{1,0:T(8,128)} %fusion.42), channel_id=1, source_target_pairs={{96,224},{128,0},{97,225},{129,1},{98,226},{130,2},{99,227},{131,3... | collective-permute-start | bytes 1572872 | tf_op jit(solution)/shard_map/ppermute | solution.py:169
  89.7 11.8 %collective-permute-start.16 = (f32[256,512]{1,0:T(8,128)}, f32[256,512]{1,0:T(8,128)S(1)}, u32[]{:S(2)}, u32[]{:S(2)}) collective-permute-start(f32[256,512]{1,0:T(8,128)} %fusion.42), channel_id=1, source_target_pairs={{96,192},{128,32},{97,193},{129,33},{98,194},{130,34},{99,195},{13... | collective-permute-start | bytes 1572872 | tf_op jit(solution)/shard_map/ppermute | solution.py:169
  90.4 20.6 %collective-permute-start.17 = (f32[256,512]{1,0:T(8,128)}, f32[256,512]{1,0:T(8,128)S(1)}, u32[]{:S(2)}, u32[]{:S(2)}) collective-permute-start(f32[256,512]{1,0:T(8,128)} %fusion.42), channel_id=1, source_target_pairs={{96,160},{128,64},{97,161},{129,65},{98,162},{130,66},{99,163},{13... | collective-permute-start | bytes 1572872 | tf_op jit(solution)/shard_map/ppermute | solution.py:169
  91.1 19.9 %collective-permute-start.18 = (f32[256,512]{1,0:T(8,128)}, f32[256,512]{1,0:T(8,128)S(1)}, u32[]{:S(2)}, u32[]{:S(2)}) collective-permute-start(f32[256,512]{1,0:T(8,128)} %fusion.42), channel_id=1, source_target_pairs={{96,128},{128,96},{97,129},{129,97},{98,130},{130,98},{99,131},{13... | collective-permute-start | bytes 1572872 | tf_op jit(solution)/shard_map/ppermute | solution.py:169
  91.8 19.2 %collective-permute-start.19 = (f32[256,512]{1,0:T(8,128)}, f32[256,512]{1,0:T(8,128)}, u32[]{:S(2)}, u32[]{:S(2)}) collective-permute-start(f32[256,512]{1,0:T(8,128)} %fusion.42), channel_id=1, source_target_pairs={{96,64},{128,160},{97,65},{129,161},{98,66},{130,162},{99,67},{131... | collective-permute-start | bytes 1572872 | tf_op jit(solution)/shard_map/ppermute | solution.py:169
  100.1 11.0 %collective-permute-start.20 = (f32[256,512]{1,0:T(8,128)}, f32[256,512]{1,0:T(8,128)}, u32[]{:S(2)}, u32[]{:S(2)}) collective-permute-start(f32[256,512]{1,0:T(8,128)} %fusion.42), channel_id=1, source_target_pairs={{96,32},{128,192},{97,33},{129,193},{98,34},{130,194},{99,35},{131... | collective-permute-start | bytes 1572872 | tf_op jit(solution)/shard_map/ppermute | solution.py:169
  101.5 18.6 %collective-permute-start.21 = (f32[256,512]{1,0:T(8,128)}, f32[256,512]{1,0:T(8,128)}, u32[]{:S(2)}, u32[]{:S(2)}) collective-permute-start(f32[256,512]{1,0:T(8,128)} %fusion.42), channel_id=1, source_target_pairs={{96,0},{128,224},{97,1},{129,225},{98,2},{130,226},{99,3},{131,227... | collective-permute-start | bytes 1572872 | tf_op jit(solution)/shard_map/ppermute | solution.py:169
  111.0 11.0 %copy-start.3 = (f32[256,512]{1,0:T(8,128)S(1)}, f32[256,512]{1,0:T(8,128)}, u32[]{:S(2)}) copy-start(f32[256,512]{1,0:T(8,128)} %broadcast_select_fusion.9) | copy-start | bytes 1572868
  111.0 11.0 %copy-start.7 = (f32[256,256]{1,0:T(8,128)S(1)}, f32[256,256]{1,0:T(8,128)}, u32[]{:S(2)}) copy-start(f32[256,256]{1,0:T(8,128)} %copy-done.6) | copy-start | bytes 786436
